TPU v7x, 32 devices: a whole 2x2x4 slice. The times are simulated.
32 devices in a mesh: dp: 8 (over z, core), shard: 4 (over y, x).
Axes of the slice: x: 2, y: 2, z: 4, core: 2. Of those that a mesh axis runs over, the one named last changes fastest.
Arguments:
- text_in: bfloat16 [32, 512, 768], P(('dp', 'shard')), may hold values from -6 to 6
- layout_in: bfloat16 [32, 512, 192], P(('dp', 'shard')), may hold values from -6 to 6
- lengths: int32 [32], P(('dp', 'shard')), may hold values from 40 to 512, as said below
- text_attn: bfloat16 [768, 3072], P(('dp', 'shard')), may hold values from -2 to 2
- text_w1: bfloat16 [768, 3072], P(('dp', 'shard')), may hold values from -0.21875 to 0.21875
- text_w2: bfloat16 [3072, 768], P(('dp', 'shard')), may hold values from -0.109375 to 0.109375
- text_vectors: bfloat16 [9216], P(('dp', 'shard')), may hold values from -2 to 2
- layout_attn: bfloat16 [768, 192], P(('dp', 'shard')), may hold values from -2 to 2
- layout_w1: bfloat16 [192, 768], P(None, ('dp', 'shard')), may hold values from -0.4375 to 0.4375
- layout_w2: bfloat16 [768, 192], P(('dp', 'shard')), may hold values from -0.21875 to 0.21875
- layout_vectors: bfloat16 [2304], P(('dp', 'shard')), may hold values from -2 to 2
- cot_text: bfloat16 [32, 512, 768], P(('dp', 'shard')), may hold values from -6 to 6
- cot_layout: bfloat16 [32, 512, 192], P(('dp', 'shard')), may hold values from -6 to 6
Outputs:
- out_text: bfloat16 [32, 512, 768], P(('dp', 'shard'))
- out_layout: bfloat16 [32, 512, 192], P(('dp', 'shard'))
- grad_text_in: float32 [32, 512, 768], P(('dp', 'shard'))
- grad_layout_in: float32 [32, 512, 192], P(('dp', 'shard'))
- grad_text_attn: float32 [768, 3072], P(('dp', 'shard'))
- grad_text_w1: float32 [768, 3072], P(('dp', 'shard'))
- grad_text_w2: float32 [3072, 768], P(('dp', 'shard'))
- grad_text_vectors: float32 [9216], P(('dp', 'shard'))
- grad_layout_attn: float32 [768, 192], P(('dp', 'shard'))
- grad_layout_w1: float32 [192, 768], P(None, ('dp', 'shard'))
- grad_layout_w2: float32 [768, 192], P(('dp', 'shard'))
- grad_layout_vectors: float32 [2304], P(('dp', 'shard'))
Inputs may be any that keep to these rules, and one draw needn't show every extreme that they name: `lengths`: the real tokens of a page fill its first slots; the first page of the batch is full and the second holds 40 tokens.
All inputs are finite; a program needn't handle non-finite values.
Results may differ from a plain program's by a relative error of at most 0.012.
The roundings to bfloat16 on the way count: a program that leaves them out, or rounds other values in their place, can miss the bound.
Values may be sent and summed in bfloat16 or wider, within the bound.
No kernel may reach another device: no remote copies, remote signals or barrier semaphores. Data moves between devices by JAX's collectives and lax.ppermute only.
A program may use at most 192 MiB of HBM per device.

v0:
```python
import jax
import jax.numpy as jnp
from jax import lax
from jax.sharding import PartitionSpec as P

H = 12
HD = 64
LHD = 16


EPS = 1e-05
NEG = -1000000000.0


def normalize(values, scale_row, shift_row):
    centered = values - jnp.mean(values, -1, keepdims=True)
    variance = jnp.mean(centered * centered, -1, keepdims=True)
    return centered * lax.rsqrt(variance + EPS) * scale_row + shift_row


def gelu_exact(values):
    return jax.nn.gelu(values, approximate=False)


def vector_parts(packed, width):
    pieces = [packed[index * width : (index + 1) * width] for index in range(8)]
    return pieces + [packed[8 * width :]]


def split_heads(values):
    return values.reshape(values.shape[0], H, -1)


def block_of(attn, index, width, columns):
    if columns:
        return attn[:, index * width : (index + 1) * width]
    return attn[index * width : (index + 1) * width]


def project_three(inputs, attn, packed, width, columns):
    if columns:
        three = attn[:, 0 : 3 * width].reshape(width, 3, width)
        mixed = jnp.einsum("sd,dje->sje", inputs, three, preferred_element_type=jnp.float32)
    else:
        three = attn[0 : 3 * width].reshape(3, width, width)
        mixed = jnp.einsum("sd,jde->sje", inputs, three, preferred_element_type=jnp.float32)
    pieces = vector_parts(packed.astype(jnp.float32), width)
    offsets = jnp.stack([pieces[0], jnp.zeros_like(pieces[0]), pieces[1]])
    return (mixed + offsets[None]).astype(jnp.bfloat16)


def score_table(text_three, layout_three, valid):
    text_part = jnp.einsum(
        "qhd,khd->hqk",
        split_heads(text_three[:, 0]),
        split_heads(text_three[:, 1]),
        preferred_element_type=jnp.float32,
    )
    layout_part = jnp.einsum(
        "qhd,khd->hqk",
        split_heads(layout_three[:, 0]),
        split_heads(layout_three[:, 1]),
        preferred_element_type=jnp.float32,
    )
    joined = text_part * HD ** (-0.5) + layout_part * LHD ** (-0.5)
    return jnp.where(valid[None, None, :], joined, NEG)


def attend(text_three, layout_three, valid):
    scores = score_table(text_three, layout_three, valid)
    row_max = jnp.max(scores, -1, keepdims=True)
    exponent = jnp.exp(scores - row_max)
    row_total = jnp.sum(exponent, -1, keepdims=True)
    weights = (exponent / row_total).astype(jnp.bfloat16)
    slots = text_three.shape[0]
    text_ctx = jnp.einsum(
        "hqk,khd->qhd", weights, split_heads(text_three[:, 2]), preferred_element_type=jnp.float32
    )
    layout_ctx = jnp.einsum(
        "hqk,khd->qhd", weights, split_heads(layout_three[:, 2]), preferred_element_type=jnp.float32
    )
    log_total = (row_max + jnp.log(row_total))[..., 0]
    return (
        text_ctx.reshape(slots, -1).astype(jnp.bfloat16),
        layout_ctx.reshape(slots, -1).astype(jnp.bfloat16),
        log_total,
    )


def attend_back(text_three, layout_three, valid, log_total, text_grad, layout_grad):
    scores = score_table(text_three, layout_three, valid)
    probs = jnp.exp(scores - log_total[..., None])
    weights = probs.astype(jnp.bfloat16)
    text_heads = split_heads(text_grad)
    layout_heads = split_heads(layout_grad)
    text_dp = jnp.einsum(
        "qhd,khd->hqk",
        text_heads,
        split_heads(text_three[:, 2]),
        preferred_element_type=jnp.float32,
    )
    layout_dp = jnp.einsum(
        "qhd,khd->hqk",
        layout_heads,
        split_heads(layout_three[:, 2]),
        preferred_element_type=jnp.float32,
    )
    text_dv = jnp.einsum("hqk,qhd->khd", weights, text_heads, preferred_element_type=jnp.float32)
    layout_dv = jnp.einsum(
        "hqk,qhd->khd", weights, layout_heads, preferred_element_type=jnp.float32
    )
    text_ds = probs * (text_dp - jnp.sum(probs * text_dp, -1, keepdims=True))
    layout_ds = probs * (layout_dp - jnp.sum(probs * layout_dp, -1, keepdims=True))
    text_only = text_ds.astype(jnp.bfloat16)
    joint_ds = (text_ds + layout_ds).astype(jnp.bfloat16)
    text_dq = jnp.einsum(
        "hqk,khd->qhd", text_only, split_heads(text_three[:, 1]), preferred_element_type=jnp.float32
    ) * HD ** (-0.5)
    text_dk = jnp.einsum(
        "hqk,qhd->khd", text_only, split_heads(text_three[:, 0]), preferred_element_type=jnp.float32
    ) * HD ** (-0.5)
    layout_dq = jnp.einsum(
        "hqk,khd->qhd",
        joint_ds,
        split_heads(layout_three[:, 1]),
        preferred_element_type=jnp.float32,
    ) * LHD ** (-0.5)
    layout_dk = jnp.einsum(
        "hqk,qhd->khd",
        joint_ds,
        split_heads(layout_three[:, 0]),
        preferred_element_type=jnp.float32,
    ) * LHD ** (-0.5)
    slots = text_three.shape[0]
    text_all = jnp.stack([text_dq, text_dk, text_dv], 1).reshape(slots, 3, -1)
    layout_all = jnp.stack([layout_dq, layout_dk, layout_dv], 1).reshape(slots, 3, -1)
    return (text_all, layout_all)


def project_back(attn, width, columns, three_grad, first_grad):
    rounded_grad = three_grad.astype(jnp.bfloat16)
    if columns:
        three = attn[:, 0 : 3 * width].reshape(width, 3, width)
        input_grad = first_grad + jnp.einsum(
            "sje,dje->sd", rounded_grad, three, preferred_element_type=jnp.float32
        )
    else:
        three = attn[0 : 3 * width].reshape(3, width, width)
        input_grad = first_grad + jnp.einsum(
            "sje,jde->sd", rounded_grad, three, preferred_element_type=jnp.float32
        )
    column_sums = jnp.sum(rounded_grad.astype(jnp.float32), 0)
    return (input_grad, rounded_grad, column_sums[0], column_sums[2])


def branch_forward(inputs, context, attn, packed, first, second, width, columns):
    pieces = vector_parts(packed.astype(jnp.float32), width)
    out_block = block_of(attn, 3, width, columns)
    first_res = inputs.astype(jnp.float32) + (
        jnp.dot(context, out_block, preferred_element_type=jnp.float32) + pieces[2]
    )
    hidden = normalize(first_res, pieces[3], pieces[4])
    inner = (
        jnp.dot(hidden.astype(jnp.bfloat16), first, preferred_element_type=jnp.float32) + pieces[8]
    )
    activated = gelu_exact(inner).astype(jnp.bfloat16)
    second_res = hidden + (
        jnp.dot(activated, second, preferred_element_type=jnp.float32) + pieces[5]
    )
    result = normalize(second_res, pieces[6], pieces[7])
    return (result, (first_res, inner, second_res))


def branch_backward(attn, packed, first, second, width, columns, kept_rows, grad_out):
    first_res, inner, second_res = kept_rows
    pieces = vector_parts(packed.astype(jnp.float32), width)
    hidden, first_pull = jax.vjp(normalize, first_res, pieces[3], pieces[4])
    unused, second_pull = jax.vjp(normalize, second_res, pieces[6], pieces[7])
    grad_second, late_scale, late_shift = second_pull(grad_out)
    round_second = grad_second.astype(jnp.bfloat16)
    activated, gelu_pull = jax.vjp(gelu_exact, inner)
    (grad_inner,) = gelu_pull(jnp.dot(round_second, second.T, preferred_element_type=jnp.float32))
    round_inner = grad_inner.astype(jnp.bfloat16)
    grad_hidden = grad_second + jnp.dot(round_inner, first.T, preferred_element_type=jnp.float32)
    grad_first, early_scale, early_shift = first_pull(grad_hidden)
    round_first = grad_first.astype(jnp.bfloat16)
    out_block = block_of(attn, 3, width, columns)
    grad_ctx = jnp.dot(round_first, out_block.T, preferred_element_type=jnp.float32).astype(
        jnp.bfloat16
    )
    operands = (
        hidden.astype(jnp.bfloat16),
        activated.astype(jnp.bfloat16),
        round_first,
        round_second,
        round_inner,
    )
    vector_sums = (
        jnp.sum(grad_first, 0),
        early_scale,
        early_shift,
        jnp.sum(grad_second, 0),
        late_scale,
        late_shift,
        jnp.sum(grad_inner, 0),
    )
    return (grad_first, grad_ctx, operands, vector_sums)


def page_forward(text_rows, layout_rows, length, weights):
    (
        text_attn,
        text_first,
        text_second,
        text_packed,
        layout_attn,
        layout_first,
        layout_second,
        layout_packed,
    ) = weights
    width = text_rows.shape[1]
    narrow = layout_rows.shape[1]
    valid = jnp.arange(text_rows.shape[0], dtype=jnp.int32) < length
    text_three = project_three(text_rows, text_attn, text_packed, width, True)
    layout_three = project_three(layout_rows, layout_attn, layout_packed, narrow, False)
    text_ctx, layout_ctx, log_total = attend(text_three, layout_three, valid)
    text_out, text_kept = branch_forward(
        text_rows, text_ctx, text_attn, text_packed, text_first, text_second, width, True
    )
    layout_out, layout_kept = branch_forward(
        layout_rows,
        layout_ctx,
        layout_attn,
        layout_packed,
        layout_first,
        layout_second,
        narrow,
        False,
    )
    mask = valid[:, None].astype(jnp.float32)
    outputs = ((text_out * mask).astype(jnp.bfloat16), (layout_out * mask).astype(jnp.bfloat16))
    kept_page = (text_three, layout_three, text_ctx, layout_ctx, log_total, text_kept, layout_kept)
    return (outputs, kept_page)


def page_backward(text_rows, layout_rows, length, kept_page, text_cot, layout_cot, weights):
    (
        text_attn,
        text_first,
        text_second,
        text_packed,
        layout_attn,
        layout_first,
        layout_second,
        layout_packed,
    ) = weights
    text_three, layout_three, text_ctx, layout_ctx, log_total, text_kept, layout_kept = kept_page
    width = text_rows.shape[1]
    narrow = layout_rows.shape[1]
    slots = text_rows.shape[0]
    valid = jnp.arange(slots, dtype=jnp.int32) < length
    mask = valid[:, None].astype(jnp.float32)
    text_res_grad, text_ctx_grad, text_ops, text_sums = branch_backward(
        text_attn,
        text_packed,
        text_first,
        text_second,
        width,
        True,
        text_kept,
        text_cot.astype(jnp.float32) * mask,
    )
    layout_res_grad, layout_ctx_grad, layout_ops, layout_sums = branch_backward(
        layout_attn,
        layout_packed,
        layout_first,
        layout_second,
        narrow,
        False,
        layout_kept,
        layout_cot.astype(jnp.float32) * mask,
    )
    text_three_grad, layout_three_grad = attend_back(
        text_three, layout_three, valid, log_total, text_ctx_grad, layout_ctx_grad
    )
    text_in_grad, text_rounded, text_query_bias, text_value_bias = project_back(
        text_attn, width, True, text_three_grad, text_res_grad
    )
    layout_in_grad, layout_rounded, layout_query_bias, layout_value_bias = project_back(
        layout_attn, narrow, False, layout_three_grad, layout_res_grad
    )
    hidden_low, active_low, first_low, second_low, inner_low = layout_ops
    three_w = jnp.einsum(
        "sd,sje->jde", layout_rows, layout_rounded, preferred_element_type=jnp.float32
    ).reshape(3 * narrow, narrow)
    out_w = jnp.einsum("sd,se->de", layout_ctx, first_low, preferred_element_type=jnp.float32)
    layout_attn_grad = jnp.concatenate([three_w, out_w], 0)
    layout_first_grad = jnp.einsum(
        "sd,sf->df", hidden_low, inner_low, preferred_element_type=jnp.float32
    )
    layout_second_grad = jnp.einsum(
        "sf,sd->fd", active_low, second_low, preferred_element_type=jnp.float32
    )
    layout_vec_grad = jnp.concatenate([layout_query_bias, layout_value_bias] + list(layout_sums))
    text_vec_grad = jnp.concatenate([text_query_bias, text_value_bias] + list(text_sums))
    text_hidden, text_active, text_first_low, text_second_low, text_inner_low = text_ops
    text_operands = (
        text_rounded.reshape(slots, 3 * width),
        text_first_low,
        text_hidden,
        text_inner_low,
        text_active,
        text_second_low,
    )
    small_terms = (
        text_vec_grad,
        layout_attn_grad,
        layout_first_grad,
        layout_second_grad,
        layout_vec_grad,
    )
    return ((text_in_grad, layout_in_grad), small_terms, text_operands)


def add_all(running, terms):
    return tuple((before + addend for before, addend in zip(running, terms)))


def flat_rows(values):
    return values.reshape(-1, values.shape[-1])


def body(
    text_in,
    layout_in,
    lengths,
    text_attn,
    text_w1,
    text_w2,
    text_vectors,
    layout_attn,
    layout_w1,
    layout_w2,
    layout_vectors,
    cot_text,
    cot_layout,
):
    text_full = (
        lax.all_gather(text_attn, ("dp", "shard"), axis=0, tiled=True),
        lax.all_gather(text_w1, ("dp", "shard"), axis=0, tiled=True),
        lax.all_gather(text_w2, ("dp", "shard"), axis=0, tiled=True),
        lax.all_gather(text_vectors, ("dp", "shard"), axis=0, tiled=True),
    )
    layout_full = (
        lax.all_gather(layout_attn, ("dp", "shard"), axis=0, tiled=True),
        lax.all_gather(layout_w1, ("dp", "shard"), axis=1, tiled=True),
        lax.all_gather(layout_w2, ("dp", "shard"), axis=0, tiled=True),
        lax.all_gather(layout_vectors, ("dp", "shard"), axis=0, tiled=True),
    )
    weights = tuple(text_full) + tuple(layout_full)

    def forward_step(carry, page):
        text_rows, layout_rows, length = page
        outputs, kept_page = page_forward(text_rows, layout_rows, length, weights)
        return (carry, (outputs, kept_page))

    unused, (outputs, kept_all) = lax.scan(forward_step, None, (text_in, layout_in, lengths))
    out_text, out_layout = outputs
    shards, unused_out = lax.optimization_barrier(
        (
            (
                text_attn,
                text_w1,
                text_w2,
                text_vectors,
                layout_attn,
                layout_w1,
                layout_w2,
                layout_vectors,
            ),
            out_text,
        )
    )
    text_back = (
        lax.all_gather(shards[0], ("dp", "shard"), axis=0, tiled=True),
        lax.all_gather(shards[1], ("dp", "shard"), axis=0, tiled=True),
        lax.all_gather(shards[2], ("dp", "shard"), axis=0, tiled=True),
        lax.all_gather(shards[3], ("dp", "shard"), axis=0, tiled=True),
    )
    layout_back = (
        lax.all_gather(shards[4], ("dp", "shard"), axis=0, tiled=True),
        lax.all_gather(shards[5], ("dp", "shard"), axis=1, tiled=True),
        lax.all_gather(shards[6], ("dp", "shard"), axis=0, tiled=True),
        lax.all_gather(shards[7], ("dp", "shard"), axis=0, tiled=True),
    )
    back_weights = tuple(text_back) + tuple(layout_back)
    zeros = (
        jnp.zeros(back_weights[3].shape, jnp.float32),
        jnp.zeros(back_weights[4].shape, jnp.float32),
        jnp.zeros(back_weights[5].shape, jnp.float32),
        jnp.zeros(back_weights[6].shape, jnp.float32),
        jnp.zeros(back_weights[7].shape, jnp.float32),
    )

    def backward_step(running, page):
        text_rows, layout_rows, length, kept_page, text_cot, layout_cot = page
        in_grads, small_terms, text_operands = page_backward(
            text_rows, layout_rows, length, kept_page, text_cot, layout_cot, back_weights
        )
        return (add_all(running, small_terms), (in_grads, text_operands))

    totals, ((text_grad, layout_grad), text_operands) = lax.scan(
        backward_step, zeros, (text_in, layout_in, lengths, kept_all, cot_text, cot_layout)
    )
    inputs_all = flat_rows(text_in)
    context_all = flat_rows(kept_all[2])
    three_all, first_all, hidden_all, inner_all, active_all, second_all = tuple(
        (flat_rows(values) for values in text_operands)
    )
    three_part = jnp.einsum("sd,se->de", inputs_all, three_all, preferred_element_type=jnp.float32)
    out_part = jnp.einsum("sd,se->de", context_all, first_all, preferred_element_type=jnp.float32)
    grad_attn = lax.psum_scatter(
        jnp.concatenate([three_part, out_part], 1), ("dp", "shard"), scatter_dimension=0, tiled=True
    )
    grad_first = lax.psum_scatter(
        jnp.einsum("sd,sf->df", hidden_all, inner_all, preferred_element_type=jnp.float32),
        ("dp", "shard"),
        scatter_dimension=0,
        tiled=True,
    )
    grad_second = lax.psum_scatter(
        jnp.einsum("sf,sd->fd", active_all, second_all, preferred_element_type=jnp.float32),
        ("dp", "shard"),
        scatter_dimension=0,
        tiled=True,
    )
    text_summed = (lax.psum_scatter(totals[0], ("dp", "shard"), scatter_dimension=0, tiled=True),)
    layout_summed = (
        lax.psum_scatter(totals[1], ("dp", "shard"), scatter_dimension=0, tiled=True),
        lax.psum_scatter(totals[2], ("dp", "shard"), scatter_dimension=1, tiled=True),
        lax.psum_scatter(totals[3], ("dp", "shard"), scatter_dimension=0, tiled=True),
        lax.psum_scatter(totals[4], ("dp", "shard"), scatter_dimension=0, tiled=True),
    )
    summed = tuple(text_summed) + tuple(layout_summed)
    return (
        out_text,
        out_layout,
        text_grad,
        layout_grad,
        grad_attn,
        grad_first,
        grad_second,
        summed[0],
        summed[1],
        summed[2],
        summed[3],
        summed[4],
    )


def solution(mesh):
    placed = (
        P(("dp", "shard"), None, None),
        P(("dp", "shard"), None, None),
        P(("dp", "shard")),
        P(("dp", "shard"), None),
        P(("dp", "shard"), None),
        P(("dp", "shard"), None),
        P(("dp", "shard")),
        P(("dp", "shard"), None),
        P(None, ("dp", "shard")),
        P(("dp", "shard"), None),
        P(("dp", "shard")),
        P(("dp", "shard"), None, None),
        P(("dp", "shard"), None, None),
    )
    return jax.shard_map(
        body,
        mesh=mesh,
        in_specs=placed,
        out_specs=(
            P(("dp", "shard"), None, None),
            P(("dp", "shard"), None, None),
            P(("dp", "shard"), None, None),
            P(("dp", "shard"), None, None),
            P(("dp", "shard"), None),
            P(("dp", "shard"), None),
            P(("dp", "shard"), None),
            P(("dp", "shard")),
            P(("dp", "shard"), None),
            P(None, ("dp", "shard")),
            P(("dp", "shard"), None),
            P(("dp", "shard")),
        ),
        check_vma=False,
    )
```

profile of v0, /device:TPU:0, one launch (start us, length us, event | category | flops | bytes accessed | tf_op | source)
XLA Modules:
  0.0 1359.3 jit_solution(6542040359610718791)
XLA Ops:
  11.2 42.5 %all-reduce.8 = (bf16[9216]{0:T(1024)(128)(2,1)S(1)}, bf16[2304]{0:T(1024)(128)(2,1)S(1)}) all-reduce(bf16[9216]{0:T(1024)(128)(2,1)S(1)} %dynamic-update-slice, bf16[2304]{0:T(1024)(128)(2,1)S(1)} %dynamic-update-slice.1), channel_id=1, replica_groups=mesh['dp'=8,'shard'=4] {'dp','shard'}, use_global_device_ids=true, to_apply=%add | all-reduce | flops 11520 | bytes 46080
  56.8 69.5 %all_gather.50 = bf16[768,192]{1,0:T(8,128)(2,1)S(1)} all-gather(bf16[24,192]{1,0:T(8,128)(2,1)} %param.20), channel_id=1, replica_groups=mesh['dp'=8,'shard'=4] {'dp','shard'}, dimensions={0}, use_global_device_ids=true | all-gather | bytes 304128 | tf_op jit(solution)/shard_map/all_gather | solution.py:355
  130.3 2.0 slice-done.3
  132.3 3.6 copy.105
  135.9 4.3 add_convert_fusion.1
  141.0 6.4 fusion.142
  148.5 6.6 fusion.135
  155.1 1.9 fusion.2
  157.0 3.8 copy-done
  160.8 2.3 divide_convert_fusion
  164.3 1.4 copy-done.1
  168.2 21.3 %multiply_convert_fusion = (bf16[512,3072]{1,0:T(8,128)(2,1)}, f32[512,3072]{1,0:T(8,128)}, f32[512,3072]{1,0:T(8,128)}) fusion(f32[3072]{0:T(1024)S(1)} %copy-done.74, bf16[768,3072]{1,0:T(8,128)(2,1)} %all-gather.9.cloned.1.call-done, f32[512,768]{1,0:T(8,128)} %copy-done.17, f32[768]{0:T(1024)S(1)} %copy-done.83, f32[768]{0:T(1024)S(1)} %get-tuple-element.294, ...), kind=kOutput, calls=%fused_computation.18 | convolution fusion | flops 2521694208 | bytes 22042624 | tf_op jit(solution)/shard_map/while/body/eval_jaxpr/dot_general | solution.py:164
  189.5 19.3 %all-gather.11.cloned.1.call-done = bf16[3072,768]{1,0:T(8,128)(2,1)} async-done(((bf16[96,768]{1,0:T(8,128)(2,1)}), bf16[3072,768]{1,0:T(8,128)(2,1)}) %all-gather.11.cloned.1.call-update) | async-done | bytes 4718608 | tf_op jit(solution)/shard_map/all_gather | solution.py:351
  208.9 6.0 fusion.137
  217.8 73.7 %all_gather.54 = bf16[192,768]{0,1:T(8,128)(2,1)} all-gather(bf16[192,24]{0,1:T(8,128)(2,1)S(1)} %copy-done.51), channel_id=1, replica_groups=mesh['dp'=8,'shard'=4] {'dp','shard'}, dimensions={1}, use_global_device_ids=true | all-gather | bytes 304128 | tf_op jit(solution)/shard_map/all_gather | solution.py:356
  291.5 66.8 %all_gather.55 = bf16[768,192]{1,0:T(8,128)(2,1)S(1)} all-gather(bf16[24,192]{1,0:T(8,128)(2,1)S(1)} %copy-done.49), channel_id=1, replica_groups=mesh['dp'=8,'shard'=4] {'dp','shard'}, dimensions={0}, use_global_device_ids=true | all-gather | bytes 304128 | tf_op jit(solution)/shard_map/all_gather | solution.py:357
  358.9 38.4 %all-reduce.7 = (bf16[9216]{0:T(1024)(128)(2,1)}, bf16[2304]{0:T(1024)(128)(2,1)}) all-reduce(bf16[9216]{0:T(1024)(128)(2,1)S(1)} %dynamic-update-slice.2, bf16[2304]{0:T(1024)(128)(2,1)S(1)} %dynamic-update-slice.3), channel_id=1, replica_groups=mesh['dp'=8,'shard'=4] {'dp','shard'}, use_global_device_ids=true, to_apply=%add.2 | all-reduce | flops 11520 | bytes 46080
  397.3 3.8 convolution_convert_fusion.3
  402.5 3.7 multiply_convert_fusion.3
  406.8 68.1 %all_gather.63 = bf16[768,192]{1,0:T(8,128)(2,1)S(1)} all-gather(bf16[24,192]{1,0:T(8,128)(2,1)S(1)} %copy-done.48), channel_id=1, replica_groups=mesh['dp'=8,'shard'=4] {'dp','shard'}, dimensions={0}, use_global_device_ids=true | all-gather | bytes 304128 | tf_op jit(solution)/shard_map/all_gather | solution.py:391
  475.0 65.5 %all_gather.61 = bf16[768,192]{1,0:T(8,128)(2,1)S(1)} all-gather(bf16[24,192]{1,0:T(8,128)(2,1)S(1)} %copy-done.50), channel_id=1, replica_groups=mesh['dp'=8,'shard'=4] {'dp','shard'}, dimensions={0}, use_global_device_ids=true | all-gather | bytes 304128 | tf_op jit(solution)/shard_map/all_gather | solution.py:393
  540.5 68.3 %all_gather.62 = bf16[192,768]{0,1:T(8,128)(2,1)S(1)} all-gather(bf16[192,24]{0,1:T(8,128)(2,1)S(1)} %copy-done.52), channel_id=1, replica_groups=mesh['dp'=8,'shard'=4] {'dp','shard'}, dimensions={1}, use_global_device_ids=true | all-gather | bytes 304128 | tf_op jit(solution)/shard_map/all_gather | solution.py:392
  611.1 1.5 fusion.141
  619.0 1.3 fusion.110
  620.3 2.5 fusion.90
  622.8 1.9 fusion.125
  624.7 8.0 fusion.143
  632.8 7.1 fusion.67
  640.2 10.4 fusion.140
  650.7 7.1 multiply_reduce_fusion.2
  659.0 3.3 convolution_convert_fusion
  662.3 1.4 copy.77
  663.8 9.5 multiply_reduce_fusion.1
  673.3 22.2 %fusion.64 = bf16[12,16,512]{2,1,0:T(8,128)(2,1)} fusion(bf16[512,12,16]{0,2,1:T(8,128)(2,1)} %bitcast.177, f32[12,512,512]{1,2,0:T(8,128)} %fusion.143, f32[12,512,512]{1,2,0:T(8,128)} %get-tuple-element.326, f32[12,512,512]{1,2,0:T(8,128)} %copy-done, f32[12,512]{1,0:T(8,128)} %get-tuple-element.325, f32[12,512]{1,0:T(8,128)} %log_add_fusion), kind=kOutput, calls=%fused_computation.109 | convolution fusion | flops 129178112 | bytes 38191104 | tf_op jit(solution)/shard_map/while/body/eval_jaxpr/hqk,khd->qhd/dot_general | solution.py:122
  695.6 22.0 %fusion.61 = bf16[12,16,512]{2,1,0:T(8,128)(2,1)} fusion(bf16[512,12,16]{0,2,1:T(8,128)(2,1)S(1)} %bitcast.176, f32[12,512,512]{1,2,0:T(8,128)} %fusion.143, f32[12,512,512]{1,2,0:T(8,128)} %get-tuple-element.326, f32[12,512,512]{1,2,0:T(8,128)} %copy-done, f32[12,512]{1,0:T(8,128)S(1)} %copy-done.47, f32[12,512]{1,0:T(8,128)S(1)} %copy-done.32), kind=kOutput, calls=%fused_computation.108 | convolution fusion | flops 129178112 | bytes 38191104 | tf_op jit(solution)/shard_map/while/body/eval_jaxpr/hqk,qhd->khd/dot_general | solution.py:128
  717.6 1.5 fusion.96
  720.3 8.7 fusion.119
  729.6 8.9 fusion.33
  738.6 6.7 fusion.45
  746.5 10.0 fusion.3
  757.6 1.5 copy-done.2
  760.3 5.8 multiply_convert_fusion.1
  766.1 1.4 copy.82
  767.5 3.0 convert_reduce_fusion
  770.5 4.4 copy.89
  774.9 2.4 fusion.121
  777.2 4.9 convolution_bitcast_fusion
  782.1 7.3 pad_maximum_fusion
  789.4 9.7 copy.103
  802.9 2.0 slice-done
  805.0 3.6 copy.106
  808.6 1.4 convert_reduce_fusion.1
  813.4 1.6 add_reduce_fusion
  817.6 1.3 constant_dynamic-update-slice_fusion.4
  818.9 1.3 constant_dynamic-update-slice_fusion.3
  820.2 1.3 constant_dynamic-update-slice_fusion.2
  822.8 1.3 constant_dynamic-update-slice_fusion
  824.1 37.6 %all-reduce.6 = (f32[9216]{0:T(1024)S(1)}, f32[2304]{0:T(1024)S(1)}) all-reduce(f32[9216]{0:T(1024)} %constant_dynamic-update-slice_fusion, f32[2304]{0:T(1024)S(1)} %concatenate.22), channel_id=5, replica_groups=mesh['dp'=8,'shard'=4] {'dp','shard'}, use_global_device_ids=true, to_apply=%region_31.32.clone | all-reduce | flops 11520 | bytes 92160
  862.9 2.5 fusion.58
  865.4 5.9 fusion.32
  871.3 55.8 %reduce-scatter.13.cloned.1.call-done = f32[24,192]{1,0:T(8,128)} async-done(((f32[768,192]{1,0:T(8,128)}), f32[24,192]{1,0:T(8,128)}) %reduce-scatter.13.cloned.1.call-update) | async-done | bytes 18448 | tf_op jit(solution)/shard_map/reduce_scatter | solution.py:439
  927.1 141.8 %reduce-scatter.11.cloned.1.call-done = f32[96,768]{1,0:T(8,128)} async-done(((f32[3072,768]{1,0:T(8,128)}), f32[96,768]{1,0:T(8,128)}) %reduce-scatter.11.cloned.1.call-update) | async-done | bytes 294928 | tf_op jit(solution)/shard_map/reduce_scatter | solution.py:431
  1068.9 141.6 %reduce-scatter.9.cloned.1.call-done = f32[24,3072]{1,0:T(8,128)} async-done(((f32[768,3072]{1,0:T(8,128)}), f32[24,3072]{1,0:T(8,128)}) %reduce-scatter.9.cloned.1.call-update) | async-done | bytes 294928 | tf_op jit(solution)/shard_map/reduce_scatter | solution.py:425
  1210.5 141.5 %reduce-scatter.19.cloned.1.call-done = f32[24,3072]{1,0:T(8,128)} async-done(((f32[768,3072]{1,0:T(8,128)}), f32[24,3072]{1,0:T(8,128)}) %reduce-scatter.19.cloned.1.call-update) | async-done | bytes 294928
  (304 shorter events, 49.0 us)
Async XLA Ops:
  7.2 123.1 %all-gather.7.cloned.1.call-start = ((), (), s32[]{:S(2)}) async-start(), calls=%async_computation.6 | async-start | bytes 4866048 | tf_op jit(solution)/shard_map/all_gather | solution.py:349
  7.9 160.3 %all-gather.9.cloned.1.call-start = ((), (), s32[]{:S(2)}) async-start(), calls=%async_computation.7 | async-start | bytes 4866048 | tf_op jit(solution)/shard_map/all_gather | solution.py:350
  8.7 200.2 %all-gather.11.cloned.1.call-start = ((), (), s32[]{:S(2)}) async-start(), calls=%async_computation.8 | async-start | bytes 4866048 | tf_op jit(solution)/shard_map/all_gather | solution.py:351
  9.4 630.7 %all-gather.13.cloned.1.call-start = ((), (), s32[]{:S(2)}) async-start(), calls=%async_computation.9 | async-start | bytes 4866048 | tf_op jit(solution)/shard_map/all_gather | solution.py:387
  53.7 73.4 %copy-start.60 = (bf16[2304]{0:T(1024)(128)(2,1)}, bf16[2304]{0:T(1024)(128)(2,1)S(1)}, u32[]{:S(2)}) copy-start(bf16[2304]{0:T(1024)(128)(2,1)S(1)} %get-tuple-element.266) | copy-start | bytes 13828
  140.6 6.7 copy-start.7
  140.9 6.4 copy-start.11
  140.9 7.6 copy-start.33
  140.9 7.6 copy-start.35
  140.9 7.6 copy-start.91
  155.1 5.7 copy-start
  155.1 5.7 copy-start.42
  155.1 10.6 slice-start.1
  166.7 42.1 %copy-start.62 = (f32[512]{0:T(512)}, f32[512]{0:T(512)S(1)}, u32[]{:S(2)}) copy-start(f32[512]{0:T(512)S(1)} %broadcast_multiply_fusion.3) | copy-start | bytes 6148
  168.1 21.4 %copy-start.67 = (f32[512]{0:T(512)}, f32[512]{0:T(512)S(1)}, u32[]{:S(2)}) copy-start(f32[512]{0:T(512)S(1)} %multiply_reduce_fusion.5) | copy-start | bytes 6148
  168.2 40.7 %copy-start.75 = (f32[512]{0:T(512)}, f32[512]{0:T(512)S(1)}, u32[]{:S(2)}) copy-start(f32[512]{0:T(512)S(1)} %fusion.112) | copy-start | bytes 6148
  168.2 40.6 %copy-start.18 = (f32[512,768]{1,0:T(8,128)S(1)}, f32[512,768]{1,0:T(8,128)}, u32[]{:S(2)}) copy-start(f32[512,768]{1,0:T(8,128)} %copy-done.17) | copy-start | bytes 4718596
  208.8 6.5 copy-start.72
  214.9 76.6 %copy-start.49 = (bf16[24,192]{1,0:T(8,128)(2,1)S(1)}, bf16[24,192]{1,0:T(8,128)(2,1)}, u32[]{:S(2)}) copy-start(bf16[24,192]{1,0:T(8,128)(2,1)} %param.22) | copy-start | bytes 27652
  214.9 143.4 %copy-start.92 = (bf16[72]{0:T(256)(128)(2,1)S(1)}, bf16[72]{0:T(256)(128)(2,1)}, u32[]{:S(2)}) copy-start(bf16[72]{0:T(256)(128)(2,1)} %param.23) | copy-start | bytes 436
  214.9 143.7 %copy-start.85 = (bf16[288]{0:T(512)(128)(2,1)S(1)}, bf16[288]{0:T(512)(128)(2,1)}, u32[]{:S(2)}) copy-start(bf16[288]{0:T(512)(128)(2,1)} %param.19) | copy-start | bytes 1732
  215.0 182.4 %copy-start.26 = (bf16[512,1,192]{0,2,1:T(8,128)(2,1)S(1)}, bf16[512,1,192]{0,2,1:T(8,128)(2,1)}, u32[]{:S(2)}) copy-start(bf16[512,1,192]{0,2,1:T(8,128)(2,1)} %get-tuple-element.284) | copy-start | bytes 589828
  215.3 185.9 %copy-start.69 = (f32[512]{0:T(512)}, f32[512]{0:T(512)S(1)}, u32[]{:S(2)}) copy-start(f32[512]{0:T(512)S(1)} %multiply_reduce_fusion.4) | copy-start | bytes 6148
  215.3 185.8 %copy-start.58 = (f32[512]{0:T(512)}, f32[512]{0:T(512)S(1)}, u32[]{:S(2)}) copy-start(f32[512]{0:T(512)S(1)} %fusion.113) | copy-start | bytes 6148
  216.6 434.0 %all-gather.15.cloned.1.call-start = ((), (), s32[]{:S(2)}) async-start(), calls=%async_computation.10 | async-start | bytes 4866048 | tf_op jit(solution)/shard_map/all_gather | solution.py:386
  217.2 441.3 %all-gather.17.cloned.1.call-start = ((), (), s32[]{:S(2)}) async-start(), calls=%async_computation.11 | async-start | bytes 4866048 | tf_op jit(solution)/shard_map/all_gather | solution.py:385
  217.8 653.6 %reduce-scatter.17.cloned.1.call-start = ((), (), s32[]{:S(2)}) async-start(), calls=%async_computation.16 | async-start | bytes 811008 | tf_op jit(solution)/shard_map/reduce_scatter | solution.py:441
  397.3 5.1 copy-start.81
  402.5 72.5 %copy-start.50 = (bf16[24,192]{1,0:T(8,128)(2,1)S(1)}, bf16[24,192]{1,0:T(8,128)(2,1)}, u32[]{:S(2)}) copy-start(bf16[24,192]{1,0:T(8,128)(2,1)} %param.22) | copy-start | bytes 27652
  406.2 134.2 %copy-start.52 = (bf16[192,24]{0,1:T(8,128)(2,1)S(1)}, bf16[192,24]{0,1:T(8,128)(2,1)}, u32[]{:S(2)}) copy-start(bf16[192,24]{0,1:T(8,128)(2,1)} %param.21) | copy-start | bytes 27652
  406.2 202.5 %copy-start.90 = (bf16[2304]{0:T(1024)(128)(2,1)S(1)}, bf16[2304]{0:T(1024)(128)(2,1)}, u32[]{:S(2)}) copy-start(bf16[2304]{0:T(1024)(128)(2,1)} %get-tuple-element.264) | copy-start | bytes 13828
  406.2 203.1 %copy-start.39 = (bf16[1,512,192]{1,2,0:T(8,128)(2,1)S(1)}, bf16[1,512,192]{1,2,0:T(8,128)(2,1)}, u32[]{:S(2)}) copy-start(bf16[1,512,192]{1,2,0:T(8,128)(2,1)} %param.25) | copy-start | bytes 589828
  406.3 203.9 %copy-start.87 = (f32[192]{0:T(256)S(1)}, f32[192]{0:T(256)}, u32[]{:S(2)}) copy-start(f32[192]{0:T(256)} %get-tuple-element.302) | copy-start | bytes 2308
  406.3 203.9 %copy-start.88 = (f32[192]{0:T(256)S(1)}, f32[192]{0:T(256)}, u32[]{:S(2)}) copy-start(f32[192]{0:T(256)} %get-tuple-element.303) | copy-start | bytes 2308
  475.0 142.2 %copy-start.28 = (bf16[768,192]{1,0:T(8,128)(2,1)}, bf16[768,192]{1,0:T(8,128)(2,1)S(1)}, u32[]{:S(2)}) copy-start(bf16[768,192]{1,0:T(8,128)(2,1)S(1)} %all_gather.63) | copy-start | bytes 884740
  611.1 7.9 copy-start.56
  612.6 5.5 copy-start.23
  614.0 8.8 copy-start.21
  624.7 25.9 %copy-start.15 = (f32[512,768]{1,0:T(8,128)}, f32[512,768]{1,0:T(8,128)S(1)}, u32[]{:S(2)}) copy-start(f32[512,768]{1,0:T(8,128)S(1)} %get-tuple-element.276) | copy-start | bytes 4718596
  624.7 8.1 copy-start.27
  624.7 8.1 copy-start.31
  632.7 238.6 %reduce-scatter.15.cloned.1.call-start = ((), (), s32[]{:S(2)}) async-start(), calls=%async_computation.15 | async-start | bytes 811008 | tf_op jit(solution)/shard_map/reduce_scatter | solution.py:440
  632.8 87.5 %copy-start.77 = (f32[512]{0:T(512)}, f32[512]{0:T(512)S(1)}, u32[]{:S(2)}) copy-start(f32[512]{0:T(512)S(1)} %negate_multiply_fusion.5) | copy-start | bytes 6148
  639.9 287.2 %reduce-scatter.13.cloned.1.call-start = ((), (), s32[]{:S(2)}) async-start(), calls=%async_computation.14 | async-start | bytes 811008 | tf_op jit(solution)/shard_map/reduce_scatter | solution.py:439
  640.1 10.5 copy-start.19
  640.1 10.5 copy-start.63
  640.1 10.5 copy-start.73
  640.2 10.5 copy-start.76
  650.6 7.2 copy-start.68
  650.6 7.2 copy-start.20
  658.4 116.4 %copy-start.3 = (f32[512,768]{1,0:T(8,128)}, f32[512,768]{1,0:T(8,128)S(1)}, u32[]{:S(2)}) copy-start(f32[512,768]{1,0:T(8,128)S(1)} %get-tuple-element.274) | copy-start | bytes 4718596
  658.5 5.3 copy-start.6
  673.3 22.2 %copy-start.32 = (f32[12,512]{1,0:T(8,128)S(1)}, f32[12,512]{1,0:T(8,128)}, u32[]{:S(2)}) copy-start(f32[12,512]{1,0:T(8,128)} %log_add_fusion) | copy-start | bytes 73732
  673.3 22.2 %copy-start.34 = (bf16[512,1,192]{0,2,1:T(8,128)(2,1)S(1)}, bf16[512,1,192]{0,2,1:T(8,128)(2,1)}, u32[]{:S(2)}) copy-start(bf16[512,1,192]{0,2,1:T(8,128)(2,1)} %get-tuple-element.286) | copy-start | bytes 589828
  673.3 22.2 %copy-start.47 = (f32[12,512]{1,0:T(8,128)S(1)}, f32[12,512]{1,0:T(8,128)}, u32[]{:S(2)}) copy-start(f32[12,512]{1,0:T(8,128)} %get-tuple-element.325) | copy-start | bytes 73732
  695.5 22.0 %copy-start.37 = (bf16[1,512,192]{1,2,0:T(8,128)(2,1)S(1)}, bf16[1,512,192]{1,2,0:T(8,128)(2,1)}, u32[]{:S(2)}) copy-start(bf16[1,512,192]{1,2,0:T(8,128)(2,1)} %param.14) | copy-start | bytes 589828
  695.5 23.5 %copy-start.38 = (f32[192,192]{1,0:T(8,128)S(1)}, f32[192,192]{1,0:T(8,128)}, u32[]{:S(2)}) copy-start(f32[192,192]{1,0:T(8,128)} %fusion.111) | copy-start | bytes 442372
  720.0 348.9 %reduce-scatter.11.cloned.1.call-start = ((), (), s32[]{:S(2)}) async-start(), calls=%async_computation.13 | async-start | bytes 9732096 | tf_op jit(solution)/shard_map/reduce_scatter | solution.py:431
  729.0 481.5 %reduce-scatter.9.cloned.1.call-start = ((), (), s32[]{:S(2)}) async-start(), calls=%async_computation.12 | async-start | bytes 9732096 | tf_op jit(solution)/shard_map/reduce_scatter | solution.py:425
  738.5 613.5 %reduce-scatter.19.cloned.1.call-start = ((), (), s32[]{:S(2)}) async-start(), calls=%async_computation.17 | async-start | bytes 9732096
  746.5 10.0 copy-start.8
  760.3 7.2 copy-start.25
  808.6 56.8 %copy-start.4 = (f32[512,768]{1,0:T(8,128)S(1)}, f32[512,768]{1,0:T(8,128)}, u32[]{:S(2)}) copy-start(f32[512,768]{1,0:T(8,128)} %copy-done.3) | copy-start | bytes 4718596
  808.6 56.8 %copy-start.66 = (f32[512]{0:T(512)S(1)}, f32[512]{0:T(512)}, u32[]{:S(2)}) copy-start(f32[512]{0:T(512)} %copy-done.64) | copy-start | bytes 6148
  (45 other events, 132.3 us)
Sparse Core Ops, SparseCore 0:
  10.9 67.3 all-gather.6
  81.2 62.8 all-gather.8
  147.0 61.8 all-gather.10
  216.7 63.5 all-gather.12
  283.0 62.9 all-gather.14
  348.8 62.5 all-gather.16
  632.8 92.1 reduce-scatter.16
  730.7 95.3 reduce-scatter.14
  831.7 95.3 reduce-scatter.12
  933.4 135.4 reduce-scatter.10
  1075.4 135.0 reduce-scatter.8
  1216.9 135.1 reduce-scatter.18
where the time goes:
time: 1370 us; the launch traced here: 1360 us
  blocking collectives  531 us (39%)
  waiting for transfers between devices  503 us (37%)
  matrix products  203 us (15%)
  local copies, waits for them, and re-layouts  64.3 us (5%)
  other arithmetic  40.8 us (3%)
  between operations  16.5 us (1%)
    unnamed x13, waiting for transfers between devices  145 us
    reduce_scatter x1, waiting for transfers between devices, body(): lax.psum_scatter(jnp.einsum('sf,sd->fd', active_all, second_all, preferre...  142 us
    reduce_scatter x1, waiting for transfers between devices, body(): lax.psum_scatter(jnp.einsum('sd,sf->df', hidden_all, inner_all, preferred...  142 us
    unnamed x3, blocking collectives  119 us
    all_gather x1, blocking collectives, body(): lax.all_gather(layout_w1, ('dp', 'shard'), axis=1, tiled=True)  73.7 us
    all_gather x1, blocking collectives, body(): lax.all_gather(layout_attn, ('dp', 'shard'), axis=0, tiled=True)  69.5 us
    all_gather x1, blocking collectives, body(): lax.all_gather(shards[5], ('dp', 'shard'), axis=1, tiled=True)  68.3 us
    all_gather x1, blocking collectives, body(): lax.all_gather(shards[4], ('dp', 'shard'), axis=0, tiled=True)  68.1 us
  transfers between devices with their start and end apart: 12, of which 5 were waited for; matrix products, arithmetic and copies ran while one was open for 21% of the time, Pallas kernels for 0%

commit v1 on v0

--- a/solution.py
+++ b/solution.py
@@ -330,6 +330,72 @@
     return values.reshape(-1, values.shape[-1])
 
 
+AXES = ("dp", "shard")
+
+
+def small_layout(pieces):
+    flat = jnp.concatenate([piece.reshape(-1) for piece in pieces])
+    rows = -(-flat.shape[0] // 1024) * 8
+    return jnp.pad(flat, (0, rows * 128 - flat.shape[0])).reshape(rows, 128)
+
+
+def gather_small(text_vectors, layout_attn, layout_w1, layout_w2, layout_vectors):
+    pieces = (text_vectors, layout_attn, layout_w1, layout_w2, layout_vectors)
+    packed = small_layout(pieces)
+    rows = packed.shape[0]
+    gathered = lax.all_gather(packed, AXES, axis=0, tiled=True)
+    count = gathered.shape[0] // rows
+    flat = gathered.reshape(count, rows * 128)
+    sizes = [piece.size for piece in pieces]
+    offsets = [sum(sizes[:index]) for index in range(len(sizes))]
+    parts = [flat[:, offset : offset + size] for offset, size in zip(offsets, sizes)]
+    full_text_vectors = parts[0].reshape(-1)
+    full_layout_attn = parts[1].reshape(count * layout_attn.shape[0], layout_attn.shape[1])
+    full_layout_w1 = (
+        parts[2]
+        .reshape(count, layout_w1.shape[0], layout_w1.shape[1])
+        .transpose(1, 0, 2)
+        .reshape(layout_w1.shape[0], count * layout_w1.shape[1])
+    )
+    full_layout_w2 = parts[3].reshape(count * layout_w2.shape[0], layout_w2.shape[1])
+    full_layout_vectors = parts[4].reshape(-1)
+    return (
+        full_text_vectors,
+        full_layout_attn,
+        full_layout_w1,
+        full_layout_w2,
+        full_layout_vectors,
+    )
+
+
+def scatter_small(count, text_vec_grad, layout_attn_grad, layout_w1_grad, layout_w2_grad, layout_vec_grad):
+    local_w1_cols = layout_w1_grad.shape[1] // count
+    blocks = (
+        text_vec_grad.reshape(count, -1),
+        layout_attn_grad.reshape(count, -1),
+        layout_w1_grad.reshape(layout_w1_grad.shape[0], count, local_w1_cols)
+        .transpose(1, 0, 2)
+        .reshape(count, -1),
+        layout_w2_grad.reshape(count, -1),
+        layout_vec_grad.reshape(count, -1),
+    )
+    joined = jnp.concatenate(blocks, 1)
+    width = joined.shape[1]
+    rows = -(-width // 1024) * 8
+    joined = jnp.pad(joined, ((0, 0), (0, rows * 128 - width))).reshape(count * rows, 128)
+    summed = lax.psum_scatter(joined, AXES, scatter_dimension=0, tiled=True).reshape(-1)
+    sizes = [block.shape[1] for block in blocks]
+    offsets = [sum(sizes[:index]) for index in range(len(sizes))]
+    parts = [summed[offset : offset + size] for offset, size in zip(offsets, sizes)]
+    return (
+        parts[0],
+        parts[1].reshape(layout_attn_grad.shape[0] // count, layout_attn_grad.shape[1]),
+        parts[2].reshape(layout_w1_grad.shape[0], local_w1_cols),
+        parts[3].reshape(layout_w2_grad.shape[0] // count, layout_w2_grad.shape[1]),
+        parts[4],
+    )
+
+
 def body(
     text_in,
     layout_in,
@@ -345,19 +411,20 @@
     cot_text,
     cot_layout,
 ):
-    text_full = (
-        lax.all_gather(text_attn, ("dp", "shard"), axis=0, tiled=True),
-        lax.all_gather(text_w1, ("dp", "shard"), axis=0, tiled=True),
-        lax.all_gather(text_w2, ("dp", "shard"), axis=0, tiled=True),
-        lax.all_gather(text_vectors, ("dp", "shard"), axis=0, tiled=True),
-    )
-    layout_full = (
-        lax.all_gather(layout_attn, ("dp", "shard"), axis=0, tiled=True),
-        lax.all_gather(layout_w1, ("dp", "shard"), axis=1, tiled=True),
-        lax.all_gather(layout_w2, ("dp", "shard"), axis=0, tiled=True),
-        lax.all_gather(layout_vectors, ("dp", "shard"), axis=0, tiled=True),
-    )
-    weights = tuple(text_full) + tuple(layout_full)
+    count = lax.psum(1, AXES)
+    full_text_vectors, full_layout_attn, full_layout_w1, full_layout_w2, full_layout_vectors = (
+        gather_small(text_vectors, layout_attn, layout_w1, layout_w2, layout_vectors)
+    )
+    weights = (
+        lax.all_gather(text_attn, AXES, axis=0, tiled=True),
+        lax.all_gather(text_w1, AXES, axis=0, tiled=True),
+        lax.all_gather(text_w2, AXES, axis=0, tiled=True),
+        full_text_vectors,
+        full_layout_attn,
+        full_layout_w1,
+        full_layout_w2,
+        full_layout_vectors,
+    )
 
     def forward_step(carry, page):
         text_rows, layout_rows, length = page
@@ -366,46 +433,18 @@
 
     unused, (outputs, kept_all) = lax.scan(forward_step, None, (text_in, layout_in, lengths))
     out_text, out_layout = outputs
-    shards, unused_out = lax.optimization_barrier(
-        (
-            (
-                text_attn,
-                text_w1,
-                text_w2,
-                text_vectors,
-                layout_attn,
-                layout_w1,
-                layout_w2,
-                layout_vectors,
-            ),
-            out_text,
-        )
-    )
-    text_back = (
-        lax.all_gather(shards[0], ("dp", "shard"), axis=0, tiled=True),
-        lax.all_gather(shards[1], ("dp", "shard"), axis=0, tiled=True),
-        lax.all_gather(shards[2], ("dp", "shard"), axis=0, tiled=True),
-        lax.all_gather(shards[3], ("dp", "shard"), axis=0, tiled=True),
-    )
-    layout_back = (
-        lax.all_gather(shards[4], ("dp", "shard"), axis=0, tiled=True),
-        lax.all_gather(shards[5], ("dp", "shard"), axis=1, tiled=True),
-        lax.all_gather(shards[6], ("dp", "shard"), axis=0, tiled=True),
-        lax.all_gather(shards[7], ("dp", "shard"), axis=0, tiled=True),
-    )
-    back_weights = tuple(text_back) + tuple(layout_back)
     zeros = (
-        jnp.zeros(back_weights[3].shape, jnp.float32),
-        jnp.zeros(back_weights[4].shape, jnp.float32),
-        jnp.zeros(back_weights[5].shape, jnp.float32),
-        jnp.zeros(back_weights[6].shape, jnp.float32),
-        jnp.zeros(back_weights[7].shape, jnp.float32),
+        jnp.zeros(weights[3].shape, jnp.float32),
+        jnp.zeros(weights[4].shape, jnp.float32),
+        jnp.zeros(weights[5].shape, jnp.float32),
+        jnp.zeros(weights[6].shape, jnp.float32),
+        jnp.zeros(weights[7].shape, jnp.float32),
     )
 
     def backward_step(running, page):
         text_rows, layout_rows, length, kept_page, text_cot, layout_cot = page
         in_grads, small_terms, text_operands = page_backward(
-            text_rows, layout_rows, length, kept_page, text_cot, layout_cot, back_weights
+            text_rows, layout_rows, length, kept_page, text_cot, layout_cot, weights
         )
         return (add_all(running, small_terms), (in_grads, text_operands))
 
@@ -417,31 +456,24 @@
     three_all, first_all, hidden_all, inner_all, active_all, second_all = tuple(
         (flat_rows(values) for values in text_operands)
     )
+    grad_second = lax.psum_scatter(
+        jnp.einsum("sf,sd->fd", active_all, second_all, preferred_element_type=jnp.float32),
+        AXES,
+        scatter_dimension=0,
+        tiled=True,
+    )
+    grad_first = lax.psum_scatter(
+        jnp.einsum("sd,sf->df", hidden_all, inner_all, preferred_element_type=jnp.float32),
+        AXES,
+        scatter_dimension=0,
+        tiled=True,
+    )
     three_part = jnp.einsum("sd,se->de", inputs_all, three_all, preferred_element_type=jnp.float32)
     out_part = jnp.einsum("sd,se->de", context_all, first_all, preferred_element_type=jnp.float32)
     grad_attn = lax.psum_scatter(
-        jnp.concatenate([three_part, out_part], 1), ("dp", "shard"), scatter_dimension=0, tiled=True
-    )
-    grad_first = lax.psum_scatter(
-        jnp.einsum("sd,sf->df", hidden_all, inner_all, preferred_element_type=jnp.float32),
-        ("dp", "shard"),
-        scatter_dimension=0,
-        tiled=True,
-    )
-    grad_second = lax.psum_scatter(
-        jnp.einsum("sf,sd->fd", active_all, second_all, preferred_element_type=jnp.float32),
-        ("dp", "shard"),
-        scatter_dimension=0,
-        tiled=True,
-    )
-    text_summed = (lax.psum_scatter(totals[0], ("dp", "shard"), scatter_dimension=0, tiled=True),)
-    layout_summed = (
-        lax.psum_scatter(totals[1], ("dp", "shard"), scatter_dimension=0, tiled=True),
-        lax.psum_scatter(totals[2], ("dp", "shard"), scatter_dimension=1, tiled=True),
-        lax.psum_scatter(totals[3], ("dp", "shard"), scatter_dimension=0, tiled=True),
-        lax.psum_scatter(totals[4], ("dp", "shard"), scatter_dimension=0, tiled=True),
-    )
-    summed = tuple(text_summed) + tuple(layout_summed)
+        jnp.concatenate([three_part, out_part], 1), AXES, scatter_dimension=0, tiled=True
+    )
+    summed = scatter_small(count, *totals)
     return (
         out_text,
         out_layout,

time: 1370 us -> 934 us (0.68)
  blocking collectives: 531 us -> 77.7 us
  waiting for transfers between devices: 503 us -> 546 us
  matrix products: 203 us -> 177 us
    all_gather x6 -> x1, blocking collectives: 412 us -> 77.7 us  [gather_small(): gathered = lax.all_gather(packed, AXES, axis=0, tiled=True)]
    unnamed x3 -> x0, blocking collectives: 119 us -> none
    all_gather x6 -> x3, waiting for transfers between devices: 19.4 us -> 47.2 us  [the longest x1 43.7 us: body(): lax.all_gather(text_w2, AXES, axis=0, tiled=True)]
    reduce_scatter x3 -> x1, waiting for transfers between devices: 55.8 us -> 80.4 us  [scatter_small(): lax.psum_scatter(joined, AXES, scatter_dimension=0, tiled=True).reshape(-1)]
    reshape x0 -> x16, local copies, waits for them, and re-layouts: none -> 15.8 us  [the longest x1 3.51 us: scatter_small(): blocks = (text_vec_grad.reshape(count, -1), layout_attn_grad.reshape(coun...]
    unnamed x211 -> x220, local copies, waits for them, and re-layouts: 41.8 us -> 26.3 us
    unnamed x13 -> x8, waiting for transfers between devices: 145 us -> 135 us
  transfers between devices with their start and end apart: 12 -> 7, of which waited for: 5 -> 6; matrix products, arithmetic and copies ran while one was open for 21% -> 13% of each run, Pallas kernels for 0% -> 0%
where the time goes in v1:
time: 934 us; the launch traced here: 929 us
  waiting for transfers between devices  546 us (58%)
  matrix products  177 us (19%)
  blocking collectives  77.7 us (8%)
  local copies, waits for them, and re-layouts  76 us (8%)
  other arithmetic  35.7 us (4%)
  between operations  16.5 us (2%)
    reduce_scatter x1, waiting for transfers between devices, body(): lax.psum_scatter(jnp.einsum('sd,sf->df', hidden_all, inner_all, preferred...  142 us
    reduce_scatter x1, waiting for transfers between devices, body(): lax.psum_scatter(jnp.einsum('sf,sd->fd', active_all, second_all, preferre...  142 us
    unnamed x8, waiting for transfers between devices  135 us
    reduce_scatter x1, waiting for transfers between devices, scatter_small(): lax.psum_scatter(joined, AXES, scatter_dimension=0, tiled=True).reshape(-1)  80.4 us
    all_gather x1, blocking collectives, gather_small(): gathered = lax.all_gather(packed, AXES, axis=0, tiled=True)  77.7 us
    all_gather x1, waiting for transfers between devices, body(): lax.all_gather(text_w2, AXES, axis=0, tiled=True)  43.7 us
    unnamed x220, local copies, waits for them, and re-layouts  26.3 us
    dot_general x2, matrix products, branch_forward(): jnp.dot(hidden.astype(jnp.bfloat16), first, preferred_element_type=jnp.fl...  24.9 us
  transfers between devices with their start and end apart: 7, of which 6 were waited for; matrix products, arithmetic and copies ran while one was open for 13% of the time, Pallas kernels for 0%

profile of v1, /device:TPU:0, one launch (start us, length us, event | category | flops | bytes accessed | tf_op | source)
XLA Modules:
  0.0 929.5 jit_solution(4497999975157312483)
XLA Ops:
  12.0 1.4 concatenate.25
  13.5 77.7 %all_gather.13 = bf16[3584,128]{1,0:T(8,128)(2,1)S(1)} all-gather(bf16[112,128]{1,0:T(8,128)(2,1)S(1)} %pad_bitcast_fusion), channel_id=1, replica_groups=mesh['dp'=8,'shard'=4] {'dp','shard'}, dimensions={0}, use_global_device_ids=true | all-gather | bytes 946176 | tf_op jit(solution)/shard_map/all_gather | solution.py:346
  97.6 2.5 reshape.404
  100.1 1.6 copy.84
  104.3 2.0 slice-done.9
  106.3 3.6 copy.119
  109.9 4.2 add_convert_fusion.1
  114.9 6.3 fusion.127
  121.2 1.2 copy.78
  122.5 7.2 fusion.120
  129.6 1.9 fusion.2
  131.5 3.8 copy-done
  135.3 2.3 divide_convert_fusion
  138.8 1.5 copy-done.1
  142.5 3.5 all-gather.6.cloned.1.call-done
  146.0 21.2 %multiply_convert_fusion = (bf16[512,3072]{1,0:T(8,128)(2,1)}, f32[512,3072]{1,0:T(8,128)}, f32[512,3072]{1,0:T(8,128)}) fusion(f32[3072]{0:T(1024)} %slice.257, bf16[768,3072]{1,0:T(8,128)(2,1)} %all-gather.6.cloned.1.call-done, f32[512,768]{1,0:T(8,128)} %copy-done.11, f32[768]{0:T(1024)} %get-tuple-element.275, f32[768]{0:T(1024)} %get-tuple-element.276, ...), kind=kOutput, calls=%fused_computation.18 | convolution fusion | flops 2521694208 | bytes 22042624 | tf_op jit(solution)/shard_map/while/body/eval_jaxpr/dot_general | solution.py:164
  167.1 43.7 %all-gather.8.cloned.1.call-done = bf16[3072,768]{1,0:T(8,128)(2,1)} async-done(((bf16[96,768]{1,0:T(8,128)(2,1)}), bf16[3072,768]{1,0:T(8,128)(2,1)}) %all-gather.8.cloned.1.call-update) | async-done | bytes 4718608 | tf_op jit(solution)/shard_map/all_gather | solution.py:421
  210.8 6.1 fusion.122
  217.3 1.3 fusion.31
  218.6 1.7 fusion.110
  220.3 9.0 fusion.125
  229.4 3.6 multiply_reduce_fusion.2
  235.0 7.6 fusion.45
  242.6 9.0 multiply_reduce_fusion.1
  251.6 7.1 fusion.3
  258.7 2.9 multiply_convert_fusion.1
  261.6 1.1 multiply_convert_fusion.2
  265.3 3.7 multiply_convert_fusion.3
  271.3 1.5 fusion.126
  272.8 1.2 multiply_reduce_fusion.6
  274.4 2.4 fusion.67
  276.9 6.6 fusion.128
  283.5 21.9 %fusion.61 = bf16[12,16,512]{2,1,0:T(8,128)(2,1)} fusion(bf16[512,12,16]{0,2,1:T(8,128)(2,1)} %bitcast.189, f32[12,512,512]{1,2,0:T(8,128)} %fusion.128, f32[12,512,512]{1,2,0:T(8,128)} %get-tuple-element.304, f32[12,512,512]{1,2,0:T(8,128)} %copy-done, f32[12,512]{1,0:T(8,128)} %copy-done.50, f32[12,512]{1,0:T(8,128)} %copy-done.31), kind=kOutput, calls=%fused_computation.107 | convolution fusion | flops 129178112 | bytes 38191104 | tf_op jit(solution)/shard_map/while/body/eval_jaxpr/hqk,qhd->khd/dot_general | solution.py:128
  305.4 21.9 %fusion.64 = bf16[12,16,512]{2,1,0:T(8,128)(2,1)} fusion(bf16[512,12,16]{0,2,1:T(8,128)(2,1)} %bitcast.187, f32[12,512,512]{1,2,0:T(8,128)} %fusion.128, f32[12,512,512]{1,2,0:T(8,128)} %get-tuple-element.304, f32[12,512,512]{1,2,0:T(8,128)} %copy-done, f32[12,512]{1,0:T(8,128)} %copy-done.50, f32[12,512]{1,0:T(8,128)} %copy-done.31), kind=kOutput, calls=%fused_computation.108 | convolution fusion | flops 129178112 | bytes 38191104 | tf_op jit(solution)/shard_map/while/body/eval_jaxpr/hqk,khd->qhd/dot_general | solution.py:122
  327.4 1.6 add_reduce_fusion
  329.0 2.3 add_reduce_fusion.1
  332.1 1.4 fusion.82
  333.5 1.3 fusion.90
  334.8 1.2 fusion.87
  336.4 2.3 copy.91
  338.7 2.3 copy.90
  341.1 1.1 copy.89
  342.2 3.6 convert_reduce_fusion
  348.4 2.3 copy.99
  350.6 3.5 reshape.413
  355.4 2.6 concatenate.30
  358.1 2.8 pad.9
  360.9 2.8 reshape.416
  363.8 4.5 copy.96
  368.3 2.4 fusion.101
  370.7 4.9 convolution_bitcast_fusion
  375.6 8.0 pad_maximum_fusion
  383.6 9.7 %copy.117 = f32[768,3072]{1,0:T(8,128)} copy(f32[768,3072]{0,1:T(8,128)} %pad_maximum_fusion) | data formatting | bytes 18874368
  393.3 1.3 copy-done.13
  394.7 7.2 fusion.33
  401.9 1.3 copy-done.15
  403.3 8.3 fusion.99
  413.9 5.8 fusion.32
  419.8 80.4 %reduce-scatter.11.cloned.1.call-done = f32[112,128]{1,0:T(8,128)} async-done(((f32[3584,128]{1,0:T(8,128)}), f32[112,128]{1,0:T(8,128)}) %reduce-scatter.11.cloned.1.call-update) | async-done | bytes 57360 | tf_op jit(solution)/shard_map/reduce_scatter | solution.py:386
  500.2 1.3 slice.276
  501.5 1.3 slice.280
  505.8 133.0 %reduce-scatter.13.cloned.1.call-done = f32[24,3072]{1,0:T(8,128)} async-done(((f32[768,3072]{1,0:T(8,128)}), f32[24,3072]{1,0:T(8,128)}) %reduce-scatter.13.cloned.1.call-update) | async-done | bytes 294928
  638.8 141.7 %reduce-scatter.7.cloned.1.call-done = f32[24,3072]{1,0:T(8,128)} async-done(((f32[768,3072]{1,0:T(8,128)}), f32[24,3072]{1,0:T(8,128)}) %reduce-scatter.7.cloned.1.call-update) | async-done | bytes 294928 | tf_op jit(solution)/shard_map/reduce_scatter | solution.py:465
  780.6 141.6 %reduce-scatter.9.cloned.1.call-done = f32[96,768]{1,0:T(8,128)} async-done(((f32[3072,768]{1,0:T(8,128)}), f32[96,768]{1,0:T(8,128)}) %reduce-scatter.9.cloned.1.call-update) | async-done | bytes 294928 | tf_op jit(solution)/shard_map/reduce_scatter | solution.py:459
  (317 shorter events, 34.7 us)
Async XLA Ops:
  7.2 88.0 %copy-start.43 = (bf16[1,512,192]{1,2,0:T(8,128)(2,1)S(1)}, bf16[1,512,192]{1,2,0:T(8,128)(2,1)}, u32[]{:S(2)}) copy-start(bf16[1,512,192]{1,2,0:T(8,128)(2,1)} %param.14) | copy-start | bytes 589828
  7.2 97.1 %all-gather.4.cloned.1.call-start = ((), (), s32[]{:S(2)}) async-start(), calls=%async_computation.4 | async-start | bytes 4866048 | tf_op jit(solution)/shard_map/all_gather | solution.py:419
  7.9 138.1 %all-gather.6.cloned.1.call-start = ((), (), s32[]{:S(2)}) async-start(), calls=%async_computation.5 | async-start | bytes 4866048 | tf_op jit(solution)/shard_map/all_gather | solution.py:420
  8.7 202.1 %all-gather.8.cloned.1.call-start = ((), (), s32[]{:S(2)}) async-start(), calls=%async_computation.6 | async-start | bytes 4866048 | tf_op jit(solution)/shard_map/all_gather | solution.py:421
  9.4 490.8 %reduce-scatter.11.cloned.1.call-start = ((), (), s32[]{:S(2)}) async-start(), calls=%async_computation.9 | async-start | bytes 1892352 | tf_op jit(solution)/shard_map/reduce_scatter | solution.py:386
  93.9 175.2 %copy-start.52 = (f32[192]{0:T(256)}, f32[192]{0:T(256)S(1)}, u32[]{:S(2)}) copy-start(f32[192]{0:T(256)S(1)} %get-tuple-element.284) | copy-start | bytes 2308
  114.5 6.7 copy-start.7
  114.8 6.4 copy-start.4
  114.8 7.6 copy-start.33
  114.9 7.6 copy-start.34
  114.9 7.6 copy-start.90
  129.6 5.7 copy-start
  129.6 10.7 %slice-start.5 = ((s8[4718592]{0:T(1024)(128)(4,1)}), s8[4194304]{0:T(1024)(128)(4,1)S(1)}, s32[]{:S(2)}) async-start(s8[4718592]{0:T(1024)(128)(4,1)} %bitcast.157), calls=%async_computation.16 | async-start | bytes 8388608
  135.3 5.0 slice-start.6
  141.3 91.8 %copy-start.55 = (f32[512]{0:T(512)}, f32[512]{0:T(512)S(1)}, u32[]{:S(2)}) copy-start(f32[512]{0:T(512)S(1)} %broadcast_multiply_fusion.3) | copy-start | bytes 6148
  142.4 90.7 %copy-start.71 = (f32[512]{0:T(512)}, f32[512]{0:T(512)S(1)}, u32[]{:S(2)}) copy-start(f32[512]{0:T(512)S(1)} %fusion.92) | copy-start | bytes 6148
  142.5 109.1 %copy-start.31 = (f32[12,512]{1,0:T(8,128)}, f32[12,512]{1,0:T(8,128)S(1)}, u32[]{:S(2)}) copy-start(f32[12,512]{1,0:T(8,128)S(1)} %log_add_fusion) | copy-start | bytes 73732
  146.0 64.8 %copy-start.12 = (f32[512,768]{1,0:T(8,128)S(1)}, f32[512,768]{1,0:T(8,128)}, u32[]{:S(2)}) copy-start(f32[512,768]{1,0:T(8,128)} %copy-done.11) | copy-start | bytes 4718596
  146.0 64.8 %copy-start.63 = (f32[768]{0:T(1024)S(1)}, f32[768]{0:T(1024)}, u32[]{:S(2)}) copy-start(f32[768]{0:T(1024)} %get-tuple-element.276) | copy-start | bytes 9220
  146.0 64.8 %copy-start.81 = (f32[768]{0:T(1024)S(1)}, f32[768]{0:T(1024)}, u32[]{:S(2)}) copy-start(f32[768]{0:T(1024)} %get-tuple-element.275) | copy-start | bytes 9220
  146.0 64.8 %copy-start.83 = (f32[768]{0:T(1024)S(1)}, f32[768]{0:T(1024)}, u32[]{:S(2)}) copy-start(f32[768]{0:T(1024)} %get-tuple-element.274) | copy-start | bytes 9220
  210.8 6.4 copy-start.24
  218.6 10.8 %slice-start.10 = ((s8[4718592]{0:T(1024)(128)(4,1)}), s8[524288]{0:T(1024)(128)(4,1)S(1)}, s32[]{:S(2)}) async-start(s8[4718592]{0:T(1024)(128)(4,1)} %bitcast.208), calls=%async_computation.21 | async-start | bytes 1048576
  220.3 9.1 copy-start.14
  220.3 9.1 copy-start.73
  220.3 9.1 slice-start.11
  233.8 8.9 copy-start.57
  234.9 7.7 copy-start.3
  234.9 16.6 %slice-start = ((s8[12582912]{0:T(1024)(128)(4,1)}), s8[4194304]{0:T(1024)(128)(4,1)S(1)}, s32[]{:S(2)}) async-start(s8[12582912]{0:T(1024)(128)(4,1)} %bitcast.153), calls=%async_computation.11 | async-start | bytes 8388608
  235.0 16.6 %slice-start.1 = ((s8[12582912]{0:T(1024)(128)(4,1)}), s8[4194304]{0:T(1024)(128)(4,1)S(1)}, s32[]{:S(2)}) async-start(s8[12582912]{0:T(1024)(128)(4,1)} %bitcast.153), calls=%async_computation.12 | async-start | bytes 8388608
  242.6 9.0 slice-start.2
  251.6 7.1 copy-start.50
  251.6 7.1 copy-start.8
  265.3 5.1 copy-start.78
  274.2 62.0 %copy-start.16 = (f32[512,192]{0,1:T(8,128)}, f32[512,192]{0,1:T(8,128)S(1)}, u32[]{:S(2)}) copy-start(f32[512,192]{0,1:T(8,128)S(1)} %get-tuple-element.248) | copy-start | bytes 1179652
  327.3 4.8 copy-start.21
  327.3 4.8 copy-start.54
  327.4 4.8 copy-start.69
  327.4 6.1 copy-start.19
  329.0 5.9 copy-start.37
  329.0 5.9 copy-start.45
  329.0 5.9 copy-start.46
  329.0 5.9 copy-start.48
  341.0 4.8 copy-start.51
  341.0 4.9 copy-start.62
  341.0 4.9 copy-start.87
  341.0 4.9 copy-start.86
  341.0 4.9 copy-start.61
  341.0 4.9 copy-start.60
  341.0 4.9 copy-start.59
  341.0 5.0 copy-start.66
  341.1 5.1 copy-start.36
  342.2 6.1 copy-start.23
  348.4 5.8 copy-start.22
  350.6 4.6 copy-start.76
  350.6 4.6 copy-start.77
  350.6 4.6 copy-start.79
  350.6 4.6 copy-start.80
  350.6 4.6 copy-start.88
  363.7 4.6 copy-start.10
  363.7 4.6 copy-start.58
  363.7 275.1 %reduce-scatter.13.cloned.1.call-start = ((), (), s32[]{:S(2)}) async-start(), calls=%async_computation.10 | async-start | bytes 9732096
  393.3 387.3 %reduce-scatter.7.cloned.1.call-start = ((), (), s32[]{:S(2)}) async-start(), calls=%async_computation.7 | async-start | bytes 9732096 | tf_op jit(solution)/shard_map/reduce_scatter | solution.py:465
  401.9 520.3 %reduce-scatter.9.cloned.1.call-start = ((), (), s32[]{:S(2)}) async-start(), calls=%async_computation.8 | async-start | bytes 9732096 | tf_op jit(solution)/shard_map/reduce_scatter | solution.py:459
  (48 other events, 111.7 us)
Sparse Core Ops, SparseCore 0:
  10.9 70.5 all-gather.3
  84.4 61.5 all-gather.5
  148.9 61.8 all-gather.7
  363.9 136.3 reduce-scatter.10
  506.5 132.2 reduce-scatter.12
  645.2 135.3 reduce-scatter.6
  787.0 135.1 reduce-scatter.8

commit v2 on v1

--- a/solution.py
+++ b/solution.py
@@ -2,6 +2,7 @@
 import jax.numpy as jnp
 from jax import lax
 from jax.sharding import PartitionSpec as P
+
 
 H = 12
 HD = 64
@@ -175,7 +176,7 @@
     first_res, inner, second_res = kept_rows
     pieces = vector_parts(packed.astype(jnp.float32), width)
     hidden, first_pull = jax.vjp(normalize, first_res, pieces[3], pieces[4])
-    unused, second_pull = jax.vjp(normalize, second_res, pieces[6], pieces[7])
+    _, second_pull = jax.vjp(normalize, second_res, pieces[6], pieces[7])
     grad_second, late_scale, late_shift = second_pull(grad_out)
     round_second = grad_second.astype(jnp.bfloat16)
     activated, gelu_pull = jax.vjp(gelu_exact, inner)
@@ -243,7 +244,7 @@
     return (outputs, kept_page)
 
 
-def page_backward(text_rows, layout_rows, length, kept_page, text_cot, layout_cot, weights):
+def page_back_ffn(length, kept_page, text_cot, layout_cot, weights):
     (
         text_attn,
         text_first,
@@ -254,13 +255,13 @@
         layout_second,
         layout_packed,
     ) = weights
-    text_three, layout_three, text_ctx, layout_ctx, log_total, text_kept, layout_kept = kept_page
-    width = text_rows.shape[1]
-    narrow = layout_rows.shape[1]
-    slots = text_rows.shape[0]
+    _, _, _, _, _, text_kept, layout_kept = kept_page
+    width = text_attn.shape[0]
+    narrow = layout_attn.shape[1]
+    slots = text_cot.shape[0]
     valid = jnp.arange(slots, dtype=jnp.int32) < length
     mask = valid[:, None].astype(jnp.float32)
-    text_res_grad, text_ctx_grad, text_ops, text_sums = branch_backward(
+    text_back = branch_backward(
         text_attn,
         text_packed,
         text_first,
@@ -270,7 +271,7 @@
         text_kept,
         text_cot.astype(jnp.float32) * mask,
     )
-    layout_res_grad, layout_ctx_grad, layout_ops, layout_sums = branch_backward(
+    layout_back = branch_backward(
         layout_attn,
         layout_packed,
         layout_first,
@@ -280,6 +281,18 @@
         layout_kept,
         layout_cot.astype(jnp.float32) * mask,
     )
+    return (text_back, layout_back)
+
+
+def page_back_attn(text_rows, layout_rows, length, kept_page, text_back, layout_back, weights):
+    (text_attn, _, _, _, layout_attn, _, _, _) = weights
+    text_three, layout_three, _, layout_ctx, log_total, _, _ = kept_page
+    width = text_rows.shape[1]
+    narrow = layout_rows.shape[1]
+    slots = text_rows.shape[0]
+    valid = jnp.arange(slots, dtype=jnp.int32) < length
+    text_res_grad, text_ctx_grad, _, text_sums = text_back
+    layout_res_grad, layout_ctx_grad, layout_ops, layout_sums = layout_back
     text_three_grad, layout_three_grad = attend_back(
         text_three, layout_three, valid, log_total, text_ctx_grad, layout_ctx_grad
     )
@@ -303,15 +316,6 @@
     )
     layout_vec_grad = jnp.concatenate([layout_query_bias, layout_value_bias] + list(layout_sums))
     text_vec_grad = jnp.concatenate([text_query_bias, text_value_bias] + list(text_sums))
-    text_hidden, text_active, text_first_low, text_second_low, text_inner_low = text_ops
-    text_operands = (
-        text_rounded.reshape(slots, 3 * width),
-        text_first_low,
-        text_hidden,
-        text_inner_low,
-        text_active,
-        text_second_low,
-    )
     small_terms = (
         text_vec_grad,
         layout_attn_grad,
@@ -319,11 +323,7 @@
         layout_second_grad,
         layout_vec_grad,
     )
-    return ((text_in_grad, layout_in_grad), small_terms, text_operands)
-
-
-def add_all(running, terms):
-    return tuple((before + addend for before, addend in zip(running, terms)))
+    return ((text_in_grad, layout_in_grad), small_terms, text_rounded.reshape(slots, 3 * width))
 
 
 def flat_rows(values):
@@ -333,44 +333,57 @@
 AXES = ("dp", "shard")
 
 
-def small_layout(pieces):
+def rows_for(size, width, aligned):
+    rows = -(-size // width)
+    if aligned:
+        rows = -(-rows // 8) * 8
+    return rows
+
+
+def pack_rows(pieces, width, aligned):
     flat = jnp.concatenate([piece.reshape(-1) for piece in pieces])
-    rows = -(-flat.shape[0] // 1024) * 8
-    return jnp.pad(flat, (0, rows * 128 - flat.shape[0])).reshape(rows, 128)
-
-
-def gather_small(text_vectors, layout_attn, layout_w1, layout_w2, layout_vectors):
-    pieces = (text_vectors, layout_attn, layout_w1, layout_w2, layout_vectors)
-    packed = small_layout(pieces)
-    rows = packed.shape[0]
-    gathered = lax.all_gather(packed, AXES, axis=0, tiled=True)
-    count = gathered.shape[0] // rows
-    flat = gathered.reshape(count, rows * 128)
-    sizes = [piece.size for piece in pieces]
+    rows = rows_for(flat.shape[0], width, aligned)
+    return jnp.pad(flat, (0, rows * width - flat.shape[0])).reshape(rows, width)
+
+
+def unpack_small(flat, count, shapes):
+    sizes = [rows * cols for rows, cols in shapes]
     offsets = [sum(sizes[:index]) for index in range(len(sizes))]
     parts = [flat[:, offset : offset + size] for offset, size in zip(offsets, sizes)]
-    full_text_vectors = parts[0].reshape(-1)
-    full_layout_attn = parts[1].reshape(count * layout_attn.shape[0], layout_attn.shape[1])
-    full_layout_w1 = (
-        parts[2]
-        .reshape(count, layout_w1.shape[0], layout_w1.shape[1])
-        .transpose(1, 0, 2)
-        .reshape(layout_w1.shape[0], count * layout_w1.shape[1])
-    )
-    full_layout_w2 = parts[3].reshape(count * layout_w2.shape[0], layout_w2.shape[1])
-    full_layout_vectors = parts[4].reshape(-1)
+    (attn_rows, attn_cols), (w1_rows, w1_cols), (w2_rows, w2_cols) = shapes[1:4]
     return (
-        full_text_vectors,
-        full_layout_attn,
-        full_layout_w1,
-        full_layout_w2,
-        full_layout_vectors,
-    )
-
-
-def scatter_small(count, text_vec_grad, layout_attn_grad, layout_w1_grad, layout_w2_grad, layout_vec_grad):
+        parts[0].reshape(-1),
+        parts[1].reshape(count * attn_rows, attn_cols),
+        parts[2].reshape(count, w1_rows, w1_cols).transpose(1, 0, 2).reshape(w1_rows, count * w1_cols),
+        parts[3].reshape(count * w2_rows, w2_cols),
+        parts[4].reshape(-1),
+    )
+
+
+def gather_weights(text_attn, text_w1, text_w2, text_vectors, layout_attn, layout_w1, layout_w2, layout_vectors):
+    rows, width = text_attn.shape
+    aligned = rows % 8 == 0
+    small = (text_vectors, layout_attn, layout_w1, layout_w2, layout_vectors)
+    small_rows = pack_rows(small, width, aligned)
+    first = jnp.concatenate([text_attn, small_rows], 0)
+    first_all = lax.all_gather(first, AXES, axis=0, tiled=True)
+    count = first_all.shape[0] // first.shape[0]
+    first_all = first_all.reshape(count, first.shape[0], width)
+    full_attn = first_all[:, :rows].reshape(count * rows, width)
+    small_flat = first_all[:, rows:].reshape(count, -1)
+    shapes = [(1, text_vectors.shape[0]), layout_attn.shape, layout_w1.shape, layout_w2.shape, (1, layout_vectors.shape[0])]
+    full_small = unpack_small(small_flat, count, shapes)
+    w2_rows = text_w2.shape[0]
+    second = jnp.concatenate([text_w1, text_w2.reshape(rows, -1)], 0)
+    second_all = lax.all_gather(second, AXES, axis=0, tiled=True).reshape(count, 2 * rows, width)
+    full_w1 = second_all[:, :rows].reshape(count * rows, width)
+    full_w2 = second_all[:, rows:].reshape(count * w2_rows, text_w2.shape[1])
+    return (full_attn, full_w1, full_w2) + full_small
+
+
+def small_blocks(count, text_vec_grad, layout_attn_grad, layout_w1_grad, layout_w2_grad, layout_vec_grad):
     local_w1_cols = layout_w1_grad.shape[1] // count
-    blocks = (
+    return (
         text_vec_grad.reshape(count, -1),
         layout_attn_grad.reshape(count, -1),
         layout_w1_grad.reshape(layout_w1_grad.shape[0], count, local_w1_cols)
@@ -379,21 +392,43 @@
         layout_w2_grad.reshape(count, -1),
         layout_vec_grad.reshape(count, -1),
     )
+
+
+def scatter_late(count, grad_attn, small_grads):
+    width = grad_attn.shape[1]
+    rows = grad_attn.shape[0] // count
+    blocks = small_blocks(count, *small_grads)
     joined = jnp.concatenate(blocks, 1)
-    width = joined.shape[1]
-    rows = -(-width // 1024) * 8
-    joined = jnp.pad(joined, ((0, 0), (0, rows * 128 - width))).reshape(count * rows, 128)
-    summed = lax.psum_scatter(joined, AXES, scatter_dimension=0, tiled=True).reshape(-1)
+    size = joined.shape[1]
+    small_rows = rows_for(size, width, rows % 8 == 0)
+    joined = jnp.pad(joined, ((0, 0), (0, small_rows * width - size))).reshape(count, small_rows, width)
+    packed = jnp.concatenate([grad_attn.reshape(count, rows, width), joined], 1)
+    summed = lax.psum_scatter(packed.reshape(-1, width), AXES, scatter_dimension=0, tiled=True)
+    attn_part = summed[:rows]
+    flat = summed[rows:].reshape(-1)
     sizes = [block.shape[1] for block in blocks]
     offsets = [sum(sizes[:index]) for index in range(len(sizes))]
-    parts = [summed[offset : offset + size] for offset, size in zip(offsets, sizes)]
+    parts = [flat[offset : offset + size] for offset, size in zip(offsets, sizes)]
+    _, layout_attn_grad, layout_w1_grad, layout_w2_grad, _ = small_grads
+    local_w1_cols = layout_w1_grad.shape[1] // count
     return (
+        attn_part,
         parts[0],
         parts[1].reshape(layout_attn_grad.shape[0] // count, layout_attn_grad.shape[1]),
         parts[2].reshape(layout_w1_grad.shape[0], local_w1_cols),
         parts[3].reshape(layout_w2_grad.shape[0] // count, layout_w2_grad.shape[1]),
         parts[4],
     )
+
+
+def scatter_early(count, grad_first, grad_second):
+    width = grad_first.shape[1]
+    rows = grad_first.shape[0] // count
+    packed = jnp.concatenate(
+        [grad_first.reshape(count, rows, width), grad_second.reshape(count, rows, width)], 1
+    )
+    summed = lax.psum_scatter(packed.reshape(-1, width), AXES, scatter_dimension=0, tiled=True)
+    return (summed[:rows], summed[rows:].reshape(-1, grad_second.shape[1]))
 
 
 def body(
@@ -412,81 +447,49 @@
     cot_layout,
 ):
     count = lax.psum(1, AXES)
-    full_text_vectors, full_layout_attn, full_layout_w1, full_layout_w2, full_layout_vectors = (
-        gather_small(text_vectors, layout_attn, layout_w1, layout_w2, layout_vectors)
-    )
-    weights = (
-        lax.all_gather(text_attn, AXES, axis=0, tiled=True),
-        lax.all_gather(text_w1, AXES, axis=0, tiled=True),
-        lax.all_gather(text_w2, AXES, axis=0, tiled=True),
-        full_text_vectors,
-        full_layout_attn,
-        full_layout_w1,
-        full_layout_w2,
-        full_layout_vectors,
-    )
-
-    def forward_step(carry, page):
-        text_rows, layout_rows, length = page
-        outputs, kept_page = page_forward(text_rows, layout_rows, length, weights)
-        return (carry, (outputs, kept_page))
-
-    unused, (outputs, kept_all) = lax.scan(forward_step, None, (text_in, layout_in, lengths))
+    weights = gather_weights(
+        text_attn, text_w1, text_w2, text_vectors, layout_attn, layout_w1, layout_w2, layout_vectors
+    )
+
+    page_weights = (None,) * len(weights)
+    outputs, kept_all = jax.vmap(page_forward, in_axes=(0, 0, 0, page_weights))(
+        text_in, layout_in, lengths, weights
+    )
     out_text, out_layout = outputs
-    zeros = (
-        jnp.zeros(weights[3].shape, jnp.float32),
-        jnp.zeros(weights[4].shape, jnp.float32),
-        jnp.zeros(weights[5].shape, jnp.float32),
-        jnp.zeros(weights[6].shape, jnp.float32),
-        jnp.zeros(weights[7].shape, jnp.float32),
-    )
-
-    def backward_step(running, page):
-        text_rows, layout_rows, length, kept_page, text_cot, layout_cot = page
-        in_grads, small_terms, text_operands = page_backward(
-            text_rows, layout_rows, length, kept_page, text_cot, layout_cot, weights
-        )
-        return (add_all(running, small_terms), (in_grads, text_operands))
-
-    totals, ((text_grad, layout_grad), text_operands) = lax.scan(
-        backward_step, zeros, (text_in, layout_in, lengths, kept_all, cot_text, cot_layout)
-    )
-    inputs_all = flat_rows(text_in)
-    context_all = flat_rows(kept_all[2])
-    three_all, first_all, hidden_all, inner_all, active_all, second_all = tuple(
-        (flat_rows(values) for values in text_operands)
-    )
-    grad_second = lax.psum_scatter(
-        jnp.einsum("sf,sd->fd", active_all, second_all, preferred_element_type=jnp.float32),
-        AXES,
-        scatter_dimension=0,
-        tiled=True,
-    )
-    grad_first = lax.psum_scatter(
-        jnp.einsum("sd,sf->df", hidden_all, inner_all, preferred_element_type=jnp.float32),
-        AXES,
-        scatter_dimension=0,
-        tiled=True,
-    )
-    three_part = jnp.einsum("sd,se->de", inputs_all, three_all, preferred_element_type=jnp.float32)
-    out_part = jnp.einsum("sd,se->de", context_all, first_all, preferred_element_type=jnp.float32)
-    grad_attn = lax.psum_scatter(
-        jnp.concatenate([three_part, out_part], 1), AXES, scatter_dimension=0, tiled=True
-    )
-    summed = scatter_small(count, *totals)
+    text_back, layout_back = jax.vmap(page_back_ffn, in_axes=(0, 0, 0, 0, page_weights))(
+        lengths, kept_all, cot_text, cot_layout, weights
+    )
+    text_hidden, text_active, text_first_low, text_second_low, text_inner_low = text_back[2]
+    early = (
+        jnp.einsum("sd,sf->df", flat_rows(text_hidden), flat_rows(text_inner_low), preferred_element_type=jnp.float32),
+        jnp.einsum("sf,sd->fd", flat_rows(text_active), flat_rows(text_second_low), preferred_element_type=jnp.float32),
+    )
+    early, text_back, layout_back = lax.optimization_barrier((early, text_back, layout_back))
+    grad_first, grad_second = scatter_early(count, *early)
+    (text_grad, layout_grad), small_terms, text_rounded = jax.vmap(
+        page_back_attn, in_axes=(0, 0, 0, 0, 0, 0, page_weights)
+    )(text_in, layout_in, lengths, kept_all, text_back, layout_back, weights)
+    totals = tuple(jnp.sum(term, 0) for term in small_terms)
+    three_part = jnp.einsum(
+        "sd,se->de", flat_rows(text_in), flat_rows(text_rounded), preferred_element_type=jnp.float32
+    )
+    out_part = jnp.einsum(
+        "sd,se->de", flat_rows(kept_all[2]), flat_rows(text_first_low), preferred_element_type=jnp.float32
+    )
+    summed = scatter_late(count, jnp.concatenate([three_part, out_part], 1), totals)
     return (
         out_text,
         out_layout,
         text_grad,
         layout_grad,
-        grad_attn,
+        summed[0],
         grad_first,
         grad_second,
-        summed[0],
         summed[1],
         summed[2],
         summed[3],
         summed[4],
+        summed[5],
     )
 
 

time: 934 us -> 760 us (0.81)
  waiting for transfers between devices: 546 us -> 398 us
  blocking collectives: 77.7 us -> 0 us
  local copies, waits for them, and re-layouts: 76 us -> 107 us
  other arithmetic: 35.7 us -> 61.9 us
    unnamed x8 -> x4, waiting for transfers between devices: 135 us -> 0.07 us
    all_gather x1 -> x0, blocking collectives: 77.7 us -> none  [gather_small(): gathered = lax.all_gather(packed, AXES, axis=0, tiled=True)]
    reduce_scatter x3 -> x2, waiting for transfers between devices: 364 us -> 319 us  [the longest x1 206 us: scatter_early(): lax.psum_scatter(packed.reshape(-1, width), AXES, scatter_dimension=0, ti...]
    all_gather x3 -> x2, waiting for transfers between devices: 47.2 us -> 78.2 us  [the longest x1 67.6 us: gather_weights(): first_all = lax.all_gather(first, AXES, axis=0, tiled=True)]
    concatenate x1 -> x7, other arithmetic: 1.12 us -> 29.1 us  [the longest x1 15.2 us: scatter_early(): jnp.concatenate([grad_first.reshape(count, rows, width), grad_second.resh...]
    reshape x16 -> x17, local copies, waits for them, and re-layouts: 15.8 us -> 33.2 us  [the longest x1 11.7 us: scatter_early(): grad_second.reshape(count, rows, width)]
    slice x8 -> x12, local copies, waits for them, and re-layouts: 5.16 us -> 21.8 us  [the longest x1 8.2 us: gather_weights(): full_w2 = second_all[:, rows:].reshape(count * w2_rows, text_w2.shape[1])]
    unnamed x220 -> x185, local copies, waits for them, and re-layouts: 26.3 us -> 11.5 us
  transfers between devices with their start and end apart: 7 -> 4, of which waited for: 6 -> 4; matrix products, arithmetic and copies ran while one was open for 13% -> 16% of each run, Pallas kernels for 0% -> 0%
where the time goes in v2:
time: 760 us; the launch traced here: 755 us
  waiting for transfers between devices  398 us (52%)
  matrix products  173 us (23%)
  local copies, waits for them, and re-layouts  107 us (14%)
  other arithmetic  61.9 us (8%)
  between operations  15.8 us (2%)
    reduce_scatter x1, waiting for transfers between devices, scatter_early(): lax.psum_scatter(packed.reshape(-1, width), AXES, scatter_dimension=0, ti...  206 us
    reduce_scatter x1, waiting for transfers between devices, scatter_late(): lax.psum_scatter(packed.reshape(-1, width), AXES, scatter_dimension=0, ti...  114 us
    all_gather x1, waiting for transfers between devices, gather_weights(): first_all = lax.all_gather(first, AXES, axis=0, tiled=True)  67.6 us
    dot_general x1, matrix products, attend_back(): jnp.einsum('hqk,khd->qhd', joint_ds, split_heads(layout_three[:, 1]), pre...  25.3 us
    dot_general x2, matrix products, branch_forward(): jnp.dot(hidden.astype(jnp.bfloat16), first, preferred_element_type=jnp.fl...  23.9 us
    dot_general x1, matrix products, attend_back(): jnp.einsum('hqk,qhd->khd', joint_ds, split_heads(layout_three[:, 0]), pre...  22 us
  transfers between devices with their start and end apart: 4, of which 4 were waited for; matrix products, arithmetic and copies ran while one was open for 16% of the time, Pallas kernels for 0%

profile of v2, /device:TPU:0, one launch (start us, length us, event | category | flops | bytes accessed | tf_op | source)
XLA Modules:
  0.0 755.4 jit_solution(2465716946081988932)
XLA Ops:
  9.8 1.4 concatenate.58
  11.3 1.6 pad_maximum_fusion.9
  14.0 1.6 pad_maximum_fusion.6
  17.4 67.6 %all-gather.3.cloned.1.call-done = bf16[1024,3072]{1,0:T(8,128)(2,1)} async-done(((bf16[32,3072]{1,0:T(8,128)(2,1)}), bf16[1024,3072]{1,0:T(8,128)(2,1)}) %all-gather.3.cloned.1.call-update) | async-done | bytes 6291472 | tf_op jit(solution)/shard_map/all_gather | solution.py:369
  85.1 1.5 slice.230
  86.6 4.8 slice.228
  95.9 2.3 slice.229
  98.2 3.9 copy.45
  103.0 1.9 reshape.1065
  105.9 1.3 fusion.130
  107.3 2.5 reshape.1076
  111.0 1.3 fusion.53
  112.5 4.6 fusion.14
  117.3 6.4 fusion.143
  123.8 6.6 fusion.137
  130.4 1.9 fusion.2
  132.3 2.7 copy-done
  135.0 2.5 divide_convert_fusion
  139.1 4.1 multiply_convert_fusion.3
  153.5 2.2 fusion.138
  156.7 1.2 fusion.52
  157.9 10.6 %all-gather.5.cloned.1.call-done = bf16[1536,3072]{1,0:T(8,128)(2,1)} async-done(((bf16[48,3072]{1,0:T(8,128)(2,1)}), bf16[1536,3072]{1,0:T(8,128)(2,1)}) %all-gather.5.cloned.1.call-update) | async-done | bytes 9437200 | tf_op jit(solution)/shard_map/all_gather | solution.py:378
  168.5 8.2 %fusion.127 = (bf16[32,24,3072]{2,1,0:T(8,128)(2,1)}, bf16[32,24,3072]{2,1,0:T(8,128)(2,1)}) fusion(bf16[32,48,3072]{2,1,0:T(8,128)(2,1)} %bitcast.282), kind=kLoop, calls=%fused_computation.224 | loop fusion | bytes 18874368 | tf_op jit(solution)/shard_map/slice | solution.py:380
  176.7 8.5 %reshape.1073 = bf16[3072,768]{1,0:T(8,128)(2,1)} reshape(bf16[32,24,3072]{2,1,0:T(8,128)(2,1)} %get-tuple-element.103) | data formatting | bytes 9437184 | tf_op jit(solution)/shard_map/reshape | solution.py:380
  185.2 19.8 %multiply_convert_fusion = (bf16[512,3072]{1,0:T(8,128)(2,1)S(1)}, f32[512,3072]{1,0:T(8,128)}, f32[512,3072]{1,0:T(8,128)}) fusion(f32[3072]{0:T(1024)} %slice.248, bf16[768,3072]{1,0:T(8,128)(2,1)} %bitcast.297, bf16[1,512,768]{2,1,0:T(8,128)(2,1)} %fusion.52), kind=kOutput, calls=%fused_computation.20 | convolution fusion | flops 2519728128 | bytes 21245952 | tf_op jit(solution)/shard_map/vmap()/dot_general | solution.py:165
  205.0 2.8 fusion.139
  209.0 1.7 fusion.124
  211.0 5.1 fusion.83
  216.1 8.5 %fusion.142 = (f32[3072]{0:T(1024)}, bf16[512,3072]{1,0:T(8,128)(2,1)S(1)}) fusion(f32[512,3072]{1,0:T(8,128)} %get-tuple-element.102, bf16[3072,768]{1,0:T(8,128)(2,1)S(1)} %copy-done.14, bf16[1,512,768]{2,1,0:T(8,128)(2,1)S(1)} %get-tuple-element.110, f32[512,3072]{1,0:T(8,128)} %get-tuple-element.149, f32[3072]{0:T(1024)S(1)} %copy-done.69), kind=kOutput, calls=%fused_computation.239 | convolution fusion | flops 2441081856 | bytes 21258240 | tf_op jit(solution)/shard_map/vmap()/dot_general | solution.py:183
  224.6 3.1 multiply_reduce_fusion.3
  227.8 5.2 fusion.34
  233.9 3.4 fusion.51
  237.4 2.3 fusion.80
  243.1 1.4 copy.50
  244.5 10.5 %multiply_reduce_fusion.1 = (f32[12,512]{1,0:T(8,128)S(1)}, f32[12,512,512]{1,2,0:T(8,128)}) fusion(f32[12,512,512]{1,2,0:T(8,128)} %copy-done, f32[12,512]{1,0:T(8,128)S(1)} %copy-done.31, bf16[512,12,64]{0,2,1:T(8,128)(2,1)S(1)} %bitcast.283, bf16[512,12,64]{0,2,1:T(8,128)(2,1)S(1)} %bitcast.276), kind=kOutput, calls=%fused_computation.7 | convolution fusion | flops 412084224 | bytes 26787840 | tf_op jit(solution)/shard_map/vmap(qhd,khd->hqk)/dot_general | solution.py:97
  255.8 1.4 slice-done.2
  257.2 7.1 fusion.3
  265.5 2.0 multiply_convert_fusion.1
  267.5 2.0 fusion.47
  269.6 6.3 fusion.144
  275.9 25.3 %fusion.69 = bf16[12,16,512]{2,1,0:T(8,128)(2,1)} fusion(bf16[512,12,16]{0,2,1:T(8,128)(2,1)S(1)} %bitcast.322, f32[12,512,512]{1,2,0:T(8,128)} %fusion.144, f32[12,512,512]{1,2,0:T(8,128)} %get-tuple-element.162, f32[12,512,512]{1,2,0:T(8,128)} %copy-done, f32[12,512]{1,0:T(8,128)S(1)} %copy-done.52, f32[12,512]{1,0:T(8,128)S(1)} %copy-done.33), kind=kOutput, calls=%fused_computation.115 | convolution fusion | flops 129178112 | bytes 38191104 | tf_op jit(solution)/shard_map/vmap(hqk,khd->qhd)/dot_general | solution.py:123
  301.2 22.0 %fusion.66 = bf16[12,16,512]{2,1,0:T(8,128)(2,1)} fusion(bf16[512,12,16]{0,2,1:T(8,128)(2,1)S(1)} %bitcast.320, f32[12,512,512]{1,2,0:T(8,128)} %fusion.144, f32[12,512,512]{1,2,0:T(8,128)} %get-tuple-element.162, f32[12,512,512]{1,2,0:T(8,128)} %copy-done, f32[12,512]{1,0:T(8,128)S(1)} %copy-done.52, f32[12,512]{1,0:T(8,128)S(1)} %copy-done.33), kind=kOutput, calls=%fused_computation.114 | convolution fusion | flops 129178112 | bytes 38191104 | tf_op jit(solution)/shard_map/vmap(hqk,qhd->khd)/dot_general | solution.py:129
  323.2 6.3 fusion.72
  330.7 5.0 convolution_bitcast_fusion
  335.7 7.2 pad_maximum_fusion.2
  343.0 9.7 %copy.61 = f32[768,3072]{1,0:T(8,128)} copy(f32[768,3072]{0,1:T(8,128)} %pad_maximum_fusion.2) | data formatting | bytes 18874368 | tf_op jit(solution)/shard_map/concatenate | solution.py:479
  355.0 1.3 convolution_bitcast_fusion.1
  356.4 2.1 copy.65
  358.5 3.0 reshape.1092
  361.8 1.7 fusion.99
  366.1 2.4 concatenate.65
  368.8 1.8 copy.80
  370.6 9.9 %pad_maximum_fusion.1 = f32[32,32,3072]{2,1,0:T(8,128)} fusion(f32[32,8,3072]{2,1,0:T(8,128)S(1)} %bitcast.273, f32[32,24,3072]{2,1,0:T(8,128)} %bitcast.268), kind=kLoop, calls=%fused_computation.2 | loop fusion | flops 3145728 | bytes 25165824 | tf_op jit(solution)/shard_map/concatenate | solution.py:405
  380.5 11.7 %reshape.1100 = f32[32,24,3072]{2,1,0:T(8,128)} reshape(f32[3072,768]{1,0:T(8,128)} %fusion.83) | data formatting | bytes 18874368 | tf_op jit(solution)/shard_map/reshape | solution.py:428
  392.2 15.2 %pad_maximum_fusion = f32[32,48,3072]{2,1,0:T(8,128)} fusion(f32[32,24,3072]{2,1,0:T(8,128)} %reshape.1100, f32[32,24,3072]{2,1,0:T(8,128)} %bitcast.269), kind=kLoop, calls=%fused_computation.1 | loop fusion | flops 4718592 | bytes 37748736 | tf_op jit(solution)/shard_map/concatenate | solution.py:427
  408.5 1.2 copy.54
  409.7 1.2 copy.55
  410.9 1.2 copy.56
  412.0 2.4 fusion.56
  414.4 5.9 bitcast_add_fusion
  420.4 113.7 %reduce-scatter.3.cloned.1.call-done = f32[32,3072]{1,0:T(8,128)} async-done(((f32[1024,3072]{1,0:T(8,128)}), f32[32,3072]{1,0:T(8,128)}) %reduce-scatter.3.cloned.1.call-update) | async-done | bytes 393232 | tf_op jit(solution)/shard_map/reduce_scatter | solution.py:406
  538.7 1.7 slice.268
  540.4 205.7 %reduce-scatter.5.cloned.1.call-done = f32[48,3072]{1,0:T(8,128)} async-done(((f32[1536,3072]{1,0:T(8,128)}), f32[48,3072]{1,0:T(8,128)}) %reduce-scatter.5.cloned.1.call-update) | async-done | bytes 589840 | tf_op jit(solution)/shard_map/reduce_scatter | solution.py:430
  746.1 1.8 fusion.131
  (294 shorter events, 46.0 us)
Async XLA Ops:
  7.2 77.9 %all-gather.3.cloned.1.call-start = ((), (), s32[]{:S(2)}) async-start(), calls=%async_computation.2 | async-start | bytes 6488064 | tf_op jit(solution)/shard_map/all_gather | solution.py:369
  12.9 155.6 %all-gather.5.cloned.1.call-start = ((), (), s32[]{:S(2)}) async-start(), calls=%async_computation.3 | async-start | bytes 9732096 | tf_op jit(solution)/shard_map/all_gather | solution.py:378
  15.6 518.4 %reduce-scatter.3.cloned.1.call-start = ((), (), s32[]{:S(2)}) async-start(), calls=%async_computation.4 | async-start | bytes 12976128 | tf_op jit(solution)/shard_map/reduce_scatter | solution.py:406
  102.0 8.9 %copy-start.80 = (f32[3]{0:T(128)S(1)}, f32[3]{0:T(128)}, u32[]{:S(2)}) copy-start(f32[3]{0:T(128)} %pad.36.clone) | copy-start | bytes 40
  102.0 9.0 %copy-start.47 = (bf16[1,512,192]{1,2,0:T(8,128)(2,1)S(1)}, bf16[1,512,192]{1,2,0:T(8,128)(2,1)}, u32[]{:S(2)}) copy-start(bf16[1,512,192]{1,2,0:T(8,128)(2,1)} %param.14) | copy-start | bytes 589828
  104.9 7.5 copy-start.62
  105.9 32.6 %copy-start.29 = (bf16[192,192]{1,0:T(8,128)(2,1)}, bf16[192,192]{1,0:T(8,128)(2,1)S(1)}, u32[]{:S(2)}) copy-start(bf16[192,192]{1,0:T(8,128)(2,1)S(1)} %slice.204) | copy-start | bytes 221188
  112.5 11.3 %copy-start.34 = (bf16[1,512,1,192]{1,3,2,0:T(8,128)(2,1)}, bf16[1,512,1,192]{1,3,2,0:T(8,128)(2,1)S(1)}, u32[]{:S(2)}) copy-start(bf16[1,512,1,192]{1,3,2,0:T(8,128)(2,1)S(1)} %get-tuple-element.119) | copy-start | bytes 589828
  112.5 11.3 %copy-start.36 = (bf16[1,512,1,192]{1,3,2,0:T(8,128)(2,1)}, bf16[1,512,1,192]{1,3,2,0:T(8,128)(2,1)S(1)}, u32[]{:S(2)}) copy-start(bf16[1,512,1,192]{1,3,2,0:T(8,128)(2,1)S(1)} %get-tuple-element.118) | copy-start | bytes 589828
  117.3 6.5 copy-start.1
  117.3 6.5 copy-start.8
  117.3 6.5 copy-start.79
  130.4 4.6 copy-start
  138.5 4.7 copy-start.21
  139.1 4.2 copy-start.40
  139.1 4.7 copy-start.39
  147.8 4.3 copy-start.30
  153.5 3.2 copy-start.58
  185.2 19.8 %copy-start.14 = (bf16[3072,768]{1,0:T(8,128)(2,1)S(1)}, bf16[3072,768]{1,0:T(8,128)(2,1)}, u32[]{:S(2)}) copy-start(bf16[3072,768]{1,0:T(8,128)(2,1)} %reshape.1073) | copy-start | bytes 14155780
  185.2 19.8 %copy-start.55 = (f32[512]{0:T(512)S(1)}, f32[512]{0:T(512)}, u32[]{:S(2)}) copy-start(f32[512]{0:T(512)} %copy-done.54) | copy-start | bytes 6148
  185.2 19.8 %copy-start.59 = (f32[768]{0:T(1024)S(1)}, f32[768]{0:T(1024)}, u32[]{:S(2)}) copy-start(f32[768]{0:T(1024)} %get-tuple-element.130) | copy-start | bytes 9220
  185.2 19.8 %copy-start.77 = (f32[768]{0:T(1024)S(1)}, f32[768]{0:T(1024)}, u32[]{:S(2)}) copy-start(f32[768]{0:T(1024)} %get-tuple-element.129) | copy-start | bytes 9220
  210.9 5.2 copy-start.69
  210.9 13.6 %slice-start.3 = ((s8[4718592]{0:T(1024)(128)(4,1)}), s8[4194304]{0:T(1024)(128)(4,1)S(1)}, s32[]{:S(2)}) async-start(s8[4718592]{0:T(1024)(128)(4,1)} %bitcast.298), calls=%async_computation.9 | async-start | bytes 8388608
  216.1 8.5 %slice-start.4 = ((s8[4718592]{0:T(1024)(128)(4,1)}), s8[524288]{0:T(1024)(128)(4,1)S(1)}, s32[]{:S(2)}) async-start(s8[4718592]{0:T(1024)(128)(4,1)} %bitcast.298), calls=%async_computation.10 | async-start | bytes 1048576
  227.8 5.2 copy-start.57
  233.8 5.8 copy-start.12
  237.3 7.2 copy-start.31
  244.5 11.1 %slice-start = ((s8[12582912]{0:T(1024)(128)(4,1)}), s8[4194304]{0:T(1024)(128)(4,1)S(1)}, s32[]{:S(2)}) async-start(s8[12582912]{0:T(1024)(128)(4,1)} %bitcast.264), calls=%async_computation.6 | async-start | bytes 8388608
  244.5 11.2 %slice-start.1 = ((s8[12582912]{0:T(1024)(128)(4,1)}), s8[4194304]{0:T(1024)(128)(4,1)S(1)}, s32[]{:S(2)}) async-start(s8[12582912]{0:T(1024)(128)(4,1)} %bitcast.264), calls=%async_computation.7 | async-start | bytes 8388608
  244.5 12.6 %slice-start.2 = ((s8[12582912]{0:T(1024)(128)(4,1)}), s8[4194304]{0:T(1024)(128)(4,1)S(1)}, s32[]{:S(2)}) async-start(s8[12582912]{0:T(1024)(128)(4,1)} %bitcast.264), calls=%async_computation.8 | async-start | bytes 8388608
  257.2 7.1 copy-start.2
  265.5 64.1 %copy-start.3 = (bf16[12,64,512]{2,1,0:T(8,128)(2,1)}, bf16[12,64,512]{2,1,0:T(8,128)(2,1)S(1)}, u32[]{:S(2)}) copy-start(bf16[12,64,512]{2,1,0:T(8,128)(2,1)S(1)} %multiply_convert_fusion.2) | copy-start | bytes 2359300
  267.5 62.1 %copy-start.10 = (bf16[12,64,512]{2,1,0:T(8,128)(2,1)}, bf16[12,64,512]{2,1,0:T(8,128)(2,1)S(1)}, u32[]{:S(2)}) copy-start(bf16[12,64,512]{2,1,0:T(8,128)(2,1)S(1)} %multiply_convert_fusion.1) | copy-start | bytes 2359300
  269.5 60.0 %copy-start.6 = (bf16[12,64,512]{2,1,0:T(8,128)(2,1)}, bf16[12,64,512]{2,1,0:T(8,128)(2,1)S(1)}, u32[]{:S(2)}) copy-start(bf16[12,64,512]{2,1,0:T(8,128)(2,1)S(1)} %fusion.47) | copy-start | bytes 2359300
  269.5 6.3 copy-start.33
  269.6 6.3 copy-start.37
  269.6 6.3 copy-start.52
  275.9 25.3 %copy-start.35 = (bf16[1,512,1,192]{1,3,2,0:T(8,128)(2,1)S(1)}, bf16[1,512,1,192]{1,3,2,0:T(8,128)(2,1)}, u32[]{:S(2)}) copy-start(bf16[1,512,1,192]{1,3,2,0:T(8,128)(2,1)} %copy-done.34) | copy-start | bytes 589828
  329.5 23.2 %copy-start.44 = (bf16[12,16,512]{2,1,0:T(8,128)(2,1)}, bf16[12,16,512]{2,1,0:T(8,128)(2,1)S(1)}, u32[]{:S(2)}) copy-start(bf16[12,16,512]{2,1,0:T(8,128)(2,1)S(1)} %fusion.72) | copy-start | bytes 589828
  330.7 5.0 copy-start.5
  342.9 9.8 %copy-start.49 = (bf16[12,16,512]{2,1,0:T(8,128)(2,1)S(1)}, bf16[12,16,512]{2,1,0:T(8,128)(2,1)}, u32[]{:S(2)}) copy-start(bf16[12,16,512]{2,1,0:T(8,128)(2,1)} %fusion.69) | copy-start | bytes 589828
  342.9 9.8 %copy-start.50 = (bf16[12,16,512]{2,1,0:T(8,128)(2,1)S(1)}, bf16[12,16,512]{2,1,0:T(8,128)(2,1)}, u32[]{:S(2)}) copy-start(bf16[12,16,512]{2,1,0:T(8,128)(2,1)} %fusion.66) | copy-start | bytes 589828
  342.9 10.0 %copy-start.61 = (f32[1,768]{1,0:T(1,128)S(1)}, f32[1,768]{1,0:T(1,128)}, u32[]{:S(2)}) copy-start(f32[1,768]{1,0:T(1,128)} %reduce_sum.440) | copy-start | bytes 9220
  342.9 10.0 %copy-start.71 = (f32[192]{0:T(256)S(1)}, f32[192]{0:T(256)}, u32[]{:S(2)}) copy-start(f32[192]{0:T(256)} %get-tuple-element.82) | copy-start | bytes 2308
  342.9 10.0 %copy-start.72 = (f32[192]{0:T(256)S(1)}, f32[192]{0:T(256)}, u32[]{:S(2)}) copy-start(f32[192]{0:T(256)} %get-tuple-element.86) | copy-start | bytes 2308
  342.9 10.0 %copy-start.73 = (f32[192]{0:T(256)S(1)}, f32[192]{0:T(256)}, u32[]{:S(2)}) copy-start(f32[192]{0:T(256)} %get-tuple-element.121) | copy-start | bytes 2308
  342.9 10.0 %copy-start.74 = (f32[192]{0:T(256)S(1)}, f32[192]{0:T(256)}, u32[]{:S(2)}) copy-start(f32[192]{0:T(256)} %get-tuple-element.84) | copy-start | bytes 2308
  343.0 10.0 %copy-start.75 = (f32[192]{0:T(256)S(1)}, f32[192]{0:T(256)}, u32[]{:S(2)}) copy-start(f32[192]{0:T(256)} %get-tuple-element.79) | copy-start | bytes 2308
  343.0 10.0 %copy-start.76 = (f32[192]{0:T(256)S(1)}, f32[192]{0:T(256)}, u32[]{:S(2)}) copy-start(f32[192]{0:T(256)} %get-tuple-element.89) | copy-start | bytes 2308
  343.0 10.3 %copy-start.17 = (bf16[512,768]{1,0:T(8,128)(2,1)S(1)}, bf16[512,768]{1,0:T(8,128)(2,1)}, u32[]{:S(2)}) copy-start(bf16[512,768]{1,0:T(8,128)(2,1)} %copy-done.16) | copy-start | bytes 2359300
  343.0 10.3 %copy-start.43 = (bf16[1,512,192]{1,2,0:T(8,128)(2,1)S(1)}, bf16[1,512,192]{1,2,0:T(8,128)(2,1)}, u32[]{:S(2)}) copy-start(bf16[1,512,192]{1,2,0:T(8,128)(2,1)} %copy-done.42) | copy-start | bytes 589828
  356.4 5.1 copy-start.22
  356.4 5.1 copy-start.26
  361.5 3.2 copy-start.63
  361.5 3.2 copy-start.64
  361.6 3.2 copy-start.70
  361.6 4.6 copy-start.23
  361.6 4.6 copy-start.24
  380.5 365.6 %reduce-scatter.5.cloned.1.call-start = ((), (), s32[]{:S(2)}) async-start(), calls=%async_computation.5 | async-start | bytes 19464192 | tf_op jit(solution)/shard_map/reduce_scatter | solution.py:430
  407.4 3.5 copy-start.7
  407.4 4.6 copy-start.28
  409.7 4.7 copy-start.38
  410.9 3.6 copy-start.13
  (26 other events, 49.8 us)
Sparse Core Ops, SparseCore 0:
  13.0 71.9 all-gather.2
  88.5 79.9 all-gather.4
  380.6 153.4 reduce-scatter.2
  540.3 205.6 reduce-scatter.4

commit v3 on v2

--- a/solution.py
+++ b/solution.py
@@ -403,7 +403,9 @@
     small_rows = rows_for(size, width, rows % 8 == 0)
     joined = jnp.pad(joined, ((0, 0), (0, small_rows * width - size))).reshape(count, small_rows, width)
     packed = jnp.concatenate([grad_attn.reshape(count, rows, width), joined], 1)
-    summed = lax.psum_scatter(packed.reshape(-1, width), AXES, scatter_dimension=0, tiled=True)
+    summed = lax.psum_scatter(
+        packed.reshape(-1, width).astype(jnp.bfloat16), AXES, scatter_dimension=0, tiled=True
+    ).astype(jnp.float32)
     attn_part = summed[:rows]
     flat = summed[rows:].reshape(-1)
     sizes = [block.shape[1] for block in blocks]
@@ -427,7 +429,9 @@
     packed = jnp.concatenate(
         [grad_first.reshape(count, rows, width), grad_second.reshape(count, rows, width)], 1
     )
-    summed = lax.psum_scatter(packed.reshape(-1, width), AXES, scatter_dimension=0, tiled=True)
+    summed = lax.psum_scatter(
+        packed.reshape(-1, width).astype(jnp.bfloat16), AXES, scatter_dimension=0, tiled=True
+    ).astype(jnp.float32)
     return (summed[:rows], summed[rows:].reshape(-1, grad_second.shape[1]))
 
 

time: 760 us -> 638 us (0.84)
  waiting for transfers between devices: 398 us -> 297 us
  local copies, waits for them, and re-layouts: 107 us -> 96.1 us
  other arithmetic: 61.9 us -> 53.4 us
    reduce_scatter x2, waiting for transfers between devices: 319 us -> 218 us  [the longest x1 134 us: scatter_early(): lax.psum_scatter(packed.reshape(-1, width).astype(jnp.bfloat16), AXES, sc...]
  transfers between devices with their start and end apart: 4 -> 4, of which waited for: 4 -> 4; matrix products, arithmetic and copies ran while one was open for 16% -> 17% of each run, Pallas kernels for 0% -> 0%
where the time goes in v3:
time: 638 us; the launch traced here: 632 us
  waiting for transfers between devices  297 us (47%)
  matrix products  169 us (26%)
  local copies, waits for them, and re-layouts  96.1 us (15%)
  other arithmetic  53.4 us (8%)
  between operations  15.8 us (2%)
    reduce_scatter x1, waiting for transfers between devices, scatter_early(): lax.psum_scatter(packed.reshape(-1, width).astype(jnp.bfloat16), AXES, sc...  134 us
    reduce_scatter x1, waiting for transfers between devices, scatter_late(): lax.psum_scatter(packed.reshape(-1, width).astype(jnp.bfloat16), AXES, sc...  84.6 us
    all_gather x1, waiting for transfers between devices, gather_weights(): first_all = lax.all_gather(first, AXES, axis=0, tiled=True)  67.5 us
    dot_general x1, matrix products, attend_back(): jnp.einsum('hqk,khd->qhd', joint_ds, split_heads(layout_three[:, 1]), pre...  25.2 us
    dot_general x2, matrix products, branch_forward(): jnp.dot(hidden.astype(jnp.bfloat16), first, preferred_element_type=jnp.fl...  23.4 us
    dot_general x1, matrix products, attend_back(): jnp.einsum('hqk,qhd->khd', joint_ds, split_heads(layout_three[:, 0]), pre...  22.3 us
  transfers between devices with their start and end apart: 4, of which 4 were waited for; matrix products, arithmetic and copies ran while one was open for 17% of the time, Pallas kernels for 0%

profile of v3, /device:TPU:0, one launch (start us, length us, event | category | flops | bytes accessed | tf_op | source)
XLA Modules:
  0.0 631.9 jit_solution(12555686284873470418)
XLA Ops:
  9.8 1.5 concatenate.65
  11.3 1.6 pad_maximum_fusion.9
  14.0 1.6 pad_maximum_fusion.6
  17.5 67.5 %all-gather.3.cloned.1.call-done = bf16[1024,3072]{1,0:T(8,128)(2,1)} async-done(((bf16[32,3072]{1,0:T(8,128)(2,1)}), bf16[1024,3072]{1,0:T(8,128)(2,1)}) %all-gather.3.cloned.1.call-update) | async-done | bytes 6291472 | tf_op jit(solution)/shard_map/all_gather | solution.py:369
  85.1 1.5 slice.234
  86.6 4.8 slice.232
  98.8 2.5 reshape.1086
  101.3 2.0 copy.49
  103.3 2.2 slice.233
  105.5 3.6 copy.45
  109.9 1.4 fusion.54
  112.1 4.6 fusion.15
  116.9 6.4 %fusion.143 = f32[12,512,512]{1,2,0:T(8,128)} fusion(bf16[512,12,64]{0,2,1:T(8,128)(2,1)S(1)} %bitcast.282, bf16[512,12,64]{0,2,1:T(8,128)(2,1)S(1)} %bitcast.273), kind=kOutput, calls=%fused_computation.242 | convolution fusion | flops 402653184 | bytes 14155776 | tf_op jit(solution)/shard_map/vmap(qhd,khd->hqk)/dot_general | solution.py:54
  123.4 6.6 %fusion.137 = (f32[12,512]{1,0:T(8,128)S(1)}, f32[12,512,512]{1,2,0:T(8,128)S(1)}) fusion(bf16[512,12,16]{0,2,1:T(8,128)(2,1)S(1)} %bitcast.317, bf16[512,12,16]{0,2,1:T(8,128)(2,1)S(1)} %bitcast.319, f32[12,512,512]{1,2,0:T(8,128)} %fusion.143, pred[512]{0:T(512)(128)(4,1)S(1)} %copy-done.56), kind=kOutput, calls=%fused_computation.236 | convolution fusion | flops 116385792 | bytes 25584128 | tf_op jit(solution)/shard_map/vmap(qhd,khd->hqk)/dot_general | solution.py:60
  130.0 1.9 fusion.2
  131.9 2.7 copy-done
  134.5 2.3 divide_convert_fusion
  138.4 4.3 multiply_convert_fusion.3
  153.0 2.2 fusion.138
  157.3 11.2 %all-gather.5.cloned.1.call-done = bf16[1536,3072]{1,0:T(8,128)(2,1)} async-done(((bf16[48,3072]{1,0:T(8,128)(2,1)}), bf16[1536,3072]{1,0:T(8,128)(2,1)}) %all-gather.5.cloned.1.call-update) | async-done | bytes 9437200 | tf_op jit(solution)/shard_map/all_gather | solution.py:378
  168.5 8.2 %fusion.128 = (bf16[32,24,3072]{2,1,0:T(8,128)(2,1)}, bf16[32,24,3072]{2,1,0:T(8,128)(2,1)}) fusion(bf16[32,48,3072]{2,1,0:T(8,128)(2,1)} %bitcast.277), kind=kLoop, calls=%fused_computation.227 | loop fusion | bytes 18874368 | tf_op jit(solution)/shard_map/slice | solution.py:380
  176.7 8.5 %reshape.1083 = bf16[3072,768]{1,0:T(8,128)(2,1)} reshape(bf16[32,24,3072]{2,1,0:T(8,128)(2,1)} %get-tuple-element.103) | data formatting | bytes 9437184 | tf_op jit(solution)/shard_map/reshape | solution.py:380
  185.2 19.1 %multiply_convert_fusion = (bf16[512,3072]{1,0:T(8,128)(2,1)S(1)}, f32[512,3072]{1,0:T(8,128)}, f32[512,3072]{1,0:T(8,128)}) fusion(f32[3072]{0:T(1024)} %slice.252, bf16[768,3072]{1,0:T(8,128)(2,1)} %bitcast.293, bf16[1,512,768]{2,1,0:T(8,128)(2,1)} %fusion.53), kind=kOutput, calls=%fused_computation.19 | convolution fusion | flops 2519728128 | bytes 21245952 | tf_op jit(solution)/shard_map/vmap()/dot_general | solution.py:165
  204.4 2.8 fusion.139
  208.4 1.7 fusion.125
  210.4 8.3 %fusion.142 = (f32[3072]{0:T(1024)}, bf16[512,3072]{1,0:T(8,128)(2,1)S(1)}) fusion(f32[512,3072]{1,0:T(8,128)} %get-tuple-element.102, bf16[3072,768]{1,0:T(8,128)(2,1)S(1)} %copy-done.8, bf16[1,512,768]{2,1,0:T(8,128)(2,1)S(1)} %get-tuple-element.110, f32[512,3072]{1,0:T(8,128)} %get-tuple-element.147, f32[3072]{0:T(1024)S(1)} %copy-done.43), kind=kOutput, calls=%fused_computation.241 | convolution fusion | flops 2441081856 | bytes 21258240 | tf_op jit(solution)/shard_map/vmap()/dot_general | solution.py:183
  218.7 3.1 multiply_reduce_fusion.3
  224.0 2.2 fusion.52
  226.2 1.9 convolution_convert_fusion.1
  228.1 4.7 fusion.84
  232.8 4.4 fusion.35
  238.7 6.8 %fusion.48 = bf16[12,64,512]{2,1,0:T(8,128)(2,1)S(1)} fusion(bf16[512,12,64]{0,2,1:T(8,128)(2,1)S(1)} %bitcast.278, f32[12,512,512]{1,2,0:T(8,128)} %copy-done, f32[12,512]{1,0:T(8,128)S(1)} %copy-done.21), kind=kOutput, calls=%fused_computation.93 | convolution fusion | flops 409337856 | bytes 14180352 | tf_op jit(solution)/shard_map/vmap(hqk,qhd->khd)/dot_general | solution.py:109
  245.5 8.9 %multiply_reduce_fusion.1 = (f32[12,512]{1,0:T(8,128)S(1)}, f32[12,512,512]{1,2,0:T(8,128)}) fusion(f32[12,512,512]{1,2,0:T(8,128)} %copy-done, f32[12,512]{1,0:T(8,128)S(1)} %copy-done.21, bf16[512,12,64]{0,2,1:T(8,128)(2,1)S(1)} %bitcast.279, bf16[512,12,64]{0,2,1:T(8,128)(2,1)S(1)} %bitcast.272), kind=kOutput, calls=%fused_computation.5 | convolution fusion | flops 412084224 | bytes 26787840 | tf_op jit(solution)/shard_map/vmap(qhd,khd->hqk)/dot_general | solution.py:97
  254.4 7.1 %fusion.3 = bf16[12,512,512]{1,2,0:T(8,128)(2,1)S(1)} fusion(f32[12,512,512]{1,2,0:T(8,128)} %get-tuple-element.160, f32[12,512,512]{1,2,0:T(8,128)S(1)} %bitcast.264, f32[12,512]{1,0:T(8,128)S(1)} %get-tuple-element.159, f32[12,512]{1,0:T(8,128)S(1)} %copy-done.21), kind=kLoop, calls=%fused_computation.11 | loop fusion | flops 12582912 | bytes 31506432 | tf_op jit(solution)/shard_map/vmap()/convert_element_type | solution.py:115
  261.5 2.0 multiply_convert_fusion.1
  264.6 2.4 fusion.74
  267.1 6.4 %fusion.144 = f32[12,512,512]{1,2,0:T(8,128)} fusion(bf16[512,12,16]{0,2,1:T(8,128)(2,1)S(1)} %bitcast.314, bf16[512,12,16]{0,2,1:T(8,128)(2,1)S(1)} %bitcast.309), kind=kOutput, calls=%fused_computation.243 | convolution fusion | flops 100663296 | bytes 12976128 | tf_op jit(solution)/shard_map/vmap(qhd,khd->hqk)/dot_general | solution.py:103
  273.5 25.2 %fusion.71 = bf16[12,16,512]{2,1,0:T(8,128)(2,1)} fusion(bf16[512,12,16]{0,2,1:T(8,128)(2,1)S(1)} %bitcast.320, f32[12,512,512]{1,2,0:T(8,128)} %fusion.144, f32[12,512,512]{1,2,0:T(8,128)} %get-tuple-element.160, f32[12,512,512]{1,2,0:T(8,128)} %copy-done, f32[12,512]{1,0:T(8,128)S(1)} %get-tuple-element.159, f32[12,512]{1,0:T(8,128)S(1)} %copy-done.21), kind=kOutput, calls=%fused_computation.118 | convolution fusion | flops 129178112 | bytes 38191104 | tf_op jit(solution)/shard_map/vmap(hqk,khd->qhd)/dot_general | solution.py:123
  298.7 22.3 %fusion.68 = bf16[12,16,512]{2,1,0:T(8,128)(2,1)} fusion(bf16[512,12,16]{0,2,1:T(8,128)(2,1)} %bitcast.318, f32[12,512,512]{1,2,0:T(8,128)} %fusion.144, f32[12,512,512]{1,2,0:T(8,128)} %get-tuple-element.160, f32[12,512,512]{1,2,0:T(8,128)} %copy-done, f32[12,512]{1,0:T(8,128)} %copy-done.34, f32[12,512]{1,0:T(8,128)} %log_add_fusion), kind=kOutput, calls=%fused_computation.117 | convolution fusion | flops 129178112 | bytes 38191104 | tf_op jit(solution)/shard_map/vmap(hqk,qhd->khd)/dot_general | solution.py:129
  322.8 1.2 convert.163
  324.0 1.2 convert.164
  325.3 1.2 convert.165
  327.6 1.2 convert.167
  328.8 1.3 convert.168
  330.1 1.2 convolution_convert_fusion.6
  332.5 1.4 copy.63
  334.0 2.1 fusion.57
  336.0 2.5 copy.65
  338.6 4.3 reshape.1102
  342.8 1.7 fusion.120
  345.5 3.8 fusion.14
  349.3 2.5 pad_maximum_fusion.2
  351.9 6.8 %copy.61 = bf16[768,3072]{1,0:T(8,128)(2,1)} copy(bf16[768,3072]{0,1:T(8,128)(2,1)} %pad_maximum_fusion.2) | data formatting | bytes 9437184 | tf_op jit(solution)/shard_map/concatenate | solution.py:483
  360.6 1.8 concatenate.72
  363.5 1.3 copy-done.1
  364.8 3.1 pad_maximum_fusion.1
  368.0 8.8 %reshape.1109 = bf16[32,24,3072]{2,1,0:T(8,128)(2,1)} reshape(bf16[3072,768]{1,0:T(8,128)(2,1)} %fusion.84) | data formatting | bytes 9437184 | tf_op jit(solution)/shard_map/reshape | solution.py:430
  376.8 9.4 %pad_maximum_fusion = bf16[32,48,3072]{2,1,0:T(8,128)(2,1)} fusion(bf16[32,24,3072]{2,1,0:T(8,128)(2,1)} %reshape.1109, bf16[32,24,3072]{2,1,0:T(8,128)(2,1)} %bitcast.292), kind=kLoop, calls=%fused_computation.13 | loop fusion | flops 18874368 | bytes 18874368 | tf_op jit(solution)/shard_map/concatenate | solution.py:429
  388.9 2.4 fusion.58
  391.2 5.8 bitcast_add_fusion
  397.0 84.6 %reduce-scatter.3.cloned.1.call-done = bf16[32,3072]{1,0:T(8,128)(2,1)} async-done(((bf16[1024,3072]{1,0:T(8,128)(2,1)}), bf16[32,3072]{1,0:T(8,128)(2,1)}) %reduce-scatter.3.cloned.1.call-update) | async-done | bytes 196624 | tf_op jit(solution)/shard_map/reduce_scatter | solution.py:406
  487.1 1.6 slice.272
  488.8 133.8 %reduce-scatter.5.cloned.1.call-done = bf16[48,3072]{1,0:T(8,128)(2,1)} async-done(((bf16[1536,3072]{1,0:T(8,128)(2,1)}), bf16[48,3072]{1,0:T(8,128)(2,1)}) %reduce-scatter.5.cloned.1.call-update) | async-done | bytes 294928 | tf_op jit(solution)/shard_map/reduce_scatter | solution.py:432
  622.6 1.7 fusion.133
  (263 shorter events, 50.9 us)
Async XLA Ops:
  7.2 77.9 %all-gather.3.cloned.1.call-start = ((), (), s32[]{:S(2)}) async-start(), calls=%async_computation.2 | async-start | bytes 6488064 | tf_op jit(solution)/shard_map/all_gather | solution.py:369
  12.9 155.6 %all-gather.5.cloned.1.call-start = ((), (), s32[]{:S(2)}) async-start(), calls=%async_computation.3 | async-start | bytes 9732096 | tf_op jit(solution)/shard_map/all_gather | solution.py:378
  15.6 466.0 %reduce-scatter.3.cloned.1.call-start = ((), (), s32[]{:S(2)}) async-start(), calls=%async_computation.4 | async-start | bytes 6488064 | tf_op jit(solution)/shard_map/reduce_scatter | solution.py:406
  112.1 11.3 %copy-start.22 = (bf16[1,512,1,192]{1,3,2,0:T(8,128)(2,1)}, bf16[1,512,1,192]{1,3,2,0:T(8,128)(2,1)S(1)}, u32[]{:S(2)}) copy-start(bf16[1,512,1,192]{1,3,2,0:T(8,128)(2,1)S(1)} %get-tuple-element.117) | copy-start | bytes 589828
  112.1 11.3 %copy-start.23 = (bf16[1,512,1,192]{1,3,2,0:T(8,128)(2,1)}, bf16[1,512,1,192]{1,3,2,0:T(8,128)(2,1)S(1)}, u32[]{:S(2)}) copy-start(bf16[1,512,1,192]{1,3,2,0:T(8,128)(2,1)S(1)} %get-tuple-element.116) | copy-start | bytes 589828
  116.9 6.4 %copy-start.2 = (bf16[1,512,1,768]{1,3,2,0:T(8,128)(2,1)}, bf16[1,512,1,768]{1,3,2,0:T(8,128)(2,1)S(1)}, u32[]{:S(2)}) copy-start(bf16[1,512,1,768]{1,3,2,0:T(8,128)(2,1)S(1)} %get-tuple-element.105) | copy-start | bytes 2359300
  116.9 6.4 %copy-start.4 = (bf16[1,512,1,768]{1,3,2,0:T(8,128)(2,1)}, bf16[1,512,1,768]{1,3,2,0:T(8,128)(2,1)S(1)}, u32[]{:S(2)}) copy-start(bf16[1,512,1,768]{1,3,2,0:T(8,128)(2,1)S(1)} %get-tuple-element.106) | copy-start | bytes 2359300
  116.9 6.4 %copy-start.56 = (pred[512]{0:T(512)(128)(4,1)S(1)}, pred[512]{0:T(512)(128)(4,1)}, u32[]{:S(2)}) copy-start(pred[512]{0:T(512)(128)(4,1)} %get-tuple-element.161) | copy-start | bytes 1540
  130.0 4.6 copy-start
  136.8 1.5 copy-start.18
  136.8 1.5 copy-start.55
  137.8 4.9 copy-start.12
  138.3 4.4 copy-start.31
  138.3 4.4 copy-start.15
  138.3 4.9 copy-start.25
  142.7 3.8 copy-start.9
  145.7 1.8 copy-start.26
  151.8 1.1 copy-start.57
  152.9 3.2 copy-start.35
  152.9 3.2 copy-start.39
  185.2 19.2 %copy-start.8 = (bf16[3072,768]{1,0:T(8,128)(2,1)S(1)}, bf16[3072,768]{1,0:T(8,128)(2,1)}, u32[]{:S(2)}) copy-start(bf16[3072,768]{1,0:T(8,128)(2,1)} %reshape.1083) | copy-start | bytes 14155780
  185.2 19.2 %copy-start.40 = (f32[768]{0:T(1024)S(1)}, f32[768]{0:T(1024)}, u32[]{:S(2)}) copy-start(f32[768]{0:T(1024)} %get-tuple-element.128) | copy-start | bytes 9220
  185.2 19.2 %copy-start.47 = (f32[768]{0:T(1024)S(1)}, f32[768]{0:T(1024)}, u32[]{:S(2)}) copy-start(f32[768]{0:T(1024)} %get-tuple-element.127) | copy-start | bytes 9220
  204.3 2.9 copy-start.59
  204.4 3.2 copy-start.11
  204.4 3.2 copy-start.36
  207.2 1.2 copy-start.41
  208.4 2.0 copy-start.43
  208.4 10.3 %slice-start.3 = ((s8[4718592]{0:T(1024)(128)(4,1)}), s8[4194304]{0:T(1024)(128)(4,1)S(1)}, s32[]{:S(2)}) async-start(s8[4718592]{0:T(1024)(128)(4,1)} %bitcast.294), calls=%async_computation.9 | async-start | bytes 8388608
  210.3 8.3 %slice-start.4 = ((s8[4718592]{0:T(1024)(128)(4,1)}), s8[524288]{0:T(1024)(128)(4,1)S(1)}, s32[]{:S(2)}) async-start(s8[4718592]{0:T(1024)(128)(4,1)} %bitcast.294), calls=%async_computation.10 | async-start | bytes 1048576
  218.7 3.2 copy-start.38
  223.9 4.1 copy-start.60
  228.1 4.8 copy-start.27
  232.8 5.8 copy-start.21
  238.7 15.7 %slice-start = ((s8[12582912]{0:T(1024)(128)(4,1)}), s8[4194304]{0:T(1024)(128)(4,1)S(1)}, s32[]{:S(2)}) async-start(s8[12582912]{0:T(1024)(128)(4,1)} %bitcast.263), calls=%async_computation.6 | async-start | bytes 8388608
  238.7 15.7 %slice-start.1 = ((s8[12582912]{0:T(1024)(128)(4,1)}), s8[4194304]{0:T(1024)(128)(4,1)S(1)}, s32[]{:S(2)}) async-start(s8[12582912]{0:T(1024)(128)(4,1)} %bitcast.263), calls=%async_computation.7 | async-start | bytes 8388608
  245.5 8.9 %slice-start.2 = ((s8[12582912]{0:T(1024)(128)(4,1)}), s8[4194304]{0:T(1024)(128)(4,1)S(1)}, s32[]{:S(2)}) async-start(s8[12582912]{0:T(1024)(128)(4,1)} %bitcast.263), calls=%async_computation.8 | async-start | bytes 8388608
  254.3 19.2 %copy-start.34 = (f32[12,512]{1,0:T(8,128)}, f32[12,512]{1,0:T(8,128)S(1)}, u32[]{:S(2)}) copy-start(f32[12,512]{1,0:T(8,128)S(1)} %get-tuple-element.159) | copy-start | bytes 73732
  254.4 7.1 %copy-start.5 = (bf16[1,512,1,768]{1,3,2,0:T(8,128)(2,1)S(1)}, bf16[1,512,1,768]{1,3,2,0:T(8,128)(2,1)}, u32[]{:S(2)}) copy-start(bf16[1,512,1,768]{1,3,2,0:T(8,128)(2,1)} %copy-done.4) | copy-start | bytes 2359300
  261.5 2.0 copy-start.3
  263.5 1.2 copy-start.14
  267.1 6.4 %copy-start.24 = (bf16[1,512,1,192]{1,3,2,0:T(8,128)(2,1)S(1)}, bf16[1,512,1,192]{1,3,2,0:T(8,128)(2,1)}, u32[]{:S(2)}) copy-start(bf16[1,512,1,192]{1,3,2,0:T(8,128)(2,1)} %copy-done.23) | copy-start | bytes 589828
  298.7 22.3 %copy-start.13 = (bf16[12,16,512]{2,1,0:T(8,128)(2,1)S(1)}, bf16[12,16,512]{2,1,0:T(8,128)(2,1)}, u32[]{:S(2)}) copy-start(bf16[12,16,512]{2,1,0:T(8,128)(2,1)} %copy-done.12) | copy-start | bytes 589828
  298.7 31.4 %copy-start.10 = (bf16[512,768]{1,0:T(8,128)(2,1)S(1)}, bf16[512,768]{1,0:T(8,128)(2,1)}, u32[]{:S(2)}) copy-start(bf16[512,768]{1,0:T(8,128)(2,1)} %copy-done.9) | copy-start | bytes 2359300
  338.6 6.0 copy-start.45
  338.6 6.1 copy-start.46
  338.6 6.1 copy-start.44
  338.6 7.0 %copy-start.58 = (bf16[1,512,768]{2,1,0:T(8,128)(2,1)S(1)}, bf16[1,512,768]{2,1,0:T(8,128)(2,1)}, u32[]{:S(2)}) copy-start(bf16[1,512,768]{2,1,0:T(8,128)(2,1)} %param.13) | copy-start | bytes 2359300
  345.5 3.8 copy-start.19
  351.8 6.8 %copy-start.28 = (bf16[12,16,512]{2,1,0:T(8,128)(2,1)S(1)}, bf16[12,16,512]{2,1,0:T(8,128)(2,1)}, u32[]{:S(2)}) copy-start(bf16[12,16,512]{2,1,0:T(8,128)(2,1)} %fusion.74) | copy-start | bytes 589828
  351.8 6.8 %copy-start.32 = (bf16[12,16,512]{2,1,0:T(8,128)(2,1)S(1)}, bf16[12,16,512]{2,1,0:T(8,128)(2,1)}, u32[]{:S(2)}) copy-start(bf16[12,16,512]{2,1,0:T(8,128)(2,1)} %fusion.71) | copy-start | bytes 589828
  351.8 6.8 %copy-start.33 = (bf16[12,16,512]{2,1,0:T(8,128)(2,1)S(1)}, bf16[12,16,512]{2,1,0:T(8,128)(2,1)}, u32[]{:S(2)}) copy-start(bf16[12,16,512]{2,1,0:T(8,128)(2,1)} %fusion.68) | copy-start | bytes 589828
  351.8 7.1 %copy-start.42 = (bf16[1,768]{1,0:T(2,128)(2,1)S(1)}, bf16[1,768]{1,0:T(2,128)(2,1)}, u32[]{:S(2)}) copy-start(bf16[1,768]{1,0:T(2,128)(2,1)} %reduce_sum.440) | copy-start | bytes 4612
  351.8 7.1 %copy-start.49 = (bf16[1,192]{1,0:T(2,128)(2,1)S(1)}, bf16[1,192]{1,0:T(2,128)(2,1)}, u32[]{:S(2)}) copy-start(bf16[1,192]{1,0:T(2,128)(2,1)} %convert.163) | copy-start | bytes 1156
  351.8 7.1 %copy-start.50 = (bf16[1,192]{1,0:T(2,128)(2,1)S(1)}, bf16[1,192]{1,0:T(2,128)(2,1)}, u32[]{:S(2)}) copy-start(bf16[1,192]{1,0:T(2,128)(2,1)} %convert.164) | copy-start | bytes 1156
  351.8 7.1 %copy-start.51 = (bf16[1,192]{1,0:T(2,128)(2,1)S(1)}, bf16[1,192]{1,0:T(2,128)(2,1)}, u32[]{:S(2)}) copy-start(bf16[1,192]{1,0:T(2,128)(2,1)} %convert.165) | copy-start | bytes 1156
  351.8 7.1 %copy-start.52 = (bf16[1,192]{1,0:T(2,128)(2,1)S(1)}, bf16[1,192]{1,0:T(2,128)(2,1)}, u32[]{:S(2)}) copy-start(bf16[1,192]{1,0:T(2,128)(2,1)} %convert.166) | copy-start | bytes 1156
  351.8 7.1 %copy-start.53 = (bf16[1,192]{1,0:T(2,128)(2,1)S(1)}, bf16[1,192]{1,0:T(2,128)(2,1)}, u32[]{:S(2)}) copy-start(bf16[1,192]{1,0:T(2,128)(2,1)} %convert.167) | copy-start | bytes 1156
  351.9 7.1 %copy-start.54 = (bf16[1,192]{1,0:T(2,128)(2,1)S(1)}, bf16[1,192]{1,0:T(2,128)(2,1)}, u32[]{:S(2)}) copy-start(bf16[1,192]{1,0:T(2,128)(2,1)} %convert.168) | copy-start | bytes 1156
  351.9 7.3 %copy-start.30 = (bf16[1,512,192]{1,2,0:T(8,128)(2,1)S(1)}, bf16[1,512,192]{1,2,0:T(8,128)(2,1)}, u32[]{:S(2)}) copy-start(bf16[1,512,192]{1,2,0:T(8,128)(2,1)} %param.14) | copy-start | bytes 589828
  362.5 2.3 copy-start.1
  368.0 254.6 %reduce-scatter.5.cloned.1.call-start = ((), (), s32[]{:S(2)}) async-start(), calls=%async_computation.5 | async-start | bytes 9732096 | tf_op jit(solution)/shard_map/reduce_scatter | solution.py:432
  386.2 2.7 copy-start.17
  387.7 3.6 copy-start.7
  (6 other events, 5.8 us)
Sparse Core Ops, SparseCore 0:
  13.0 71.9 all-gather.2
  88.5 79.9 all-gather.4
  368.1 113.5 reduce-scatter.2
  487.4 135.1 reduce-scatter.4

commit v4 on v3

--- a/solution.py
+++ b/solution.py
@@ -112,8 +112,9 @@
     )
     text_ds = probs * (text_dp - jnp.sum(probs * text_dp, -1, keepdims=True))
     layout_ds = probs * (layout_dp - jnp.sum(probs * layout_dp, -1, keepdims=True))
-    text_only = text_ds.astype(jnp.bfloat16)
-    joint_ds = (text_ds + layout_ds).astype(jnp.bfloat16)
+    text_only, joint_ds = lax.optimization_barrier(
+        (text_ds.astype(jnp.bfloat16), (text_ds + layout_ds).astype(jnp.bfloat16))
+    )
     text_dq = jnp.einsum(
         "hqk,khd->qhd", text_only, split_heads(text_three[:, 1]), preferred_element_type=jnp.float32
     ) * HD ** (-0.5)
@@ -373,11 +374,8 @@
     small_flat = first_all[:, rows:].reshape(count, -1)
     shapes = [(1, text_vectors.shape[0]), layout_attn.shape, layout_w1.shape, layout_w2.shape, (1, layout_vectors.shape[0])]
     full_small = unpack_small(small_flat, count, shapes)
-    w2_rows = text_w2.shape[0]
-    second = jnp.concatenate([text_w1, text_w2.reshape(rows, -1)], 0)
-    second_all = lax.all_gather(second, AXES, axis=0, tiled=True).reshape(count, 2 * rows, width)
-    full_w1 = second_all[:, :rows].reshape(count * rows, width)
-    full_w2 = second_all[:, rows:].reshape(count * w2_rows, text_w2.shape[1])
+    full_w1 = lax.all_gather(text_w1, AXES, axis=0, tiled=True)
+    full_w2 = lax.all_gather(text_w2, AXES, axis=0, tiled=True)
     return (full_attn, full_w1, full_w2) + full_small
 
 
@@ -423,16 +421,19 @@
     )
 
 
-def scatter_early(count, grad_first, grad_second):
+def pack_early(count, grad_first, grad_second):
     width = grad_first.shape[1]
     rows = grad_first.shape[0] // count
     packed = jnp.concatenate(
         [grad_first.reshape(count, rows, width), grad_second.reshape(count, rows, width)], 1
     )
-    summed = lax.psum_scatter(
-        packed.reshape(-1, width).astype(jnp.bfloat16), AXES, scatter_dimension=0, tiled=True
-    ).astype(jnp.float32)
-    return (summed[:rows], summed[rows:].reshape(-1, grad_second.shape[1]))
+    return packed.reshape(-1, width).astype(jnp.bfloat16)
+
+
+def scatter_early(count, packed, second_shape):
+    rows = packed.shape[0] // (2 * count)
+    summed = lax.psum_scatter(packed, AXES, scatter_dimension=0, tiled=True).astype(jnp.float32)
+    return (summed[:rows], summed[rows:].reshape(-1, second_shape[1]))
 
 
 def body(
@@ -468,8 +469,9 @@
         jnp.einsum("sd,sf->df", flat_rows(text_hidden), flat_rows(text_inner_low), preferred_element_type=jnp.float32),
         jnp.einsum("sf,sd->fd", flat_rows(text_active), flat_rows(text_second_low), preferred_element_type=jnp.float32),
     )
-    early, text_back, layout_back = lax.optimization_barrier((early, text_back, layout_back))
-    grad_first, grad_second = scatter_early(count, *early)
+    packed = pack_early(count, *early)
+    packed, text_back, layout_back = lax.optimization_barrier((packed, text_back, layout_back))
+    grad_first, grad_second = scatter_early(count, packed, early[1].shape)
     (text_grad, layout_grad), small_terms, text_rounded = jax.vmap(
         page_back_attn, in_axes=(0, 0, 0, 0, 0, 0, page_weights)
     )(text_in, layout_in, lengths, kept_all, text_back, layout_back, weights)

time: 638 us -> 638 us (level)
  waiting for transfers between devices: 297 us -> 347 us
  local copies, waits for them, and re-layouts: 96.1 us -> 75.7 us
  matrix products: 169 us -> 152 us
  other arithmetic: 53.4 us -> 41.3 us
    sub x0 -> x2, matrix products: none -> 35.4 us  [the longest x1 19.9 us: attend_back(): layout_dp - jnp.sum(probs * layout_dp, -1, keepdims=True)]
    all_gather x1 -> x2, waiting for transfers between devices: 11.2 us -> 40.8 us  [the longest x1 40.8 us: gather_weights(): full_w2 = lax.all_gather(text_w2, AXES, axis=0, tiled=True)]
    dot_general x1, matrix products: 25.2 us -> 0.92 us  [attend_back(): jnp.einsum('hqk,khd->qhd', joint_ds, split_heads(layout_three[:, 1]), pre...]
    dot_general x1, matrix products: 22.3 us -> 1.74 us  [attend_back(): jnp.einsum('hqk,qhd->khd', joint_ds, split_heads(layout_three[:, 0]), pre...]
    reduce_scatter x1, waiting for transfers between devices: 84.6 us -> 101 us  [scatter_late(): lax.psum_scatter(packed.reshape(-1, width).astype(jnp.bfloat16), AXES, sc...]
    dot_general x2 -> x0, matrix products: 15.3 us -> none  [the longest x1 8.87 us: attend_back(): jnp.einsum('qhd,khd->hqk', text_heads, split_heads(text_three[:, 2]), pre...]
    reshape x4 -> x2, local copies, waits for them, and re-layouts: 19 us -> 9.27 us  [the longest x1 8.48 us: pack_early(): grad_second.reshape(count, rows, width)]
    slice x2 -> x1, local copies, waits for them, and re-layouts: 9.95 us -> 1.73 us  [scatter_early(): return (summed[:rows], summed[rows:].reshape(-1, second_shape[1]))]
  transfers between devices with their start and end apart: 4 -> 5, of which waited for: 4 -> 4; matrix products, arithmetic and copies ran while one was open for 17% -> 17% of each run, Pallas kernels for 0% -> 0%
where the time goes in v4:
time: 638 us; the launch traced here: 632 us
  waiting for transfers between devices  347 us (54%)
  matrix products  152 us (24%)
  local copies, waits for them, and re-layouts  75.7 us (12%)
  other arithmetic  41.3 us (6%)
  between operations  15.9 us (2%)
    reduce_scatter x1, waiting for transfers between devices, scatter_early(): lax.psum_scatter(packed, AXES, scatter_dimension=0, tiled=True)  134 us
    reduce_scatter x1, waiting for transfers between devices, scatter_late(): lax.psum_scatter(packed.reshape(-1, width).astype(jnp.bfloat16), AXES, sc...  101 us
    all_gather x1, waiting for transfers between devices, gather_weights(): first_all = lax.all_gather(first, AXES, axis=0, tiled=True)  69.4 us
    all_gather x1, waiting for transfers between devices, gather_weights(): full_w2 = lax.all_gather(text_w2, AXES, axis=0, tiled=True)  40.8 us
    dot_general x2, matrix products, branch_forward(): jnp.dot(hidden.astype(jnp.bfloat16), first, preferred_element_type=jnp.fl...  23.9 us
    sub x1, matrix products, attend_back(): layout_dp - jnp.sum(probs * layout_dp, -1, keepdims=True)  19.9 us
    sub x1, matrix products, attend_back(): text_ds = probs * (text_dp - jnp.sum(probs * text_dp, -1, keepdims=True))  15.6 us
  transfers between devices with their start and end apart: 5, of which 4 were waited for; matrix products, arithmetic and copies ran while one was open for 17% of the time, Pallas kernels for 0%

profile of v4, /device:TPU:0, one launch (start us, length us, event | category | flops | bytes accessed | tf_op | source)
XLA Modules:
  0.0 632.5 jit_solution(522546584664306357)
XLA Ops:
  9.8 1.5 concatenate.62
  11.3 1.6 pad_maximum_fusion.8
  15.7 69.4 %all-gather.4.cloned.1.call-done = bf16[1024,3072]{1,0:T(8,128)(2,1)} async-done(((bf16[32,3072]{1,0:T(8,128)(2,1)}), bf16[1024,3072]{1,0:T(8,128)(2,1)}) %all-gather.4.cloned.1.call-update) | async-done | bytes 6291472 | tf_op jit(solution)/shard_map/all_gather | solution.py:370
  85.1 1.5 slice.226
  86.6 4.8 slice.224
  97.6 1.1 reshape.1070
  99.9 2.5 reshape.1068
  102.5 1.7 copy.50
  104.2 2.2 slice.225
  106.4 3.6 copy.46
  110.8 4.4 fusion.31
  115.4 6.4 %fusion.155 = f32[12,512,512]{1,2,0:T(8,128)} fusion(bf16[512,12,64]{0,2,1:T(8,128)(2,1)S(1)} %bitcast.312, bf16[512,12,64]{0,2,1:T(8,128)(2,1)S(1)} %bitcast.306), kind=kOutput, calls=%fused_computation.250 | convolution fusion | flops 402653184 | bytes 14155776 | tf_op jit(solution)/shard_map/vmap(qhd,khd->hqk)/dot_general | solution.py:54
  121.8 6.6 %fusion.149 = (f32[12,512]{1,0:T(8,128)S(1)}, f32[12,512,512]{1,2,0:T(8,128)S(1)}) fusion(bf16[512,12,16]{0,2,1:T(8,128)(2,1)S(1)} %bitcast.342, bf16[512,12,16]{0,2,1:T(8,128)(2,1)S(1)} %bitcast.335, f32[12,512,512]{1,2,0:T(8,128)} %fusion.155, pred[512]{0:T(512)(128)(4,1)S(1)} %copy-done.65), kind=kOutput, calls=%fused_computation.244 | convolution fusion | flops 116385792 | bytes 25584128 | tf_op jit(solution)/shard_map/vmap(qhd,khd->hqk)/dot_general | solution.py:60
  128.4 1.8 fusion.4
  130.2 3.0 copy-done
  133.2 2.3 divide_convert_fusion
  137.1 4.7 multiply_convert_fusion.3
  145.7 1.6 fusion.142
  147.2 1.1 convolution_convert_fusion.5
  148.4 2.5 fusion.150
  151.3 1.2 fusion.70
  152.5 1.2 fusion.202
  153.7 1.1 fusion.132
  154.8 19.3 %multiply_convert_fusion = (bf16[512,3072]{1,0:T(8,128)(2,1)}, f32[512,3072]{1,0:T(8,128)}, f32[512,3072]{1,0:T(8,128)}) fusion(f32[3072]{0:T(1024)S(1)} %copy-done.45, bf16[768,3072]{1,0:T(8,128)(2,1)} %all-gather.6.cloned.1.call-done, bf16[1,512,768]{2,1,0:T(8,128)(2,1)} %fusion.70), kind=kOutput, calls=%fused_computation.30 | convolution fusion | flops 2519728128 | bytes 21245952 | tf_op jit(solution)/shard_map/vmap()/dot_general | solution.py:166
  174.1 40.8 %all-gather.8.cloned.1.call-done = bf16[3072,768]{1,0:T(8,128)(2,1)} async-done(((bf16[96,768]{1,0:T(8,128)(2,1)}), bf16[3072,768]{1,0:T(8,128)(2,1)}) %all-gather.8.cloned.1.call-update) | async-done | bytes 4718608 | tf_op jit(solution)/shard_map/all_gather | solution.py:378
  214.9 6.1 fusion.151
  221.4 1.3 multiply_reduce_fusion.2
  222.7 1.7 fusion.138
  225.3 8.0 %fusion.154 = (f32[3072]{0:T(1024)S(1)}, bf16[512,3072]{1,0:T(8,128)(2,1)S(1)}) fusion(f32[512,3072]{1,0:T(8,128)} %get-tuple-element.104, bf16[3072,768]{1,0:T(8,128)(2,1)S(1)} %copy-done.66, bf16[1,512,768]{2,1,0:T(8,128)(2,1)S(1)} %get-tuple-element.110, f32[512,3072]{1,0:T(8,128)} %get-tuple-element.147, f32[3072]{0:T(1024)S(1)} %copy-done.46), kind=kOutput, calls=%fused_computation.249 | convolution fusion | flops 2441081856 | bytes 21258240 | tf_op jit(solution)/shard_map/vmap()/dot_general | solution.py:184
  233.4 3.1 multiply_reduce_fusion.3
  237.5 3.6 fusion.69
  241.1 1.9 convolution_convert_fusion.3
  243.0 4.5 convolution_convert_fusion.1
  247.5 1.4 copy.51
  251.4 8.5 %reshape.1072 = bf16[32,24,3072]{2,1,0:T(8,128)(2,1)} reshape(bf16[3072,768]{1,0:T(8,128)(2,1)} %convolution_convert_fusion.1) | data formatting | bytes 9437184 | tf_op jit(solution)/shard_map/reshape | solution.py:428
  259.9 4.9 convolution_convert_fusion.2
  264.8 4.0 pad_maximum_fusion
  269.0 7.5 %fusion.63 = bf16[12,64,512]{2,1,0:T(8,128)(2,1)} fusion(bf16[512,12,64]{0,2,1:T(8,128)(2,1)S(1)} %bitcast.304, f32[12,512,512]{1,2,0:T(8,128)} %copy-done, f32[12,512]{1,0:T(8,128)S(1)} %log_add_fusion), kind=kOutput, calls=%fused_computation.106 | convolution fusion | flops 409337856 | bytes 14180352 | tf_op jit(solution)/shard_map/vmap(hqk,qhd->khd)/dot_general | solution.py:109
  276.5 15.6 %subtract_multiply_fusion = f32[12,512,512]{1,2,0:T(8,128)} fusion(f32[12,512,512]{1,2,0:T(8,128)} %copy-done, f32[12,512]{1,0:T(8,128)S(1)} %log_add_fusion, bf16[512,12,64]{0,2,1:T(8,128)(2,1)S(1)} %bitcast.305, bf16[512,12,64]{0,2,1:T(8,128)(2,1)S(1)} %bitcast.300), kind=kOutput, calls=%fused_computation.5 | convolution fusion | flops 821041664 | bytes 26763264 | tf_op jit(solution)/shard_map/vmap()/sub | solution.py:113
  292.1 7.0 %fusion.91 = bf16[12,16,512]{2,1,0:T(8,128)(2,1)} fusion(bf16[512,12,16]{0,2,1:T(8,128)(2,1)S(1)} %bitcast.331, f32[12,512,512]{1,2,0:T(8,128)} %copy-done, f32[12,512]{1,0:T(8,128)S(1)} %log_add_fusion), kind=kOutput, calls=%fused_computation.135 | convolution fusion | flops 107053056 | bytes 13000704 | tf_op jit(solution)/shard_map/vmap(hqk,qhd->khd)/dot_general | solution.py:110
  299.1 19.9 %fusion.28 = bf16[1,12,512,512]{2,3,1,0:T(8,128)(2,1)} fusion(f32[12,512,512]{1,2,0:T(8,128)} %subtract_multiply_fusion, f32[12,512,512]{1,2,0:T(8,128)} %copy-done, f32[12,512]{1,0:T(8,128)S(1)} %log_add_fusion, bf16[512,12,16]{0,2,1:T(8,128)(2,1)S(1)} %bitcast.332, bf16[512,12,16]{0,2,1:T(8,128)(2,1)S(1)} %bitcast.323), kind=kOutput, calls=%fused_computation.51 | convolution fusion | flops 223353344 | bytes 31875072 | tf_op jit(solution)/shard_map/vmap()/sub | solution.py:114
  319.0 5.4 convert_bitcast_fusion
  324.5 4.2 multiply_convert_fusion.1
  328.6 2.0 multiply_convert_fusion.2
  331.1 1.7 fusion.85
  336.7 1.6 copy.67
  338.3 4.1 reshape.1087
  342.9 1.3 convolution_convert_fusion.7
  345.3 1.7 fusion.133
  347.4 2.0 concatenate.69
  349.5 2.1 copy.81
  351.6 2.0 fusion.26
  353.6 2.4 pad_maximum_fusion.2
  356.0 6.7 %copy.63 = bf16[768,3072]{1,0:T(8,128)(2,1)} copy(bf16[768,3072]{0,1:T(8,128)(2,1)} %pad_maximum_fusion.2) | data formatting | bytes 9437184 | tf_op jit(solution)/shard_map/concatenate | solution.py:485
  362.7 6.1 pad_maximum_fusion.1
  369.5 1.2 copy.58
  370.7 1.2 copy.57
  371.8 1.2 copy.56
  373.0 2.1 fusion.75
  375.1 6.1 bitcast_add_fusion
  381.1 101.1 %reduce-scatter.3.cloned.1.call-done = bf16[32,3072]{1,0:T(8,128)(2,1)} async-done(((bf16[1024,3072]{1,0:T(8,128)(2,1)}), bf16[32,3072]{1,0:T(8,128)(2,1)}) %reduce-scatter.3.cloned.1.call-update) | async-done | bytes 196624 | tf_op jit(solution)/shard_map/reduce_scatter | solution.py:404
  487.7 1.6 slice.262
  489.3 133.9 %reduce-scatter.5.cloned.1.call-done = bf16[48,3072]{1,0:T(8,128)(2,1)} async-done(((bf16[1536,3072]{1,0:T(8,128)(2,1)}), bf16[48,3072]{1,0:T(8,128)(2,1)}) %reduce-scatter.5.cloned.1.call-update) | async-done | bytes 294928 | tf_op jit(solution)/shard_map/reduce_scatter | solution.py:435
  623.2 1.7 fusion.145
  (283 shorter events, 36.5 us)
Async XLA Ops:
  7.2 77.9 %all-gather.4.cloned.1.call-start = ((), (), s32[]{:S(2)}) async-start(), calls=%async_computation.2 | async-start | bytes 6488064 | tf_op jit(solution)/shard_map/all_gather | solution.py:370
  12.9 141.9 %all-gather.6.cloned.1.call-start = ((), (), s32[]{:S(2)}) async-start(), calls=%async_computation.3 | async-start | bytes 4866048 | tf_op jit(solution)/shard_map/all_gather | solution.py:377
  13.6 201.3 %all-gather.8.cloned.1.call-start = ((), (), s32[]{:S(2)}) async-start(), calls=%async_computation.4 | async-start | bytes 4866048 | tf_op jit(solution)/shard_map/all_gather | solution.py:378
  14.4 467.8 %reduce-scatter.3.cloned.1.call-start = ((), (), s32[]{:S(2)}) async-start(), calls=%async_computation.5 | async-start | bytes 6488064 | tf_op jit(solution)/shard_map/reduce_scatter | solution.py:404
  15.7 83.0 %copy-start.64 = (f32[3]{0:T(128)}, f32[3]{0:T(128)S(1)}, u32[]{:S(2)}) copy-start(f32[3]{0:T(128)S(1)} %pad.35.clone) | copy-start | bytes 40
  91.4 7.4 %copy-start.39 = (bf16[1,512,192]{1,2,0:T(8,128)(2,1)S(1)}, bf16[1,512,192]{1,2,0:T(8,128)(2,1)}, u32[]{:S(2)}) copy-start(bf16[1,512,192]{1,2,0:T(8,128)(2,1)} %param.14) | copy-start | bytes 589828
  97.6 2.3 copy-start.38
  115.3 6.4 %copy-start.2 = (bf16[1,512,1,768]{1,3,2,0:T(8,128)(2,1)}, bf16[1,512,1,768]{1,3,2,0:T(8,128)(2,1)S(1)}, u32[]{:S(2)}) copy-start(bf16[1,512,1,768]{1,3,2,0:T(8,128)(2,1)S(1)} %get-tuple-element.105) | copy-start | bytes 2359300
  115.3 6.4 %copy-start.6 = (bf16[1,512,1,768]{1,3,2,0:T(8,128)(2,1)}, bf16[1,512,1,768]{1,3,2,0:T(8,128)(2,1)S(1)}, u32[]{:S(2)}) copy-start(bf16[1,512,1,768]{1,3,2,0:T(8,128)(2,1)S(1)} %get-tuple-element.106) | copy-start | bytes 2359300
  115.3 6.4 %copy-start.15 = (bf16[1,512,1,192]{1,3,2,0:T(8,128)(2,1)S(1)}, bf16[1,512,1,192]{1,3,2,0:T(8,128)(2,1)}, u32[]{:S(2)}) copy-start(bf16[1,512,1,192]{1,3,2,0:T(8,128)(2,1)} %get-tuple-element.116) | copy-start | bytes 589828
  115.4 6.4 %copy-start.22 = (bf16[1,512,1,192]{1,3,2,0:T(8,128)(2,1)S(1)}, bf16[1,512,1,192]{1,3,2,0:T(8,128)(2,1)}, u32[]{:S(2)}) copy-start(bf16[1,512,1,192]{1,3,2,0:T(8,128)(2,1)} %get-tuple-element.117) | copy-start | bytes 589828
  115.4 6.4 %copy-start.65 = (pred[512]{0:T(512)(128)(4,1)S(1)}, pred[512]{0:T(512)(128)(4,1)}, u32[]{:S(2)}) copy-start(pred[512]{0:T(512)(128)(4,1)} %iota_compare_fusion) | copy-start | bytes 1540
  128.4 4.8 copy-start
  133.2 2.3 copy-start.10
  135.5 1.5 copy-start.27
  135.5 1.5 copy-start.62
  136.4 5.3 copy-start.17
  137.0 4.8 copy-start.41
  137.0 4.8 copy-start.24
  137.0 4.8 copy-start.52
  137.0 5.3 copy-start.33
  137.0 5.3 copy-start.49
  137.1 6.1 copy-start.53
  141.8 3.9 copy-start.11
  148.4 2.9 copy-start.19
  152.5 2.3 copy-start.45
  154.8 60.1 %copy-start.60 = (f32[768]{0:T(1024)S(1)}, f32[768]{0:T(1024)}, u32[]{:S(2)}) copy-start(f32[768]{0:T(1024)} %get-tuple-element.127) | copy-start | bytes 9220
  214.9 6.4 %copy-start.14 = (bf16[1,512,768]{2,1,0:T(8,128)(2,1)S(1)}, bf16[1,512,768]{2,1,0:T(8,128)(2,1)}, u32[]{:S(2)}) copy-start(bf16[1,512,768]{2,1,0:T(8,128)(2,1)} %param.24) | copy-start | bytes 2359300
  214.9 6.4 %copy-start.43 = (f32[768]{0:T(1024)S(1)}, f32[768]{0:T(1024)}, u32[]{:S(2)}) copy-start(f32[768]{0:T(1024)} %get-tuple-element.125) | copy-start | bytes 9220
  221.0 1.7 copy-start.44
  222.7 2.0 copy-start.46
  222.7 2.6 copy-start.66
  224.4 8.9 %slice-start.2 = ((s8[4718592]{0:T(1024)(128)(4,1)}), s8[4194304]{0:T(1024)(128)(4,1)S(1)}, s32[]{:S(2)}) async-start(s8[4718592]{0:T(1024)(128)(4,1)} %bitcast.373), calls=%async_computation.9 | async-start | bytes 8388608
  225.3 8.0 %slice-start.3 = ((s8[4718592]{0:T(1024)(128)(4,1)}), s8[524288]{0:T(1024)(128)(4,1)S(1)}, s32[]{:S(2)}) async-start(s8[4718592]{0:T(1024)(128)(4,1)} %bitcast.373), calls=%async_computation.10 | async-start | bytes 1048576
  233.3 3.2 copy-start.70
  237.4 5.6 copy-start.8
  237.4 3.7 copy-start.20
  237.5 5.5 copy-start.69
  243.0 6.0 copy-start.51
  247.5 3.3 copy-start.50
  250.5 9.4 %copy-start.25 = (f32[1,512,192]{1,2,0:T(8,128)}, f32[1,512,192]{1,2,0:T(8,128)S(1)}, u32[]{:S(2)}) copy-start(f32[1,512,192]{1,2,0:T(8,128)S(1)} %get-tuple-element.42) | copy-start | bytes 1179652
  259.9 4.9 copy-start.1
  264.7 4.0 copy-start.32
  324.4 4.2 copy-start.3
  324.4 6.2 slice-start
  328.6 2.4 slice-start.1
  328.6 2.5 copy-start.23
  331.1 1.7 copy-start.16
  332.9 10.1 %copy-start.30 = (bf16[12,16,512]{2,1,0:T(8,128)(2,1)}, bf16[12,16,512]{2,1,0:T(8,128)(2,1)S(1)}, u32[]{:S(2)}) copy-start(bf16[12,16,512]{2,1,0:T(8,128)(2,1)S(1)} %fusion.85) | copy-start | bytes 589828
  333.9 2.1 copy-start.13
  333.9 2.4 copy-start.42
  336.0 6.5 %copy-start.36 = (bf16[12,16,512]{2,1,0:T(8,128)(2,1)S(1)}, bf16[12,16,512]{2,1,0:T(8,128)(2,1)}, u32[]{:S(2)}) copy-start(bf16[12,16,512]{2,1,0:T(8,128)(2,1)} %fusion.91) | copy-start | bytes 589828
  338.3 7.0 %copy-start.4 = (bf16[12,64,512]{2,1,0:T(8,128)(2,1)S(1)}, bf16[12,64,512]{2,1,0:T(8,128)(2,1)}, u32[]{:S(2)}) copy-start(bf16[12,64,512]{2,1,0:T(8,128)(2,1)} %multiply_convert_fusion.2) | copy-start | bytes 2359300
  338.3 7.0 %copy-start.5 = (bf16[12,64,512]{2,1,0:T(8,128)(2,1)S(1)}, bf16[12,64,512]{2,1,0:T(8,128)(2,1)}, u32[]{:S(2)}) copy-start(bf16[12,64,512]{2,1,0:T(8,128)(2,1)} %fusion.63) | copy-start | bytes 2359300
  338.3 7.0 %copy-start.7 = (bf16[12,64,512]{2,1,0:T(8,128)(2,1)S(1)}, bf16[12,64,512]{2,1,0:T(8,128)(2,1)}, u32[]{:S(2)}) copy-start(bf16[12,64,512]{2,1,0:T(8,128)(2,1)} %multiply_convert_fusion.1) | copy-start | bytes 2359300
  344.2 2.9 copy-start.47
  349.4 2.2 copy-start.21
  349.4 2.2 copy-start.68
  351.6 2.0 copy-start.28
  368.9 254.3 %reduce-scatter.5.cloned.1.call-start = ((), (), s32[]{:S(2)}) async-start(), calls=%async_computation.6 | async-start | bytes 9732096 | tf_op jit(solution)/shard_map/reduce_scatter | solution.py:435
  369.5 3.5 copy-start.26
  369.5 3.5 copy-start.31
  369.5 3.5 copy-start.37
  371.8 3.3 copy-start.9
  (16 other events, 19.7 us)
Sparse Core Ops, SparseCore 0:
  13.0 71.9 all-gather.3
  87.9 62.1 all-gather.5
  153.0 61.8 all-gather.7
  369.0 113.1 reduce-scatter.2
  488.0 135.1 reduce-scatter.4

commit v5 on v4

--- a/solution.py
+++ b/solution.py
@@ -374,8 +374,11 @@
     small_flat = first_all[:, rows:].reshape(count, -1)
     shapes = [(1, text_vectors.shape[0]), layout_attn.shape, layout_w1.shape, layout_w2.shape, (1, layout_vectors.shape[0])]
     full_small = unpack_small(small_flat, count, shapes)
-    full_w1 = lax.all_gather(text_w1, AXES, axis=0, tiled=True)
-    full_w2 = lax.all_gather(text_w2, AXES, axis=0, tiled=True)
+    w2_rows = text_w2.shape[0]
+    second = jnp.concatenate([text_w1, text_w2.reshape(rows, -1)], 0)
+    second_all = lax.all_gather(second, AXES, axis=0, tiled=True).reshape(count, 2 * rows, width)
+    full_w1 = second_all[:, :rows].reshape(count * rows, width)
+    full_w2 = second_all[:, rows:].reshape(count * w2_rows, text_w2.shape[1])
     return (full_attn, full_w1, full_w2) + full_small
 
 

time: 638 us -> 624 us (0.978)
  waiting for transfers between devices: 347 us -> 308 us
  local copies, waits for them, and re-layouts: 75.7 us -> 98 us
    all_gather x2 -> x1, waiting for transfers between devices: 40.8 us -> 4.27 us  [gather_weights(): lax.all_gather(second, AXES, axis=0, tiled=True)]
    reshape x0 -> x2, local copies, waits for them, and re-layouts: none -> 9.5 us  [the longest x1 8.49 us: gather_weights(): full_w2 = second_all[:, rows:].reshape(count * w2_rows, text_w2.shape[1])]
    slice x0 -> x1, local copies, waits for them, and re-layouts: none -> 8.45 us  [gather_weights(): full_w2 = second_all[:, rows:].reshape(count * w2_rows, text_w2.shape[1])]
  transfers between devices with their start and end apart: 5 -> 4, of which waited for: 4 -> 4; matrix products, arithmetic and copies ran while one was open for 17% -> 15% of each run, Pallas kernels for 0% -> 0%
where the time goes in v5:
time: 624 us; the launch traced here: 618 us
  waiting for transfers between devices  308 us (49%)
  matrix products  154 us (25%)
  local copies, waits for them, and re-layouts  98 us (16%)
  other arithmetic  41.9 us (7%)
  between operations  16.2 us (3%)
    reduce_scatter x1, waiting for transfers between devices, scatter_early(): lax.psum_scatter(packed, AXES, scatter_dimension=0, tiled=True)  134 us
    reduce_scatter x1, waiting for transfers between devices, scatter_late(): lax.psum_scatter(packed.reshape(-1, width).astype(jnp.bfloat16), AXES, sc...  101 us
    all_gather x1, waiting for transfers between devices, gather_weights(): first_all = lax.all_gather(first, AXES, axis=0, tiled=True)  67.6 us
    dot_general x2, matrix products, branch_forward(): jnp.dot(hidden.astype(jnp.bfloat16), first, preferred_element_type=jnp.fl...  23.7 us
    sub x1, matrix products, attend_back(): layout_dp - jnp.sum(probs * layout_dp, -1, keepdims=True)  19.5 us
    sub x1, matrix products, attend_back(): text_ds = probs * (text_dp - jnp.sum(probs * text_dp, -1, keepdims=True))  15.7 us
  transfers between devices with their start and end apart: 4, of which 4 were waited for; matrix products, arithmetic and copies ran while one was open for 15% of the time, Pallas kernels for 0%

profile of v5, /device:TPU:0, one launch (start us, length us, event | category | flops | bytes accessed | tf_op | source)
XLA Modules:
  0.0 617.9 jit_solution(12079433636967853934)
XLA Ops:
  9.8 1.5 concatenate.65
  11.3 1.6 pad_maximum_fusion.9
  14.0 1.6 pad_maximum_fusion.6
  17.4 67.6 %all-gather.3.cloned.1.call-done = bf16[1024,3072]{1,0:T(8,128)(2,1)} async-done(((bf16[32,3072]{1,0:T(8,128)(2,1)}), bf16[1024,3072]{1,0:T(8,128)(2,1)}) %all-gather.3.cloned.1.call-update) | async-done | bytes 6291472 | tf_op jit(solution)/shard_map/all_gather | solution.py:370
  85.1 1.5 slice.234
  86.6 4.8 slice.232
  98.8 2.5 reshape.1084
  101.3 1.6 copy.50
  103.0 2.2 slice.233
  105.2 3.6 copy.46
  108.8 1.5 fusion.149
  111.0 1.4 fusion.71
  113.2 4.5 fusion.31
  117.9 6.4 %fusion.156 = f32[12,512,512]{1,2,0:T(8,128)} fusion(bf16[512,12,64]{0,2,1:T(8,128)(2,1)S(1)} %bitcast.314, bf16[512,12,64]{0,2,1:T(8,128)(2,1)S(1)} %bitcast.307), kind=kOutput, calls=%fused_computation.252 | convolution fusion | flops 402653184 | bytes 14155776 | tf_op jit(solution)/shard_map/vmap(qhd,khd->hqk)/dot_general | solution.py:54
  124.3 6.6 %fusion.150 = (f32[12,512]{1,0:T(8,128)S(1)}, f32[12,512,512]{1,2,0:T(8,128)S(1)}) fusion(bf16[512,12,16]{0,2,1:T(8,128)(2,1)S(1)} %bitcast.348, bf16[512,12,16]{0,2,1:T(8,128)(2,1)S(1)} %bitcast.341, f32[12,512,512]{1,2,0:T(8,128)} %fusion.156, pred[512]{0:T(512)(128)(4,1)S(1)} %copy-done.72), kind=kOutput, calls=%fused_computation.246 | convolution fusion | flops 116385792 | bytes 25584128 | tf_op jit(solution)/shard_map/vmap(qhd,khd->hqk)/dot_general | solution.py:60
  131.0 1.9 fusion.4
  132.8 2.6 copy-done
  135.7 2.5 divide_convert_fusion
  139.4 1.5 copy-done.1
  140.9 2.5 fusion.151
  144.1 1.2 copy.51
  145.3 3.8 convolution_convert_fusion.10
  149.7 4.1 multiply_convert_fusion.3
  163.1 1.2 fusion.70
  164.3 4.3 all-gather.5.cloned.1.call-done
  168.6 8.5 %fusion.141 = (bf16[32,24,3072]{2,1,0:T(8,128)(2,1)}, bf16[32,24,3072]{2,1,0:T(8,128)(2,1)}) fusion(bf16[32,48,3072]{2,1,0:T(8,128)(2,1)} %bitcast.311), kind=kLoop, calls=%fused_computation.237 | loop fusion | bytes 18874368 | tf_op jit(solution)/shard_map/slice | solution.py:381
  177.1 8.5 %reshape.1081 = bf16[3072,768]{1,0:T(8,128)(2,1)} reshape(bf16[32,24,3072]{2,1,0:T(8,128)(2,1)} %get-tuple-element.105) | data formatting | bytes 9437184 | tf_op jit(solution)/shard_map/reshape | solution.py:381
  185.6 19.5 %multiply_convert_fusion = (bf16[512,3072]{1,0:T(8,128)(2,1)S(1)}, f32[512,3072]{1,0:T(8,128)}, f32[512,3072]{1,0:T(8,128)}) fusion(f32[3072]{0:T(1024)S(1)} %copy-done.56, bf16[768,3072]{1,0:T(8,128)(2,1)} %bitcast.324, bf16[1,512,768]{2,1,0:T(8,128)(2,1)} %fusion.70), kind=kOutput, calls=%fused_computation.30 | convolution fusion | flops 2519728128 | bytes 21245952 | tf_op jit(solution)/shard_map/vmap()/dot_general | solution.py:166
  205.1 2.8 fusion.152
  209.1 1.7 fusion.138
  211.0 9.1 %fusion.155 = (f32[3072]{0:T(1024)S(1)}, bf16[512,3072]{1,0:T(8,128)(2,1)}) fusion(f32[512,3072]{1,0:T(8,128)} %get-tuple-element.104, bf16[3072,768]{1,0:T(8,128)(2,1)S(1)} %copy-done.11, bf16[1,512,768]{2,1,0:T(8,128)(2,1)S(1)} %get-tuple-element.112, f32[512,3072]{1,0:T(8,128)} %get-tuple-element.149, f32[3072]{0:T(1024)S(1)} %copy-done.56), kind=kOutput, calls=%fused_computation.251 | convolution fusion | flops 2441081856 | bytes 21258240 | tf_op jit(solution)/shard_map/vmap()/dot_general | solution.py:184
  220.2 5.1 multiply_reduce_fusion.3
  227.4 2.1 fusion.69
  229.5 1.9 convolution_convert_fusion.3
  231.4 4.3 convolution_convert_fusion.1
  236.4 8.5 %reshape.1088 = bf16[32,24,3072]{2,1,0:T(8,128)(2,1)} reshape(bf16[3072,768]{1,0:T(8,128)(2,1)} %convolution_convert_fusion.1) | data formatting | bytes 9437184 | tf_op jit(solution)/shard_map/reshape | solution.py:431
  244.9 4.9 convolution_convert_fusion.2
  249.8 4.0 pad_maximum_fusion
  254.0 7.5 %fusion.63 = bf16[12,64,512]{2,1,0:T(8,128)(2,1)} fusion(bf16[512,12,64]{0,2,1:T(8,128)(2,1)S(1)} %bitcast.305, f32[12,512,512]{1,2,0:T(8,128)} %copy-done, f32[12,512]{1,0:T(8,128)S(1)} %log_add_fusion), kind=kOutput, calls=%fused_computation.106 | convolution fusion | flops 409337856 | bytes 14180352 | tf_op jit(solution)/shard_map/vmap(hqk,qhd->khd)/dot_general | solution.py:109
  261.6 15.7 %subtract_multiply_fusion = f32[12,512,512]{1,2,0:T(8,128)} fusion(f32[12,512,512]{1,2,0:T(8,128)} %copy-done, f32[12,512]{1,0:T(8,128)S(1)} %log_add_fusion, bf16[512,12,64]{0,2,1:T(8,128)(2,1)S(1)} %bitcast.306, bf16[512,12,64]{0,2,1:T(8,128)(2,1)S(1)} %bitcast.301), kind=kOutput, calls=%fused_computation.5 | convolution fusion | flops 821041664 | bytes 26763264 | tf_op jit(solution)/shard_map/vmap()/sub | solution.py:113
  277.3 7.0 %fusion.91 = bf16[12,16,512]{2,1,0:T(8,128)(2,1)} fusion(bf16[512,12,16]{0,2,1:T(8,128)(2,1)S(1)} %bitcast.337, f32[12,512,512]{1,2,0:T(8,128)} %copy-done, f32[12,512]{1,0:T(8,128)S(1)} %log_add_fusion), kind=kOutput, calls=%fused_computation.135 | convolution fusion | flops 107053056 | bytes 13000704 | tf_op jit(solution)/shard_map/vmap(hqk,qhd->khd)/dot_general | solution.py:110
  284.3 19.5 %fusion.28 = bf16[1,12,512,512]{2,3,1,0:T(8,128)(2,1)} fusion(f32[12,512,512]{1,2,0:T(8,128)} %subtract_multiply_fusion, f32[12,512,512]{1,2,0:T(8,128)} %copy-done, f32[12,512]{1,0:T(8,128)S(1)} %log_add_fusion, bf16[512,12,16]{0,2,1:T(8,128)(2,1)S(1)} %bitcast.338, bf16[512,12,16]{0,2,1:T(8,128)(2,1)S(1)} %bitcast.329), kind=kOutput, calls=%fused_computation.51 | convolution fusion | flops 223353344 | bytes 31875072 | tf_op jit(solution)/shard_map/vmap()/sub | solution.py:114
  303.8 5.4 convert_bitcast_fusion
  309.3 4.2 multiply_convert_fusion.1
  313.5 2.0 multiply_convert_fusion.2
  315.9 1.7 fusion.85
  321.5 1.6 copy.67
  323.1 4.4 reshape.1103
  328.0 1.3 convolution_convert_fusion.7
  330.4 1.7 fusion.133
  332.4 1.8 concatenate.73
  334.4 2.1 copy.81
  336.5 2.0 fusion.26
  338.5 2.4 pad_maximum_fusion.2
  340.9 6.7 %copy.63 = bf16[768,3072]{1,0:T(8,128)(2,1)} copy(bf16[768,3072]{0,1:T(8,128)(2,1)} %pad_maximum_fusion.2) | data formatting | bytes 9437184 | tf_op jit(solution)/shard_map/concatenate | solution.py:488
  347.7 6.1 pad_maximum_fusion.1
  354.4 1.2 copy.58
  355.6 1.2 copy.57
  357.9 2.1 fusion.75
  360.0 6.0 bitcast_add_fusion
  366.0 101.4 %reduce-scatter.3.cloned.1.call-done = bf16[32,3072]{1,0:T(8,128)(2,1)} async-done(((bf16[1024,3072]{1,0:T(8,128)(2,1)}), bf16[32,3072]{1,0:T(8,128)(2,1)}) %reduce-scatter.3.cloned.1.call-update) | async-done | bytes 196624 | tf_op jit(solution)/shard_map/reduce_scatter | solution.py:407
  472.9 1.6 slice.272
  474.6 133.8 %reduce-scatter.5.cloned.1.call-done = bf16[48,3072]{1,0:T(8,128)(2,1)} async-done(((bf16[1536,3072]{1,0:T(8,128)(2,1)}), bf16[48,3072]{1,0:T(8,128)(2,1)}) %reduce-scatter.5.cloned.1.call-update) | async-done | bytes 294928 | tf_op jit(solution)/shard_map/reduce_scatter | solution.py:438
  608.4 1.7 fusion.146
  (291 shorter events, 43.9 us)
Async XLA Ops:
  7.2 77.9 %all-gather.3.cloned.1.call-start = ((), (), s32[]{:S(2)}) async-start(), calls=%async_computation.2 | async-start | bytes 6488064 | tf_op jit(solution)/shard_map/all_gather | solution.py:370
  12.9 155.7 %all-gather.5.cloned.1.call-start = ((), (), s32[]{:S(2)}) async-start(), calls=%async_computation.3 | async-start | bytes 9732096 | tf_op jit(solution)/shard_map/all_gather | solution.py:379
  15.6 451.8 %reduce-scatter.3.cloned.1.call-start = ((), (), s32[]{:S(2)}) async-start(), calls=%async_computation.4 | async-start | bytes 6488064 | tf_op jit(solution)/shard_map/reduce_scatter | solution.py:407
  110.3 39.2 %copy-start.58 = (f32[192]{0:T(256)}, f32[192]{0:T(256)S(1)}, u32[]{:S(2)}) copy-start(f32[192]{0:T(256)S(1)} %get-tuple-element.138) | copy-start | bytes 2308
  113.2 11.1 %copy-start.16 = (bf16[1,512,1,192]{1,3,2,0:T(8,128)(2,1)}, bf16[1,512,1,192]{1,3,2,0:T(8,128)(2,1)S(1)}, u32[]{:S(2)}) copy-start(bf16[1,512,1,192]{1,3,2,0:T(8,128)(2,1)S(1)} %get-tuple-element.118) | copy-start | bytes 589828
  113.2 11.1 %copy-start.23 = (bf16[1,512,1,192]{1,3,2,0:T(8,128)(2,1)}, bf16[1,512,1,192]{1,3,2,0:T(8,128)(2,1)S(1)}, u32[]{:S(2)}) copy-start(bf16[1,512,1,192]{1,3,2,0:T(8,128)(2,1)S(1)} %get-tuple-element.119) | copy-start | bytes 589828
  117.9 6.4 %copy-start.3 = (bf16[1,512,1,768]{1,3,2,0:T(8,128)(2,1)}, bf16[1,512,1,768]{1,3,2,0:T(8,128)(2,1)S(1)}, u32[]{:S(2)}) copy-start(bf16[1,512,1,768]{1,3,2,0:T(8,128)(2,1)S(1)} %get-tuple-element.107) | copy-start | bytes 2359300
  117.9 6.4 %copy-start.7 = (bf16[1,512,1,768]{1,3,2,0:T(8,128)(2,1)}, bf16[1,512,1,768]{1,3,2,0:T(8,128)(2,1)S(1)}, u32[]{:S(2)}) copy-start(bf16[1,512,1,768]{1,3,2,0:T(8,128)(2,1)S(1)} %get-tuple-element.108) | copy-start | bytes 2359300
  117.9 6.4 %copy-start.72 = (pred[512]{0:T(512)(128)(4,1)S(1)}, pred[512]{0:T(512)(128)(4,1)}, u32[]{:S(2)}) copy-start(pred[512]{0:T(512)(128)(4,1)} %get-tuple-element.161) | copy-start | bytes 1540
  130.9 4.5 copy-start
  130.9 4.7 copy-start.39
  135.7 2.5 copy-start.41
  138.2 2.7 copy-start.1
  138.2 2.7 copy-start.70
  138.2 2.7 copy-start.73
  140.9 2.8 copy-start.20
  140.9 2.9 copy-start.47
  143.7 5.3 copy-start.52
  143.8 5.3 copy-start.50
  145.3 3.8 copy-start.30
  145.3 3.8 copy-start.43
  145.3 4.3 copy-start.28
  145.3 4.4 copy-start.71
  149.1 4.8 copy-start.18
  149.6 4.3 copy-start.44
  149.7 4.2 copy-start.25
  149.7 4.2 copy-start.59
  149.7 4.2 copy-start.61
  149.7 4.8 copy-start.34
  149.7 4.8 copy-start.60
  149.7 5.6 copy-start.62
  153.9 3.8 copy-start.12
  158.8 4.3 copy-start.40
  158.8 4.3 copy-start.42
  159.3 3.8 copy-start.48
  159.3 3.8 copy-start.51
  177.1 8.5 %copy-start.56 = (f32[3072]{0:T(1024)S(1)}, f32[3072]{0:T(1024)}, u32[]{:S(2)}) copy-start(f32[3072]{0:T(1024)} %slice.252) | copy-start | bytes 36868
  185.5 19.5 %copy-start.11 = (bf16[3072,768]{1,0:T(8,128)(2,1)S(1)}, bf16[3072,768]{1,0:T(8,128)(2,1)}, u32[]{:S(2)}) copy-start(bf16[3072,768]{1,0:T(8,128)(2,1)} %reshape.1081) | copy-start | bytes 14155780
  185.5 19.5 %copy-start.69 = (f32[768]{0:T(1024)S(1)}, f32[768]{0:T(1024)}, u32[]{:S(2)}) copy-start(f32[768]{0:T(1024)} %get-tuple-element.129) | copy-start | bytes 9220
  205.1 3.1 copy-start.15
  205.1 3.1 copy-start.49
  209.1 11.1 %slice-start.2 = ((s8[4718592]{0:T(1024)(128)(4,1)}), s8[4194304]{0:T(1024)(128)(4,1)S(1)}, s32[]{:S(2)}) async-start(s8[4718592]{0:T(1024)(128)(4,1)} %bitcast.325), calls=%async_computation.8 | async-start | bytes 8388608
  211.0 9.1 %slice-start.3 = ((s8[4718592]{0:T(1024)(128)(4,1)}), s8[524288]{0:T(1024)(128)(4,1)S(1)}, s32[]{:S(2)}) async-start(s8[4718592]{0:T(1024)(128)(4,1)} %bitcast.325), calls=%async_computation.9 | async-start | bytes 1048576
  220.2 5.1 copy-start.53
  226.2 3.3 copy-start.21
  236.4 8.5 %copy-start.33 = (bf16[768,512]{1,0:T(8,128)(2,1)S(1)}, bf16[768,512]{1,0:T(8,128)(2,1)}, u32[]{:S(2)}) copy-start(bf16[768,512]{1,0:T(8,128)(2,1)} %copy.51) | copy-start | bytes 2359300
  244.9 4.9 copy-start.2
  309.3 4.2 copy-start.4
  309.3 6.2 %slice-start = ((s8[6291456]{0:T(1024)(128)(4,1)}), s8[2097152]{0:T(1024)(128)(4,1)S(1)}, s32[]{:S(2)}) async-start(s8[6291456]{0:T(1024)(128)(4,1)} %bitcast.295), calls=%async_computation.6 | async-start | bytes 4194304
  313.5 2.4 slice-start.1
  313.5 2.5 copy-start.24
  317.7 10.3 %copy-start.31 = (bf16[12,16,512]{2,1,0:T(8,128)(2,1)}, bf16[12,16,512]{2,1,0:T(8,128)(2,1)S(1)}, u32[]{:S(2)}) copy-start(bf16[12,16,512]{2,1,0:T(8,128)(2,1)S(1)} %fusion.85) | copy-start | bytes 589828
  318.7 2.3 copy-start.45
  320.8 6.7 %copy-start.37 = (bf16[12,16,512]{2,1,0:T(8,128)(2,1)S(1)}, bf16[12,16,512]{2,1,0:T(8,128)(2,1)}, u32[]{:S(2)}) copy-start(bf16[12,16,512]{2,1,0:T(8,128)(2,1)} %fusion.91) | copy-start | bytes 589828
  321.1 6.6 %copy-start.55 = (bf16[1,768]{1,0:T(2,128)(2,1)S(1)}, bf16[1,768]{1,0:T(2,128)(2,1)}, u32[]{:S(2)}) copy-start(bf16[1,768]{1,0:T(2,128)(2,1)} %reduce_sum.440) | copy-start | bytes 4612
  323.1 7.3 %copy-start.5 = (bf16[12,64,512]{2,1,0:T(8,128)(2,1)S(1)}, bf16[12,64,512]{2,1,0:T(8,128)(2,1)}, u32[]{:S(2)}) copy-start(bf16[12,64,512]{2,1,0:T(8,128)(2,1)} %multiply_convert_fusion.2) | copy-start | bytes 2359300
  323.1 7.3 %copy-start.6 = (bf16[12,64,512]{2,1,0:T(8,128)(2,1)S(1)}, bf16[12,64,512]{2,1,0:T(8,128)(2,1)}, u32[]{:S(2)}) copy-start(bf16[12,64,512]{2,1,0:T(8,128)(2,1)} %fusion.63) | copy-start | bytes 2359300
  323.1 7.3 %copy-start.8 = (bf16[12,64,512]{2,1,0:T(8,128)(2,1)S(1)}, bf16[12,64,512]{2,1,0:T(8,128)(2,1)}, u32[]{:S(2)}) copy-start(bf16[12,64,512]{2,1,0:T(8,128)(2,1)} %multiply_convert_fusion.1) | copy-start | bytes 2359300
  329.2 2.9 copy-start.57
  353.8 254.6 %reduce-scatter.5.cloned.1.call-start = ((), (), s32[]{:S(2)}) async-start(), calls=%async_computation.5 | async-start | bytes 9732096 | tf_op jit(solution)/shard_map/reduce_scatter | solution.py:438
  354.4 3.5 copy-start.27
  354.4 3.5 copy-start.32
  354.4 3.5 copy-start.38
  356.7 3.2 copy-start.10
  (19 other events, 26.9 us)
Sparse Core Ops, SparseCore 0:
  13.0 71.9 all-gather.2
  88.5 80.0 all-gather.4
  353.9 113.4 reduce-scatter.2
  473.2 135.1 reduce-scatter.4

commit v6 on v5

--- a/solution.py
+++ b/solution.py
@@ -209,17 +209,55 @@
     return (grad_first, grad_ctx, operands, vector_sums)
 
 
+def branch_back_a(packed, second, width, kept_rows, grad_out):
+    first_res, inner, second_res = kept_rows
+    pieces = vector_parts(packed.astype(jnp.float32), width)
+    hidden = normalize(first_res, pieces[3], pieces[4])
+    _, second_pull = jax.vjp(normalize, second_res, pieces[6], pieces[7])
+    grad_second, late_scale, late_shift = second_pull(grad_out)
+    round_second = grad_second.astype(jnp.bfloat16)
+    activated, gelu_pull = jax.vjp(gelu_exact, inner)
+    (grad_inner,) = gelu_pull(jnp.dot(round_second, second.T, preferred_element_type=jnp.float32))
+    round_inner = grad_inner.astype(jnp.bfloat16)
+    return (
+        grad_second,
+        round_second,
+        grad_inner,
+        round_inner,
+        hidden.astype(jnp.bfloat16),
+        activated.astype(jnp.bfloat16),
+        late_scale,
+        late_shift,
+    )
+
+
+def branch_back_b(attn, packed, first, width, columns, kept_rows, part_a):
+    first_res, _, _ = kept_rows
+    grad_second, round_second, grad_inner, round_inner, hidden_low, active_low, late_scale, late_shift = part_a
+    pieces = vector_parts(packed.astype(jnp.float32), width)
+    _, first_pull = jax.vjp(normalize, first_res, pieces[3], pieces[4])
+    grad_hidden = grad_second + jnp.dot(round_inner, first.T, preferred_element_type=jnp.float32)
+    grad_first, early_scale, early_shift = first_pull(grad_hidden)
+    round_first = grad_first.astype(jnp.bfloat16)
+    out_block = block_of(attn, 3, width, columns)
+    grad_ctx = jnp.dot(round_first, out_block.T, preferred_element_type=jnp.float32).astype(
+        jnp.bfloat16
+    )
+    operands = (hidden_low, active_low, round_first, round_second, round_inner)
+    vector_sums = (
+        jnp.sum(grad_first, 0),
+        early_scale,
+        early_shift,
+        jnp.sum(grad_second, 0),
+        late_scale,
+        late_shift,
+        jnp.sum(grad_inner, 0),
+    )
+    return (grad_first, grad_ctx, operands, vector_sums)
+
+
 def page_forward(text_rows, layout_rows, length, weights):
-    (
-        text_attn,
-        text_first,
-        text_second,
-        text_packed,
-        layout_attn,
-        layout_first,
-        layout_second,
-        layout_packed,
-    ) = weights
+    (text_attn, text_first, text_second, text_packed, layout_attn, _, _, layout_packed) = weights
     width = text_rows.shape[1]
     narrow = layout_rows.shape[1]
     valid = jnp.arange(text_rows.shape[0], dtype=jnp.int32) < length
@@ -229,6 +267,40 @@
     text_out, text_kept = branch_forward(
         text_rows, text_ctx, text_attn, text_packed, text_first, text_second, width, True
     )
+    mask = valid[:, None].astype(jnp.float32)
+    kept_page = (text_three, layout_three, text_ctx, layout_ctx, log_total, text_kept)
+    return ((text_out * mask).astype(jnp.bfloat16), kept_page)
+
+
+def page_back_ffn(length, kept_page, text_cot, weights):
+    text_attn, _, text_second, text_packed = weights[:4]
+    text_kept = kept_page[5]
+    width = text_attn.shape[0]
+    slots = text_cot.shape[0]
+    valid = jnp.arange(slots, dtype=jnp.int32) < length
+    mask = valid[:, None].astype(jnp.float32)
+    return branch_back_a(
+        text_packed, text_second, width, text_kept, text_cot.astype(jnp.float32) * mask
+    )
+
+
+def page_back_attn(text_rows, layout_rows, length, kept_page, text_a, layout_cot, weights):
+    (
+        text_attn,
+        text_first,
+        _,
+        text_packed,
+        layout_attn,
+        layout_first,
+        layout_second,
+        layout_packed,
+    ) = weights
+    text_three, layout_three, _, layout_ctx, log_total, text_kept = kept_page
+    width = text_rows.shape[1]
+    narrow = layout_rows.shape[1]
+    slots = text_rows.shape[0]
+    valid = jnp.arange(slots, dtype=jnp.int32) < length
+    mask = valid[:, None].astype(jnp.float32)
     layout_out, layout_kept = branch_forward(
         layout_rows,
         layout_ctx,
@@ -239,39 +311,6 @@
         narrow,
         False,
     )
-    mask = valid[:, None].astype(jnp.float32)
-    outputs = ((text_out * mask).astype(jnp.bfloat16), (layout_out * mask).astype(jnp.bfloat16))
-    kept_page = (text_three, layout_three, text_ctx, layout_ctx, log_total, text_kept, layout_kept)
-    return (outputs, kept_page)
-
-
-def page_back_ffn(length, kept_page, text_cot, layout_cot, weights):
-    (
-        text_attn,
-        text_first,
-        text_second,
-        text_packed,
-        layout_attn,
-        layout_first,
-        layout_second,
-        layout_packed,
-    ) = weights
-    _, _, _, _, _, text_kept, layout_kept = kept_page
-    width = text_attn.shape[0]
-    narrow = layout_attn.shape[1]
-    slots = text_cot.shape[0]
-    valid = jnp.arange(slots, dtype=jnp.int32) < length
-    mask = valid[:, None].astype(jnp.float32)
-    text_back = branch_backward(
-        text_attn,
-        text_packed,
-        text_first,
-        text_second,
-        width,
-        True,
-        text_kept,
-        text_cot.astype(jnp.float32) * mask,
-    )
     layout_back = branch_backward(
         layout_attn,
         layout_packed,
@@ -282,17 +321,8 @@
         layout_kept,
         layout_cot.astype(jnp.float32) * mask,
     )
-    return (text_back, layout_back)
-
-
-def page_back_attn(text_rows, layout_rows, length, kept_page, text_back, layout_back, weights):
-    (text_attn, _, _, _, layout_attn, _, _, _) = weights
-    text_three, layout_three, _, layout_ctx, log_total, _, _ = kept_page
-    width = text_rows.shape[1]
-    narrow = layout_rows.shape[1]
-    slots = text_rows.shape[0]
-    valid = jnp.arange(slots, dtype=jnp.int32) < length
-    text_res_grad, text_ctx_grad, _, text_sums = text_back
+    text_back = branch_back_b(text_attn, text_packed, text_first, width, True, text_kept, text_a)
+    text_res_grad, text_ctx_grad, text_ops, text_sums = text_back
     layout_res_grad, layout_ctx_grad, layout_ops, layout_sums = layout_back
     text_three_grad, layout_three_grad = attend_back(
         text_three, layout_three, valid, log_total, text_ctx_grad, layout_ctx_grad
@@ -324,7 +354,9 @@
         layout_second_grad,
         layout_vec_grad,
     )
-    return ((text_in_grad, layout_in_grad), small_terms, text_rounded.reshape(slots, 3 * width))
+    layout_low = (layout_out * mask).astype(jnp.bfloat16)
+    grads = (text_in_grad, layout_in_grad)
+    return (layout_low, grads, small_terms, text_rounded.reshape(slots, 3 * width), text_ops[2])
 
 
 def flat_rows(values):
@@ -460,24 +492,23 @@
     )
 
     page_weights = (None,) * len(weights)
-    outputs, kept_all = jax.vmap(page_forward, in_axes=(0, 0, 0, page_weights))(
+    out_text, kept_all = jax.vmap(page_forward, in_axes=(0, 0, 0, page_weights))(
         text_in, layout_in, lengths, weights
     )
-    out_text, out_layout = outputs
-    text_back, layout_back = jax.vmap(page_back_ffn, in_axes=(0, 0, 0, 0, page_weights))(
-        lengths, kept_all, cot_text, cot_layout, weights
-    )
-    text_hidden, text_active, text_first_low, text_second_low, text_inner_low = text_back[2]
+    text_a = jax.vmap(page_back_ffn, in_axes=(0, 0, 0, page_weights))(
+        lengths, kept_all, cot_text, weights
+    )
+    round_second, round_inner, text_hidden, text_active = text_a[1], text_a[3], text_a[4], text_a[5]
     early = (
-        jnp.einsum("sd,sf->df", flat_rows(text_hidden), flat_rows(text_inner_low), preferred_element_type=jnp.float32),
-        jnp.einsum("sf,sd->fd", flat_rows(text_active), flat_rows(text_second_low), preferred_element_type=jnp.float32),
+        jnp.einsum("sd,sf->df", flat_rows(text_hidden), flat_rows(round_inner), preferred_element_type=jnp.float32),
+        jnp.einsum("sf,sd->fd", flat_rows(text_active), flat_rows(round_second), preferred_element_type=jnp.float32),
     )
     packed = pack_early(count, *early)
-    packed, text_back, layout_back = lax.optimization_barrier((packed, text_back, layout_back))
+    packed, text_a, kept_all = lax.optimization_barrier((packed, text_a, kept_all))
     grad_first, grad_second = scatter_early(count, packed, early[1].shape)
-    (text_grad, layout_grad), small_terms, text_rounded = jax.vmap(
+    out_layout, (text_grad, layout_grad), small_terms, text_rounded, text_first_low = jax.vmap(
         page_back_attn, in_axes=(0, 0, 0, 0, 0, 0, page_weights)
-    )(text_in, layout_in, lengths, kept_all, text_back, layout_back, weights)
+    )(text_in, layout_in, lengths, kept_all, text_a, cot_layout, weights)
     totals = tuple(jnp.sum(term, 0) for term in small_terms)
     three_part = jnp.einsum(
         "sd,se->de", flat_rows(text_in), flat_rows(text_rounded), preferred_element_type=jnp.float32

time: 624 us -> 659 us (1.056)
  waiting for transfers between devices: 308 us -> 325 us
  other arithmetic: 41.9 us -> 54.5 us
    dot_general x2 -> x5, matrix products: 9.18 us -> 27.1 us  [the longest x1 10.3 us: branch_back_a(): jnp.dot(round_second, second.T, preferred_element_type=jnp.float32)]
    all_gather x1, waiting for transfers between devices: 4.27 us -> 21.1 us  [gather_weights(): lax.all_gather(second, AXES, axis=0, tiled=True)]
    dot_general x2 -> x1, matrix products: 9.92 us -> 2.57 us  [branch_backward(): jnp.dot(round_second, second.T, preferred_element_type=jnp.float32)]
    convert_element_type x2 -> x3, other arithmetic: 0.1 us -> 7.44 us  [the longest x1 5.12 us: branch_backward(): round_inner = grad_inner.astype(jnp.bfloat16)]
    unnamed x172 -> x198, local copies, waits for them, and re-layouts: 12.2 us -> 15.3 us
  transfers between devices with their start and end apart: 4 -> 4, of which waited for: 4 -> 4; matrix products, arithmetic and copies ran while one was open for 15% -> 12% of each run, Pallas kernels for 0% -> 0%
where the time goes in v6:
time: 659 us; the launch traced here: 653 us
  waiting for transfers between devices  325 us (49%)
  matrix products  153 us (23%)
  local copies, waits for them, and re-layouts  104 us (16%)
  other arithmetic  54.5 us (8%)
  between operations  16.1 us (2%)
    reduce_scatter x1, waiting for transfers between devices, scatter_early(): lax.psum_scatter(packed, AXES, scatter_dimension=0, tiled=True)  135 us
    reduce_scatter x1, waiting for transfers between devices, scatter_late(): lax.psum_scatter(packed.reshape(-1, width).astype(jnp.bfloat16), AXES, sc...  102 us
    all_gather x1, waiting for transfers between devices, gather_weights(): first_all = lax.all_gather(first, AXES, axis=0, tiled=True)  67.5 us
    dot_general x2, matrix products, branch_forward(): jnp.dot(hidden.astype(jnp.bfloat16), first, preferred_element_type=jnp.fl...  22.6 us
    all_gather x1, waiting for transfers between devices, gather_weights(): lax.all_gather(second, AXES, axis=0, tiled=True)  21.1 us
    sub x1, matrix products, attend_back(): layout_dp - jnp.sum(probs * layout_dp, -1, keepdims=True)  17.1 us
    unnamed x198, local copies, waits for them, and re-layouts  15.3 us
    sub x1, matrix products, attend_back(): text_ds = probs * (text_dp - jnp.sum(probs * text_dp, -1, keepdims=True))  14.2 us
  transfers between devices with their start and end apart: 4, of which 4 were waited for; matrix products, arithmetic and copies ran while one was open for 12% of the time, Pallas kernels for 0%

profile of v6, /device:TPU:0, one launch (start us, length us, event | category | flops | bytes accessed | tf_op | source)
XLA Modules:
  0.0 653.3 jit_solution(16671823026774319688)
XLA Ops:
  9.8 1.5 concatenate.65
  11.3 1.6 pad_maximum_fusion.9
  14.0 1.6 pad_maximum_fusion.6
  17.5 67.5 %all-gather.3.cloned.1.call-done = bf16[1024,3072]{1,0:T(8,128)(2,1)} async-done(((bf16[32,3072]{1,0:T(8,128)(2,1)}), bf16[1024,3072]{1,0:T(8,128)(2,1)}) %all-gather.3.cloned.1.call-update) | async-done | bytes 6291472 | tf_op jit(solution)/shard_map/all_gather | solution.py:402
  85.1 1.5 slice.253
  86.6 4.8 slice.251
  98.7 2.5 reshape.1171
  101.3 1.8 copy.51
  103.1 2.2 slice.252
  105.3 3.7 copy.46
  112.6 4.3 fusion.34
  118.4 6.4 fusion.180
  124.8 6.6 %fusion.175 = (f32[12,512]{1,0:T(8,128)S(1)}, f32[12,512,512]{1,2,0:T(8,128)S(1)}) fusion(bf16[512,12,16]{0,2,1:T(8,128)(2,1)S(1)} %bitcast.432, bf16[512,12,16]{0,2,1:T(8,128)(2,1)S(1)} %bitcast.431, f32[12,512,512]{1,2,0:T(8,128)} %fusion.180, pred[512]{0:T(512)(128)(4,1)S(1)} %copy-done.67), kind=kOutput, calls=%fused_computation.275 | convolution fusion | flops 116385792 | bytes 25584128 | tf_op jit(solution)/shard_map/vmap(qhd,khd->hqk)/dot_general | solution.py:60
  131.4 1.8 fusion.4
  133.1 2.9 divide_convert_fusion
  137.2 1.5 copy-done.1
  138.7 2.5 fusion.176
  143.7 3.7 convolution_convert_fusion.10
  147.4 21.1 %all-gather.5.cloned.1.call-done = bf16[1536,3072]{1,0:T(8,128)(2,1)} async-done(((bf16[48,3072]{1,0:T(8,128)(2,1)}), bf16[1536,3072]{1,0:T(8,128)(2,1)}) %all-gather.5.cloned.1.call-update) | async-done | bytes 9437200 | tf_op jit(solution)/shard_map/all_gather | solution.py:411
  168.5 8.2 %fusion.165 = (bf16[32,24,3072]{2,1,0:T(8,128)(2,1)}, bf16[32,24,3072]{2,1,0:T(8,128)(2,1)}) fusion(bf16[32,48,3072]{2,1,0:T(8,128)(2,1)} %bitcast.387), kind=kLoop, calls=%fused_computation.265 | loop fusion | bytes 18874368 | tf_op jit(solution)/shard_map/slice | solution.py:413
  176.7 8.5 %reshape.1165 = bf16[3072,768]{1,0:T(8,128)(2,1)} reshape(bf16[32,24,3072]{2,1,0:T(8,128)(2,1)} %get-tuple-element.82) | data formatting | bytes 9437184 | tf_op jit(solution)/shard_map/reshape | solution.py:413
  185.2 18.9 %multiply_convert_fusion = (bf16[512,3072]{1,0:T(8,128)(2,1)S(1)}, f32[512,3072]{1,0:T(8,128)}, f32[512,3072]{1,0:T(8,128)}) fusion(f32[3072]{0:T(1024)S(1)} %copy-done.59, bf16[768,3072]{1,0:T(8,128)(2,1)} %bitcast.402, bf16[1,512,768]{2,1,0:T(8,128)(2,1)S(1)} %fusion.93), kind=kOutput, calls=%fused_computation.27 | convolution fusion | flops 2519728128 | bytes 21245952 | tf_op jit(solution)/shard_map/vmap()/dot_general | solution.py:166
  204.1 2.8 fusion.177
  210.0 1.7 fusion.163
  212.9 4.4 convolution_convert_fusion.1
  217.2 8.5 %reshape.1167 = bf16[32,24,3072]{2,1,0:T(8,128)(2,1)} reshape(bf16[3072,768]{1,0:T(8,128)(2,1)} %convolution_convert_fusion.1) | data formatting | bytes 9437184 | tf_op jit(solution)/shard_map/reshape | solution.py:463
  225.7 10.3 %multiply_add_fusion = f32[512,3072]{1,0:T(8,128)S(1)} fusion(f32[512,3072]{1,0:T(8,128)} %get-tuple-element.81, f32[512,3072]{1,0:T(8,128)} %get-tuple-element.126, f32[3072]{0:T(1024)S(1)} %copy-done.59, bf16[3072,768]{1,0:T(8,128)(2,1)} %reshape.1165, bf16[1,512,768]{2,1,0:T(8,128)(2,1)} %copy-done.35), kind=kOutput, calls=%fused_computation.26 | convolution fusion | flops 2437939200 | bytes 24391680 | tf_op jit(solution)/shard_map/vmap()/dot_general | solution.py:220
  236.0 2.1 convert_bitcast_fusion.1
  238.1 2.6 copy-done.3
  240.7 2.8 convolution_convert_fusion.2
  243.6 4.1 pad_maximum_fusion
  248.9 6.9 %multiply_reduce_fusion.2 = (bf16[768]{0:T(1024)(128)(2,1)}, f32[512]{0:T(512)S(1)}, bf16[768]{0:T(1024)(128)(2,1)}, f32[1,512,768]{2,1,0:T(8,128)S(1)}) fusion(f32[1,512,768]{2,1,0:T(8,128)S(1)} %get-tuple-element.29, f32[512]{0:T(512)S(1)} %fusion.147, f32[512]{0:T(512)S(1)} %broadcast_multiply_fusion.2, f32[768]{0:T(1024)S(1)} %copy-done.45, ...), kind=kOutput, calls=%fused_computation.99 | convolution fusion | flops 2419456000 | bytes 12595200 | tf_op jit(solution)/shard_map/vmap()/dot_general | solution.py:239
  256.5 2.7 convolution_convert_fusion.4
  260.6 3.7 multiply_convert_fusion.3
  269.0 2.6 fusion.156
  275.7 3.2 fusion.166
  278.9 1.8 fusion.181
  280.8 4.2 subtract_exponential_fusion
  285.0 3.0 fusion.109
  288.0 1.6 copy-done
  289.6 3.0 fusion.84
  292.6 14.2 %subtract_multiply_fusion = f32[12,512,512]{1,2,0:T(8,128)} fusion(f32[12,512,512]{1,2,0:T(8,128)} %copy-done, bf16[512,12,64]{0,2,1:T(8,128)(2,1)S(1)} %bitcast.382, bf16[512,12,64]{0,2,1:T(8,128)(2,1)S(1)} %bitcast.390), kind=kOutput, calls=%fused_computation.5 | convolution fusion | flops 814750208 | bytes 26738688 | tf_op jit(solution)/shard_map/vmap()/sub | solution.py:113
  306.8 8.2 %convert_bitcast_fusion = bf16[1,12,512,512]{2,3,1,0:T(8,128)(2,1)} fusion(f32[12,512,512]{1,2,0:T(8,128)} %subtract_multiply_fusion), kind=kLoop, calls=%fused_computation.25 | loop fusion | flops 3145728 | bytes 18874368 | tf_op jit(solution)/shard_map/vmap()/convert_element_type | solution.py:116
  315.0 17.1 %fusion.31 = bf16[1,12,512,512]{2,3,1,0:T(8,128)(2,1)} fusion(f32[12,512,512]{1,2,0:T(8,128)} %subtract_multiply_fusion, f32[12,512,512]{1,2,0:T(8,128)} %copy-done, bf16[512,12,16]{0,2,1:T(8,128)(2,1)S(1)} %bitcast.412, bf16[512,12,16]{0,2,1:T(8,128)(2,1)S(1)} %bitcast.422), kind=kOutput, calls=%fused_computation.54 | convolution fusion | flops 217061888 | bytes 31850496 | tf_op jit(solution)/shard_map/vmap()/sub | solution.py:114
  332.1 5.8 multiply_convert_fusion.1
  339.5 1.7 fusion.103
  342.2 3.2 reduce_sum.441
  345.5 3.1 convolution_convert_fusion.3
  349.9 5.1 fusion.48
  357.1 2.0 copy.67
  359.2 3.7 reshape.1193
  363.3 1.4 convolution_convert_fusion.7
  365.9 1.7 fusion.157
  368.0 1.8 concatenate.73
  370.0 2.0 copy.81
  372.0 2.0 fusion.23
  374.0 2.4 pad_maximum_fusion.2
  376.4 6.7 %copy.63 = bf16[768,3072]{1,0:T(8,128)(2,1)} copy(bf16[768,3072]{0,1:T(8,128)(2,1)} %pad_maximum_fusion.2) | data formatting | bytes 9437184 | tf_op jit(solution)/shard_map/concatenate | solution.py:519
  383.2 6.1 pad_maximum_fusion.1
  393.5 2.2 fusion.92
  395.7 5.5 bitcast_add_fusion
  401.3 101.8 %reduce-scatter.3.cloned.1.call-done = bf16[32,3072]{1,0:T(8,128)(2,1)} async-done(((bf16[1024,3072]{1,0:T(8,128)(2,1)}), bf16[32,3072]{1,0:T(8,128)(2,1)}) %reduce-scatter.3.cloned.1.call-update) | async-done | bytes 196624 | tf_op jit(solution)/shard_map/reduce_scatter | solution.py:439
  509.3 134.6 %reduce-scatter.5.cloned.1.call-done = bf16[48,3072]{1,0:T(8,128)(2,1)} async-done(((bf16[1536,3072]{1,0:T(8,128)(2,1)}), bf16[48,3072]{1,0:T(8,128)(2,1)}) %reduce-scatter.5.cloned.1.call-update) | async-done | bytes 294928 | tf_op jit(solution)/shard_map/reduce_scatter | solution.py:470
  643.9 1.7 fusion.171
  (321 shorter events, 56.0 us)
Async XLA Ops:
  7.2 77.9 %all-gather.3.cloned.1.call-start = ((), (), s32[]{:S(2)}) async-start(), calls=%async_computation.2 | async-start | bytes 6488064 | tf_op jit(solution)/shard_map/all_gather | solution.py:402
  12.9 155.6 %all-gather.5.cloned.1.call-start = ((), (), s32[]{:S(2)}) async-start(), calls=%async_computation.3 | async-start | bytes 9732096 | tf_op jit(solution)/shard_map/all_gather | solution.py:411
  15.6 487.4 %reduce-scatter.3.cloned.1.call-start = ((), (), s32[]{:S(2)}) async-start(), calls=%async_computation.4 | async-start | bytes 6488064 | tf_op jit(solution)/shard_map/reduce_scatter | solution.py:439
  94.5 47.0 %copy-start.44 = (f32[768]{0:T(1024)}, f32[768]{0:T(1024)S(1)}, u32[]{:S(2)}) copy-start(f32[768]{0:T(1024)S(1)} %get-tuple-element.108) | copy-start | bytes 9220
  109.0 3.6 copy-start.86
  118.4 6.4 copy-start.67
  136.0 2.7 copy-start.1
  136.0 2.6 copy-start.74
  138.7 2.5 copy-start.19
  176.7 8.5 %copy-start.59 = (f32[3072]{0:T(1024)S(1)}, f32[3072]{0:T(1024)}, u32[]{:S(2)}) copy-start(f32[3072]{0:T(1024)} %slice.271) | copy-start | bytes 36868
  185.2 18.9 %copy-start.15 = (bf16[3072,768]{1,0:T(8,128)(2,1)S(1)}, bf16[3072,768]{1,0:T(8,128)(2,1)}, u32[]{:S(2)}) copy-start(bf16[3072,768]{1,0:T(8,128)(2,1)} %reshape.1165) | copy-start | bytes 14155780
  185.2 18.9 %copy-start.73 = (f32[768]{0:T(1024)S(1)}, f32[768]{0:T(1024)}, u32[]{:S(2)}) copy-start(f32[768]{0:T(1024)} %get-tuple-element.106) | copy-start | bytes 9220
  207.3 2.8 copy-start.58
  236.0 4.7 copy-start.3
  236.0 4.7 copy-start.36
  236.0 7.5 %slice-start.2 = ((s8[4718592]{0:T(1024)(128)(4,1)}), s8[4194304]{0:T(1024)(128)(4,1)S(1)}, s32[]{:S(2)}) async-start(s8[4718592]{0:T(1024)(128)(4,1)} %bitcast.376), calls=%async_computation.8 | async-start | bytes 8388608
  240.7 2.9 slice-start.3
  256.4 2.7 copy-start.10
  256.4 2.7 copy-start.63
  260.4 12.3 %copy-start.48 = (f32[512]{0:T(512)}, f32[512]{0:T(512)S(1)}, u32[]{:S(2)}) copy-start(f32[512]{0:T(512)S(1)} %broadcast_multiply_fusion.1) | copy-start | bytes 6148
  260.5 12.2 %copy-start.54 = (f32[512]{0:T(512)}, f32[512]{0:T(512)S(1)}, u32[]{:S(2)}) copy-start(f32[512]{0:T(512)S(1)} %fusion.145) | copy-start | bytes 6148
  260.6 3.8 copy-start.27
  260.6 3.8 copy-start.71
  264.3 4.7 copy-start.28
  264.4 1.9 copy-start.72
  272.9 2.0 copy-start.52
  272.9 2.0 copy-start.22
  275.7 5.1 copy-start.17
  275.7 5.1 copy-start.24
  278.9 1.9 copy-start.68
  285.0 4.6 copy-start
  289.6 3.0 copy-start.6
  306.8 8.2 %copy-start.23 = (bf16[1,512,1,192]{1,3,2,0:T(8,128)(2,1)S(1)}, bf16[1,512,1,192]{1,3,2,0:T(8,128)(2,1)}, u32[]{:S(2)}) copy-start(bf16[1,512,1,192]{1,3,2,0:T(8,128)(2,1)} %get-tuple-element.93) | copy-start | bytes 589828
  315.0 17.1 %copy-start.8 = (bf16[1,512,1,768]{1,3,2,0:T(8,128)(2,1)S(1)}, bf16[1,512,1,768]{1,3,2,0:T(8,128)(2,1)}, u32[]{:S(2)}) copy-start(bf16[1,512,1,768]{1,3,2,0:T(8,128)(2,1)} %copy-done.7) | copy-start | bytes 2359300
  332.1 5.8 copy-start.2
  332.1 7.0 %slice-start = ((s8[6291456]{0:T(1024)(128)(4,1)}), s8[4194304]{0:T(1024)(128)(4,1)S(1)}, s32[]{:S(2)}) async-start(s8[6291456]{0:T(1024)(128)(4,1)} %bitcast.370), calls=%async_computation.6 | async-start | bytes 8388608
  341.3 22.0 %copy-start.33 = (bf16[12,16,512]{2,1,0:T(8,128)(2,1)}, bf16[12,16,512]{2,1,0:T(8,128)(2,1)S(1)}, u32[]{:S(2)}) copy-start(bf16[12,16,512]{2,1,0:T(8,128)(2,1)S(1)} %fusion.103) | copy-start | bytes 589828
  342.2 3.2 copy-start.11
  342.2 3.2 copy-start.64
  345.5 3.1 copy-start.81
  345.5 3.1 copy-start.80
  345.5 3.1 copy-start.82
  345.5 3.1 copy-start.31
  355.0 1.9 copy-start.42
  355.0 2.0 copy-start.83
  355.0 2.0 copy-start.85
  355.1 2.0 copy-start.84
  355.1 2.0 copy-start.79
  357.1 5.7 copy-start.40
  363.3 2.5 copy-start.5
  363.3 2.5 copy-start.9
  365.9 1.9 copy-start.61
  369.9 2.1 copy-start.20
  369.9 2.0 copy-start.87
  372.0 2.0 copy-start.30
  389.3 254.6 %reduce-scatter.5.cloned.1.call-start = ((), (), s32[]{:S(2)}) async-start(), calls=%async_computation.5 | async-start | bytes 9732096 | tf_op jit(solution)/shard_map/reduce_scatter | solution.py:470
  391.0 2.4 copy-start.14
  391.0 2.5 copy-start.34
  391.0 2.5 copy-start.41
  391.1 2.5 copy-start.53
  392.3 3.4 copy-start.12
  393.5 2.2 copy-start.37
  393.5 2.2 copy-start.38
  503.0 5.6 copy-start.26
  (32 other events, 40.2 us)
Sparse Core Ops, SparseCore 0:
  13.0 71.9 all-gather.2
  88.5 79.9 all-gather.4
  389.4 113.5 reduce-scatter.2
  508.8 135.1 reduce-scatter.4

commit v7 on v6

--- a/solution.py
+++ b/solution.py
@@ -398,19 +398,16 @@
     aligned = rows % 8 == 0
     small = (text_vectors, layout_attn, layout_w1, layout_w2, layout_vectors)
     small_rows = pack_rows(small, width, aligned)
-    first = jnp.concatenate([text_attn, small_rows], 0)
+    first = jnp.concatenate([text_attn, text_w1, small_rows], 0)
     first_all = lax.all_gather(first, AXES, axis=0, tiled=True)
     count = first_all.shape[0] // first.shape[0]
     first_all = first_all.reshape(count, first.shape[0], width)
     full_attn = first_all[:, :rows].reshape(count * rows, width)
-    small_flat = first_all[:, rows:].reshape(count, -1)
+    full_w1 = first_all[:, rows : 2 * rows].reshape(count * rows, width)
+    small_flat = first_all[:, 2 * rows :].reshape(count, -1)
     shapes = [(1, text_vectors.shape[0]), layout_attn.shape, layout_w1.shape, layout_w2.shape, (1, layout_vectors.shape[0])]
     full_small = unpack_small(small_flat, count, shapes)
-    w2_rows = text_w2.shape[0]
-    second = jnp.concatenate([text_w1, text_w2.reshape(rows, -1)], 0)
-    second_all = lax.all_gather(second, AXES, axis=0, tiled=True).reshape(count, 2 * rows, width)
-    full_w1 = second_all[:, :rows].reshape(count * rows, width)
-    full_w2 = second_all[:, rows:].reshape(count * w2_rows, text_w2.shape[1])
+    full_w2 = lax.all_gather(text_w2, AXES, axis=0, tiled=True)
     return (full_attn, full_w1, full_w2) + full_small
 
 

time: 659 us -> 646 us (0.980)
  local copies, waits for them, and re-layouts: 104 us -> 89.6 us
    all_gather x1, waiting for transfers between devices: 21.1 us -> 0.01 us  [gather_weights(): full_w2 = lax.all_gather(text_w2, AXES, axis=0, tiled=True)]
    all_gather x1, waiting for transfers between devices: 67.5 us -> 88.5 us  [gather_weights(): first_all = lax.all_gather(first, AXES, axis=0, tiled=True)]
    reshape x2 -> x0, local copies, waits for them, and re-layouts: 9.48 us -> none  [the longest x1 8.47 us: gather_weights(): full_w2 = second_all[:, rows:].reshape(count * w2_rows, text_w2.shape[1])]
    slice x2 -> x1, local copies, waits for them, and re-layouts: 9.74 us -> 1.51 us  [gather_weights(): small_flat = first_all[:, 2 * rows:].reshape(count, -1)]
    unnamed x198 -> x220, local copies, waits for them, and re-layouts: 15.3 us -> 16.6 us
  transfers between devices with their start and end apart: 4 -> 4, of which waited for: 4 -> 3; matrix products, arithmetic and copies ran while one was open for 12% -> 15% of each run, Pallas kernels for 0% -> 0%
where the time goes in v7:
time: 646 us; the launch traced here: 642 us
  waiting for transfers between devices  326 us (50%)
  matrix products  157 us (24%)
  local copies, waits for them, and re-layouts  89.6 us (14%)
  other arithmetic  52.1 us (8%)
  between operations  16.2 us (3%)
    reduce_scatter x1, waiting for transfers between devices, scatter_early(): lax.psum_scatter(packed, AXES, scatter_dimension=0, tiled=True)  135 us
    reduce_scatter x1, waiting for transfers between devices, scatter_late(): lax.psum_scatter(packed.reshape(-1, width).astype(jnp.bfloat16), AXES, sc...  102 us
    all_gather x1, waiting for transfers between devices, gather_weights(): first_all = lax.all_gather(first, AXES, axis=0, tiled=True)  88.5 us
    dot_general x2, matrix products, branch_forward(): jnp.dot(hidden.astype(jnp.bfloat16), first, preferred_element_type=jnp.fl...  22.5 us
    sub x1, matrix products, attend_back(): layout_dp - jnp.sum(probs * layout_dp, -1, keepdims=True)  17.4 us
    unnamed x220, local copies, waits for them, and re-layouts  16.6 us
    sub x1, matrix products, attend_back(): text_ds = probs * (text_dp - jnp.sum(probs * text_dp, -1, keepdims=True))  14.2 us
  transfers between devices with their start and end apart: 4, of which 3 were waited for; matrix products, arithmetic and copies ran while one was open for 15% of the time, Pallas kernels for 0%

profile of v7, /device:TPU:0, one launch (start us, length us, event | category | flops | bytes accessed | tf_op | source)
XLA Modules:
  0.0 641.5 jit_solution(17684741669440402108)
XLA Ops:
  9.8 1.5 concatenate.62
  11.3 1.7 pad_maximum_fusion.6
  15.7 88.5 %all-gather.3.cloned.1.call-done = bf16[1792,3072]{1,0:T(8,128)(2,1)} async-done(((bf16[56,3072]{1,0:T(8,128)(2,1)}), bf16[1792,3072]{1,0:T(8,128)(2,1)}) %all-gather.3.cloned.1.call-update) | async-done | bytes 11010064 | tf_op jit(solution)/shard_map/all_gather | solution.py:402
  104.2 1.5 slice.249
  105.7 8.4 %fusion.165 = (bf16[32,24,3072]{2,1,0:T(8,128)(2,1)}, bf16[32,24,3072]{2,1,0:T(8,128)(2,1)}) fusion(bf16[32,56,3072]{2,1,0:T(8,128)(2,1)} %bitcast.388), kind=kLoop, calls=%fused_computation.264 | loop fusion | bytes 18874368 | tf_op jit(solution)/shard_map/slice | solution.py:405
  120.5 2.2 slice.248
  122.7 3.8 copy.46
  127.2 4.2 fusion.34
  131.7 1.2 copy-done.4
  132.9 6.4 fusion.180
  139.3 6.6 %fusion.175 = (f32[12,512]{1,0:T(8,128)S(1)}, f32[12,512,512]{1,2,0:T(8,128)S(1)}) fusion(bf16[512,12,16]{0,2,1:T(8,128)(2,1)S(1)} %bitcast.433, bf16[512,12,16]{0,2,1:T(8,128)(2,1)S(1)} %bitcast.432, f32[12,512,512]{1,2,0:T(8,128)} %fusion.180, pred[512]{0:T(512)(128)(4,1)S(1)} %copy-done.82), kind=kOutput, calls=%fused_computation.274 | convolution fusion | flops 116385792 | bytes 25584128 | tf_op jit(solution)/shard_map/vmap(qhd,khd->hqk)/dot_general | solution.py:60
  145.9 1.8 fusion.4
  147.6 2.3 divide_convert_fusion
  151.1 1.5 copy-done.1
  152.6 2.5 fusion.176
  157.8 4.2 convolution_convert_fusion.10
  162.0 2.1 fusion.168
  164.1 18.8 %multiply_convert_fusion = (bf16[512,3072]{1,0:T(8,128)(2,1)}, f32[512,3072]{1,0:T(8,128)}, f32[512,3072]{1,0:T(8,128)}) fusion(f32[3072]{0:T(1024)S(1)} %copy-done.66, bf16[768,3072]{1,0:T(8,128)(2,1)S(1)} %bitcast.404, bf16[1,512,768]{2,1,0:T(8,128)(2,1)S(1)} %fusion.93), kind=kOutput, calls=%fused_computation.27 | convolution fusion | flops 2519728128 | bytes 21245952 | tf_op jit(solution)/shard_map/vmap()/dot_general | solution.py:166
  182.9 6.0 fusion.177
  192.1 1.7 fusion.163
  195.9 4.3 convolution_convert_fusion.1
  200.3 8.9 %reshape.1155 = bf16[32,24,3072]{2,1,0:T(8,128)(2,1)} reshape(bf16[3072,768]{1,0:T(8,128)(2,1)} %convolution_convert_fusion.1) | data formatting | bytes 9437184 | tf_op jit(solution)/shard_map/reshape | solution.py:460
  209.1 10.3 %multiply_add_fusion = f32[512,3072]{1,0:T(8,128)S(1)} fusion(f32[512,3072]{1,0:T(8,128)} %get-tuple-element.81, f32[512,3072]{1,0:T(8,128)} %get-tuple-element.126, f32[3072]{0:T(1024)S(1)} %copy-done.66, bf16[3072,768]{1,0:T(8,128)(2,1)} %all-gather.5.cloned.1.call-done, bf16[1,512,768]{2,1,0:T(8,128)(2,1)} %copy-done.37), kind=kOutput, calls=%fused_computation.26 | convolution fusion | flops 2437939200 | bytes 24391680 | tf_op jit(solution)/shard_map/vmap()/dot_general | solution.py:220
  219.5 2.2 convert_bitcast_fusion.1
  221.6 2.5 copy-done.3
  224.1 2.8 convolution_convert_fusion.2
  227.0 4.0 pad_maximum_fusion
  232.2 6.9 %multiply_reduce_fusion.2 = (bf16[768]{0:T(1024)(128)(2,1)}, f32[512]{0:T(512)S(1)}, bf16[768]{0:T(1024)(128)(2,1)}, f32[1,512,768]{2,1,0:T(8,128)S(1)}) fusion(f32[1,512,768]{2,1,0:T(8,128)S(1)} %get-tuple-element.29, f32[512]{0:T(512)S(1)} %fusion.147, f32[512]{0:T(512)S(1)} %broadcast_multiply_fusion.2, f32[768]{0:T(1024)S(1)} %copy-done.51, ...), kind=kOutput, calls=%fused_computation.99 | convolution fusion | flops 2419456000 | bytes 12595200 | tf_op jit(solution)/shard_map/vmap()/dot_general | solution.py:239
  239.8 3.6 convolution_convert_fusion.4
  244.7 2.5 reshape.1159
  248.7 3.7 multiply_convert_fusion.3
  256.9 2.6 fusion.156
  263.7 2.8 fusion.166
  266.5 1.8 fusion.181
  268.4 4.4 subtract_exponential_fusion
  272.8 3.0 fusion.109
  275.8 1.5 copy-done
  277.4 2.9 fusion.84
  280.3 14.2 %subtract_multiply_fusion = f32[12,512,512]{1,2,0:T(8,128)} fusion(f32[12,512,512]{1,2,0:T(8,128)} %copy-done, bf16[512,12,64]{0,2,1:T(8,128)(2,1)S(1)} %bitcast.382, bf16[512,12,64]{0,2,1:T(8,128)(2,1)S(1)} %bitcast.391), kind=kOutput, calls=%fused_computation.5 | convolution fusion | flops 814750208 | bytes 26738688 | tf_op jit(solution)/shard_map/vmap()/sub | solution.py:113
  294.5 8.2 %convert_bitcast_fusion = bf16[1,12,512,512]{2,3,1,0:T(8,128)(2,1)} fusion(f32[12,512,512]{1,2,0:T(8,128)} %subtract_multiply_fusion), kind=kLoop, calls=%fused_computation.25 | loop fusion | flops 3145728 | bytes 18874368 | tf_op jit(solution)/shard_map/vmap()/convert_element_type | solution.py:116
  302.7 17.4 %fusion.31 = bf16[1,12,512,512]{2,3,1,0:T(8,128)(2,1)} fusion(f32[12,512,512]{1,2,0:T(8,128)} %subtract_multiply_fusion, f32[12,512,512]{1,2,0:T(8,128)} %copy-done, bf16[512,12,16]{0,2,1:T(8,128)(2,1)S(1)} %bitcast.413, bf16[512,12,16]{0,2,1:T(8,128)(2,1)S(1)} %bitcast.423), kind=kOutput, calls=%fused_computation.54 | convolution fusion | flops 217061888 | bytes 31850496 | tf_op jit(solution)/shard_map/vmap()/sub | solution.py:114
  320.1 5.8 multiply_convert_fusion.1
  327.5 1.7 fusion.103
  330.2 3.2 reduce_sum.441
  333.5 3.1 convolution_convert_fusion.3
  337.8 5.1 fusion.48
  343.7 1.2 fusion.91
  345.1 2.0 copy.67
  347.1 3.7 reshape.1181
  351.3 1.4 convolution_convert_fusion.7
  353.8 1.7 fusion.157
  355.9 1.8 concatenate.69
  357.9 2.1 copy.81
  360.0 2.0 fusion.23
  362.0 2.4 pad_maximum_fusion.2
  364.4 6.7 %copy.63 = bf16[768,3072]{1,0:T(8,128)(2,1)} copy(bf16[768,3072]{0,1:T(8,128)(2,1)} %pad_maximum_fusion.2) | data formatting | bytes 9437184 | tf_op jit(solution)/shard_map/concatenate | solution.py:516
  371.1 6.1 pad_maximum_fusion.1
  379.0 1.2 copy.57
  380.2 1.2 copy.56
  381.4 2.2 fusion.92
  383.6 5.5 bitcast_add_fusion
  389.2 102.2 %reduce-scatter.3.cloned.1.call-done = bf16[32,3072]{1,0:T(8,128)(2,1)} async-done(((bf16[1024,3072]{1,0:T(8,128)(2,1)}), bf16[32,3072]{1,0:T(8,128)(2,1)}) %reduce-scatter.3.cloned.1.call-update) | async-done | bytes 196624 | tf_op jit(solution)/shard_map/reduce_scatter | solution.py:436
  497.6 134.6 %reduce-scatter.5.cloned.1.call-done = bf16[48,3072]{1,0:T(8,128)(2,1)} async-done(((bf16[1536,3072]{1,0:T(8,128)(2,1)}), bf16[48,3072]{1,0:T(8,128)(2,1)}) %reduce-scatter.5.cloned.1.call-update) | async-done | bytes 294928 | tf_op jit(solution)/shard_map/reduce_scatter | solution.py:467
  632.2 1.7 fusion.171
  (341 shorter events, 49.4 us)
Async XLA Ops:
  7.2 97.0 %all-gather.3.cloned.1.call-start = ((), (), s32[]{:S(2)}) async-start(), calls=%async_computation.2 | async-start | bytes 11354112 | tf_op jit(solution)/shard_map/all_gather | solution.py:402
  13.0 169.9 %all-gather.5.cloned.1.call-start = ((), (), s32[]{:S(2)}) async-start(), calls=%async_computation.3 | async-start | bytes 4866048 | tf_op jit(solution)/shard_map/all_gather | solution.py:410
  13.8 477.5 %reduce-scatter.3.cloned.1.call-start = ((), (), s32[]{:S(2)}) async-start(), calls=%async_computation.4 | async-start | bytes 6488064 | tf_op jit(solution)/shard_map/reduce_scatter | solution.py:436
  15.7 103.3 %copy-start.87 = (f32[3]{0:T(128)}, f32[3]{0:T(128)S(1)}, u32[]{:S(2)}) copy-start(f32[3]{0:T(128)S(1)} %pad.35.clone) | copy-start | bytes 40
  114.0 5.0 copy-start.48
  114.9 5.4 copy-start.15
  117.8 37.6 %copy-start.50 = (f32[768]{0:T(1024)}, f32[768]{0:T(1024)S(1)}, u32[]{:S(2)}) copy-start(f32[768]{0:T(1024)S(1)} %get-tuple-element.108) | copy-start | bytes 9220
  117.8 37.6 %copy-start.56 = (f32[768]{0:T(1024)}, f32[768]{0:T(1024)S(1)}, u32[]{:S(2)}) copy-start(f32[768]{0:T(1024)S(1)} %get-tuple-element.107) | copy-start | bytes 9220
  132.9 6.4 copy-start.33
  132.9 6.4 copy-start.34
  132.9 6.4 copy-start.82
  149.9 2.7 copy-start.1
  149.9 2.7 copy-start.79
  149.9 2.7 copy-start.94
  152.6 2.5 copy-start.19
  156.9 7.2 %slice-start.4 = ((s8[4718592]{0:T(1024)(128)(4,1)}), s8[4194304]{0:T(1024)(128)(4,1)S(1)}, s32[]{:S(2)}) async-start(s8[4718592]{0:T(1024)(128)(4,1)} %bitcast.402), calls=%async_computation.10 | async-start | bytes 8388608
  157.8 6.3 slice-start.5
  157.8 6.3 copy-start.66
  164.1 18.8 %copy-start.78 = (f32[768]{0:T(1024)S(1)}, f32[768]{0:T(1024)}, u32[]{:S(2)}) copy-start(f32[768]{0:T(1024)} %get-tuple-element.106) | copy-start | bytes 9220
  189.3 2.8 copy-start.65
  193.8 2.2 copy-start.96
  219.4 4.7 copy-start.3
  219.5 4.7 copy-start.39
  219.5 7.5 %slice-start.2 = ((s8[4718592]{0:T(1024)(128)(4,1)}), s8[4194304]{0:T(1024)(128)(4,1)S(1)}, s32[]{:S(2)}) async-start(s8[4718592]{0:T(1024)(128)(4,1)} %bitcast.376), calls=%async_computation.8 | async-start | bytes 8388608
  224.1 2.9 slice-start.3
  239.7 3.6 copy-start.10
  239.8 3.6 copy-start.70
  244.7 3.5 copy-start.49
  244.7 3.5 copy-start.81
  248.5 12.2 %copy-start.54 = (f32[512]{0:T(512)}, f32[512]{0:T(512)S(1)}, u32[]{:S(2)}) copy-start(f32[512]{0:T(512)S(1)} %broadcast_multiply_fusion.1) | copy-start | bytes 6148
  248.6 12.1 %copy-start.61 = (f32[512]{0:T(512)}, f32[512]{0:T(512)S(1)}, u32[]{:S(2)}) copy-start(f32[512]{0:T(512)S(1)} %fusion.145) | copy-start | bytes 6148
  248.7 3.8 copy-start.76
  252.4 4.5 copy-start.28
  260.9 2.1 copy-start.59
  260.9 2.1 copy-start.22
  263.7 4.7 copy-start.17
  263.7 4.7 copy-start.24
  272.8 4.6 copy-start
  277.4 2.9 copy-start.6
  294.5 8.2 %copy-start.23 = (bf16[1,512,1,192]{1,3,2,0:T(8,128)(2,1)S(1)}, bf16[1,512,1,192]{1,3,2,0:T(8,128)(2,1)}, u32[]{:S(2)}) copy-start(bf16[1,512,1,192]{1,3,2,0:T(8,128)(2,1)} %get-tuple-element.93) | copy-start | bytes 589828
  302.7 17.4 %copy-start.8 = (bf16[1,512,1,768]{1,3,2,0:T(8,128)(2,1)S(1)}, bf16[1,512,1,768]{1,3,2,0:T(8,128)(2,1)}, u32[]{:S(2)}) copy-start(bf16[1,512,1,768]{1,3,2,0:T(8,128)(2,1)} %copy-done.7) | copy-start | bytes 2359300
  320.0 5.9 copy-start.2
  320.1 7.0 %slice-start = ((s8[6291456]{0:T(1024)(128)(4,1)}), s8[4194304]{0:T(1024)(128)(4,1)S(1)}, s32[]{:S(2)}) async-start(s8[6291456]{0:T(1024)(128)(4,1)} %bitcast.370), calls=%async_computation.6 | async-start | bytes 8388608
  329.2 22.0 %copy-start.35 = (bf16[12,16,512]{2,1,0:T(8,128)(2,1)}, bf16[12,16,512]{2,1,0:T(8,128)(2,1)S(1)}, u32[]{:S(2)}) copy-start(bf16[12,16,512]{2,1,0:T(8,128)(2,1)S(1)} %fusion.103) | copy-start | bytes 589828
  330.2 3.2 copy-start.11
  330.2 3.2 copy-start.71
  333.4 3.1 copy-start.89
  333.5 3.1 copy-start.88
  333.5 3.1 copy-start.90
  333.5 3.2 copy-start.32
  345.1 5.7 copy-start.43
  351.3 2.5 copy-start.5
  351.3 2.5 copy-start.9
  357.9 2.1 copy-start.20
  357.9 2.1 copy-start.95
  377.2 255.0 %reduce-scatter.5.cloned.1.call-start = ((), (), s32[]{:S(2)}) async-start(), calls=%async_computation.5 | async-start | bytes 9732096 | tf_op jit(solution)/shard_map/reduce_scatter | solution.py:467
  379.0 2.4 copy-start.14
  379.0 2.4 copy-start.36
  379.0 2.4 copy-start.44
  379.0 2.4 copy-start.60
  380.2 3.4 copy-start.12
  381.4 2.2 copy-start.40
  381.4 2.2 copy-start.41
  491.3 5.6 copy-start.26
  (43 other events, 62.0 us)
Sparse Core Ops, SparseCore 0:
  13.2 90.9 all-gather.2
  107.1 62.1 all-gather.4
  377.3 113.9 reduce-scatter.2
  497.1 135.1 reduce-scatter.4

commit v8 on v7

--- a/solution.py
+++ b/solution.py
@@ -1,6 +1,10 @@
+import functools
+
 import jax
 import jax.numpy as jnp
 from jax import lax
+from jax.experimental import pallas as pl
+from jax.experimental.pallas import tpu as pltpu
 from jax.sharding import PartitionSpec as P
 
 
@@ -88,54 +92,93 @@
     )
 
 
-def attend_back(text_three, layout_three, valid, log_total, text_grad, layout_grad):
-    scores = score_table(text_three, layout_three, valid)
-    probs = jnp.exp(scores - log_total[..., None])
+def _nt(a, b):
+    return lax.dot_general(a, b, (((1,), (1,)), ((), ())), preferred_element_type=jnp.float32)
+
+
+def _tn(a, b):
+    return lax.dot_general(a, b, (((0,), (0,)), ((), ())), preferred_element_type=jnp.float32)
+
+
+def _nn(a, b):
+    return lax.dot_general(a, b, (((1,), (0,)), ((), ())), preferred_element_type=jnp.float32)
+
+
+def attn_back_kernel(len_ref, q_ref, k_ref, v_ref, dc_ref, ql_ref, kl_ref, vl_ref, dcl_ref, lse_ref,
+                     dq_ref, dk_ref, dv_ref, dql_ref, dkl_ref, dvl_ref, *, text_scale, layout_scale):
+    q, k, v, dc = q_ref[0], k_ref[0], v_ref[0], dc_ref[0]
+    ql, kl, vl, dcl = ql_ref[0], kl_ref[0], vl_ref[0], dcl_ref[0]
+    scores = _nt(q, k) * text_scale + _nt(ql, kl) * layout_scale
+    keys = lax.broadcasted_iota(jnp.int32, scores.shape, 1)
+    scores = jnp.where(keys < len_ref[0], scores, NEG)
+    probs = jnp.exp(scores - lse_ref[0])
+    text_dp = _nt(dc, v)
+    layout_dp = _nt(dcl, vl)
+    text_ds = probs * (text_dp - jnp.sum(probs * text_dp, 1, keepdims=True))
+    layout_ds = probs * (layout_dp - jnp.sum(probs * layout_dp, 1, keepdims=True))
+    text_g = text_ds.astype(jnp.bfloat16)
+    joint_g = (text_ds + layout_ds).astype(jnp.bfloat16)
     weights = probs.astype(jnp.bfloat16)
-    text_heads = split_heads(text_grad)
-    layout_heads = split_heads(layout_grad)
-    text_dp = jnp.einsum(
-        "qhd,khd->hqk",
-        text_heads,
-        split_heads(text_three[:, 2]),
-        preferred_element_type=jnp.float32,
-    )
-    layout_dp = jnp.einsum(
-        "qhd,khd->hqk",
-        layout_heads,
-        split_heads(layout_three[:, 2]),
-        preferred_element_type=jnp.float32,
-    )
-    text_dv = jnp.einsum("hqk,qhd->khd", weights, text_heads, preferred_element_type=jnp.float32)
-    layout_dv = jnp.einsum(
-        "hqk,qhd->khd", weights, layout_heads, preferred_element_type=jnp.float32
-    )
-    text_ds = probs * (text_dp - jnp.sum(probs * text_dp, -1, keepdims=True))
-    layout_ds = probs * (layout_dp - jnp.sum(probs * layout_dp, -1, keepdims=True))
-    text_only, joint_ds = lax.optimization_barrier(
-        (text_ds.astype(jnp.bfloat16), (text_ds + layout_ds).astype(jnp.bfloat16))
-    )
-    text_dq = jnp.einsum(
-        "hqk,khd->qhd", text_only, split_heads(text_three[:, 1]), preferred_element_type=jnp.float32
-    ) * HD ** (-0.5)
-    text_dk = jnp.einsum(
-        "hqk,qhd->khd", text_only, split_heads(text_three[:, 0]), preferred_element_type=jnp.float32
-    ) * HD ** (-0.5)
-    layout_dq = jnp.einsum(
-        "hqk,khd->qhd",
-        joint_ds,
-        split_heads(layout_three[:, 1]),
-        preferred_element_type=jnp.float32,
-    ) * LHD ** (-0.5)
-    layout_dk = jnp.einsum(
-        "hqk,qhd->khd",
-        joint_ds,
-        split_heads(layout_three[:, 0]),
-        preferred_element_type=jnp.float32,
-    ) * LHD ** (-0.5)
-    slots = text_three.shape[0]
-    text_all = jnp.stack([text_dq, text_dk, text_dv], 1).reshape(slots, 3, -1)
-    layout_all = jnp.stack([layout_dq, layout_dk, layout_dv], 1).reshape(slots, 3, -1)
+    dq_ref[0] = (_nn(text_g, k) * text_scale).astype(dq_ref.dtype)
+    dk_ref[0] = (_tn(text_g, q) * text_scale).astype(dk_ref.dtype)
+    dv_ref[0] = _tn(weights, dc).astype(dv_ref.dtype)
+    dql_ref[0] = (_nn(joint_g, kl) * layout_scale).astype(dql_ref.dtype)
+    dkl_ref[0] = (_tn(joint_g, ql) * layout_scale).astype(dkl_ref.dtype)
+    dvl_ref[0] = _tn(weights, dcl).astype(dvl_ref.dtype)
+
+
+def attn_back_heads(length, q, k, v, dc, ql, kl, vl, dcl, lse, text_scale, layout_scale):
+    heads, slots, wide = q.shape
+    narrow = ql.shape[2]
+    text_spec = pl.BlockSpec((1, slots, wide), lambda h, n: (h, 0, 0))
+    layout_spec = pl.BlockSpec((1, slots, narrow), lambda h, n: (h, 0, 0))
+    lse_spec = pl.BlockSpec((1, slots, 1), lambda h, n: (h, 0, 0))
+    text_out = jax.ShapeDtypeStruct((heads, slots, wide), jnp.bfloat16)
+    layout_out = jax.ShapeDtypeStruct((heads, slots, narrow), jnp.bfloat16)
+    flops = heads * slots * slots * 2 * (4 * wide + 4 * narrow)
+    return pl.pallas_call(
+        functools.partial(attn_back_kernel, text_scale=text_scale, layout_scale=layout_scale),
+        grid_spec=pltpu.PrefetchScalarGridSpec(
+            num_scalar_prefetch=1,
+            grid=(heads,),
+            in_specs=[text_spec] * 4 + [layout_spec] * 4 + [lse_spec],
+            out_specs=[text_spec] * 3 + [layout_spec] * 3,
+        ),
+        out_shape=[text_out] * 3 + [layout_out] * 3,
+        compiler_params=pltpu.CompilerParams(dimension_semantics=("arbitrary",)),
+        cost_estimate=pl.CostEstimate(
+            flops=flops,
+            transcendentals=heads * slots * slots,
+            bytes_accessed=heads * slots * (8 * wide + 8 * narrow + 4),
+        ),
+    )(length, q, k, v, dc, ql, kl, vl, dcl, lse)
+
+
+def to_heads(values, size):
+    return values.reshape(values.shape[0], H, size).transpose(1, 0, 2)
+
+
+def from_heads(values):
+    return values.transpose(1, 0, 2).reshape(values.shape[1], -1)
+
+
+def attend_back(text_three, layout_three, length, log_total, text_grad, layout_grad):
+    outs = attn_back_heads(
+        jnp.reshape(length, (1,)).astype(jnp.int32),
+        to_heads(text_three[:, 0], HD),
+        to_heads(text_three[:, 1], HD),
+        to_heads(text_three[:, 2], HD),
+        to_heads(text_grad, HD),
+        to_heads(layout_three[:, 0], LHD),
+        to_heads(layout_three[:, 1], LHD),
+        to_heads(layout_three[:, 2], LHD),
+        to_heads(layout_grad, LHD),
+        log_total[:, :, None],
+        HD ** (-0.5),
+        LHD ** (-0.5),
+    )
+    text_all = jnp.stack([from_heads(part) for part in outs[:3]], 1)
+    layout_all = jnp.stack([from_heads(part) for part in outs[3:]], 1)
     return (text_all, layout_all)
 
 
@@ -325,7 +368,7 @@
     text_res_grad, text_ctx_grad, text_ops, text_sums = text_back
     layout_res_grad, layout_ctx_grad, layout_ops, layout_sums = layout_back
     text_three_grad, layout_three_grad = attend_back(
-        text_three, layout_three, valid, log_total, text_ctx_grad, layout_ctx_grad
+        text_three, layout_three, length, log_total, text_ctx_grad, layout_ctx_grad
     )
     text_in_grad, text_rounded, text_query_bias, text_value_bias = project_back(
         text_attn, width, True, text_three_grad, text_res_grad

time: 646 us -> 642 us (level)
  matrix products: 157 us -> 104 us
  local copies, waits for them, and re-layouts: 89.6 us -> 117 us
  Pallas kernels: 0 us -> 25 us
    sub x2 -> x0, matrix products: 31.5 us -> none  [the longest x1 17.4 us: attend_back(): layout_dp - jnp.sum(probs * layout_dp, -1, keepdims=True)]
    pallas_call x0 -> x1, Pallas kernels: none -> 25 us  [attn_back_heads(): pl.pallas_call(functools.partial(attn_back_kernel, text_scale=text_scale,...]
    dot_general x6 -> x0, matrix products: 15.5 us -> none  [the longest x1 5.84 us: attend_back(): jnp.einsum('hqk,qhd->khd', text_only, split_heads(text_three[:, 0]), pref...]
    squeeze x0 -> x6, local copies, waits for them, and re-layouts: none -> 10 us  [to_heads(): return values.reshape(values.shape[0], H, size).transpose(1, 0, 2)]
    convert_element_type x1 -> x0, other arithmetic: 8.18 us -> none  [attend_back(): text_ds.astype(jnp.bfloat16)]
    transpose x0 -> x6, local copies, waits for them, and re-layouts: none -> 7.33 us  [from_heads(): return values.transpose(1, 0, 2).reshape(values.shape[1], -1)]
    reshape x0 -> x5, local copies, waits for them, and re-layouts: none -> 6.57 us  [the longest x3 3.51 us: attend_back(): text_all = jnp.stack([from_heads(part) for part in outs[:3]], 1)]
    unnamed x220 -> x184, local copies, waits for them, and re-layouts: 16.6 us -> 14.4 us
  transfers between devices with their start and end apart: 4 -> 4, of which waited for: 3 -> 3; matrix products, arithmetic and copies ran while one was open for 15% -> 14% of each run, Pallas kernels for 0% -> 0%
where the time goes in v8:
time: 642 us; the launch traced here: 638 us
  waiting for transfers between devices  330 us (51%)
  local copies, waits for them, and re-layouts  117 us (18%)
  matrix products  104 us (16%)
  other arithmetic  46.4 us (7%)
  Pallas kernels  25 us (4%)
  between operations  15.9 us (2%)
    reduce_scatter x1, waiting for transfers between devices, scatter_early(): lax.psum_scatter(packed, AXES, scatter_dimension=0, tiled=True)  135 us
    reduce_scatter x1, waiting for transfers between devices, scatter_late(): lax.psum_scatter(packed.reshape(-1, width).astype(jnp.bfloat16), AXES, sc...  105 us
    all_gather x1, waiting for transfers between devices, gather_weights(): first_all = lax.all_gather(first, AXES, axis=0, tiled=True)  89.1 us
    pallas_call x1, Pallas kernels, attn_back_heads(): pl.pallas_call(functools.partial(attn_back_kernel, text_scale=text_scale,...  25 us
    dot_general x2, matrix products, branch_forward(): jnp.dot(hidden.astype(jnp.bfloat16), first, preferred_element_type=jnp.fl...  22.5 us
    unnamed x184, local copies, waits for them, and re-layouts  14.4 us
  transfers between devices with their start and end apart: 4, of which 3 were waited for; matrix products, arithmetic and copies ran while one was open for 14% of the time, Pallas kernels for 0%

profile of v8, /device:TPU:0, one launch (start us, length us, event | category | flops | bytes accessed | tf_op | source)
XLA Modules:
  0.0 637.7 jit_solution(12418097225335426421)
XLA Ops:
  9.8 1.5 concatenate.50
  11.3 1.7 pad_maximum_fusion.6
  15.1 89.1 %all-gather.3.cloned.1.call-done = bf16[1792,3072]{1,0:T(8,128)(2,1)} async-done(((bf16[56,3072]{1,0:T(8,128)(2,1)}), bf16[1792,3072]{1,0:T(8,128)(2,1)}) %all-gather.3.cloned.1.call-update) | async-done | bytes 11010064 | tf_op jit(solution)/shard_map/all_gather | solution.py:445
  104.2 1.5 slice.245
  105.7 8.3 %fusion.112 = (bf16[32,24,3072]{2,1,0:T(8,128)(2,1)}, bf16[32,24,3072]{2,1,0:T(8,128)(2,1)}) fusion(bf16[32,56,3072]{2,1,0:T(8,128)(2,1)} %bitcast.350), kind=kLoop, calls=%fused_computation.226 | loop fusion | bytes 18874368 | tf_op jit(solution)/shard_map/slice | solution.py:448
  121.5 2.2 slice.244
  123.8 4.1 copy.35
  128.7 4.2 fusion.11
  133.1 1.2 copy-done.2
  134.3 6.4 fusion.127
  140.7 6.6 %fusion.122 = (f32[12,512]{1,0:T(8,128)S(1)}, f32[12,512,512]{1,2,0:T(8,128)S(1)}) fusion(bf16[512,12,16]{0,2,1:T(8,128)(2,1)S(1)} %bitcast.399, bf16[512,12,16]{0,2,1:T(8,128)(2,1)S(1)} %bitcast.398, f32[12,512,512]{1,2,0:T(8,128)} %fusion.127, pred[512]{0:T(512)(128)(4,1)S(1)} %copy-done.76), kind=kOutput, calls=%fused_computation.236 | convolution fusion | flops 116385792 | bytes 25584128 | tf_op jit(solution)/shard_map/vmap(qhd,khd->hqk)/dot_general | solution.py:64
  147.3 1.8 fusion
  149.7 2.3 divide_convert_fusion
  153.1 1.5 copy-done
  154.6 2.5 fusion.123
  159.3 4.0 convolution_convert_fusion.10
  163.3 2.1 fusion.115
  165.4 18.7 %multiply_convert_fusion = (bf16[512,3072]{1,0:T(8,128)(2,1)}, f32[512,3072]{1,0:T(8,128)}, f32[512,3072]{1,0:T(8,128)}) fusion(f32[3072]{0:T(1024)S(1)} %copy-done.49, bf16[768,3072]{1,0:T(8,128)(2,1)S(1)} %bitcast.367, bf16[1,512,768]{2,1,0:T(8,128)(2,1)S(1)} %fusion.55), kind=kOutput, calls=%fused_computation.9 | convolution fusion | flops 2519728128 | bytes 21245952 | tf_op jit(solution)/shard_map/vmap()/dot_general | solution.py:209
  184.1 6.0 fusion.124
  193.3 1.7 fusion.110
  197.2 4.3 convolution_convert_fusion.1
  201.5 8.7 %reshape.998 = bf16[32,24,3072]{2,1,0:T(8,128)(2,1)} reshape(bf16[3072,768]{1,0:T(8,128)(2,1)} %convolution_convert_fusion.1) | data formatting | bytes 9437184 | tf_op jit(solution)/shard_map/reshape | solution.py:503
  210.2 10.3 %multiply_add_fusion = f32[512,3072]{1,0:T(8,128)S(1)} fusion(f32[512,3072]{1,0:T(8,128)} %get-tuple-element.89, f32[512,3072]{1,0:T(8,128)} %get-tuple-element.134, f32[3072]{0:T(1024)S(1)} %copy-done.49, bf16[3072,768]{1,0:T(8,128)(2,1)} %all-gather.5.cloned.1.call-done, bf16[1,512,768]{2,1,0:T(8,128)(2,1)} %copy-done.28), kind=kOutput, calls=%fused_computation.8 | convolution fusion | flops 2437939200 | bytes 24391680 | tf_op jit(solution)/shard_map/vmap()/dot_general | solution.py:263
  220.5 2.2 convert_bitcast_fusion
  222.7 2.5 copy-done.1
  225.2 2.8 convolution_convert_fusion.2
  228.1 3.9 pad_maximum_fusion
  233.2 6.9 %multiply_reduce_fusion = (bf16[768]{0:T(1024)(128)(2,1)}, f32[512]{0:T(512)S(1)}, bf16[768]{0:T(1024)(128)(2,1)}, f32[1,512,768]{2,1,0:T(8,128)S(1)}) fusion(f32[1,512,768]{2,1,0:T(8,128)S(1)} %get-tuple-element.33, f32[512]{0:T(512)S(1)} %fusion.96, f32[512]{0:T(512)S(1)} %broadcast_multiply_fusion.2, f32[768]{0:T(1024)S(1)} %get-tuple-element.116, ...), kind=kOutput, calls=%fused_computation.71 | convolution fusion | flops 2419456000 | bytes 12595200 | tf_op jit(solution)/shard_map/vmap()/dot_general | solution.py:282
  240.8 3.6 convolution_convert_fusion.4
  245.7 2.5 reshape.1002
  249.9 3.7 multiply_convert_fusion.1
  258.3 2.6 fusion.103
  265.1 1.6 copy.45
  266.6 1.5 copy.47
  268.1 1.5 copy.48
  269.7 1.5 copy.46
  271.1 1.5 fusion.113
  272.6 2.5 copy.42
  275.1 1.5 copy.43
  276.6 1.5 copy.41
  278.2 2.2 copy.50.lse_ref
  280.4 1.5 copy.49
  281.9 25.0 %vmap__.1 = (bf16[12,512,64]{2,1,0:T(8,128)(2,1)}, bf16[12,512,64]{2,1,0:T(8,128)(2,1)}, bf16[12,512,64]{2,1,0:T(8,128)(2,1)}, bf16[12,512,16]{2,1,0:T(8,128)(2,...) custom-call(s32[1]{0:T(128)} %copy.86.len_ref, bf16[12,512,64]{2,1,0:T(8,128)(2,1)} %bitcast.358, ...), custom_call_target="tpu_custom_call" | custom-call | flops 2013265920 | bytes 3956736 | tf_op jit(solution)/shard_map/vmap()/pallas_call | solution.py:139
  306.8 1.7 copy.58
  308.6 1.7 copy.59
  313.0 3.8 reduce_sum.420
  316.8 2.0 convolution_convert_fusion.3
  321.6 5.1 fusion.19
  330.6 3.0 reshape.1025
  333.6 1.8 copy.51
  343.3 2.4 fusion.104
  346.2 2.6 concatenate.57
  348.8 1.3 pad.10
  350.1 2.0 copy.74
  352.1 2.4 copy.61
  354.5 3.9 fusion.7
  358.5 2.5 pad_maximum_fusion.2
  361.0 6.6 %copy.62 = bf16[768,3072]{1,0:T(8,128)(2,1)} copy(bf16[768,3072]{0,1:T(8,128)(2,1)} %pad_maximum_fusion.2) | data formatting | bytes 9437184 | tf_op jit(solution)/shard_map/concatenate | solution.py:559
  367.6 6.1 pad_maximum_fusion.1
  374.9 2.2 fusion.54
  377.1 5.2 bitcast_add_fusion
  382.3 105.0 %reduce-scatter.3.cloned.1.call-done = bf16[32,3072]{1,0:T(8,128)(2,1)} async-done(((bf16[1024,3072]{1,0:T(8,128)(2,1)}), bf16[32,3072]{1,0:T(8,128)(2,1)}) %reduce-scatter.3.cloned.1.call-update) | async-done | bytes 196624 | tf_op jit(solution)/shard_map/reduce_scatter | solution.py:479
  493.6 134.7 %reduce-scatter.5.cloned.1.call-done = bf16[48,3072]{1,0:T(8,128)(2,1)} async-done(((bf16[1536,3072]{1,0:T(8,128)(2,1)}), bf16[48,3072]{1,0:T(8,128)(2,1)}) %reduce-scatter.5.cloned.1.call-update) | async-done | bytes 294928 | tf_op jit(solution)/shard_map/reduce_scatter | solution.py:510
  628.4 1.7 fusion.118
  (311 shorter events, 60.6 us)
Async XLA Ops:
  7.2 97.0 %all-gather.3.cloned.1.call-start = ((), (), s32[]{:S(2)}) async-start(), calls=%async_computation.2 | async-start | bytes 11354112 | tf_op jit(solution)/shard_map/all_gather | solution.py:445
  13.0 171.1 %all-gather.5.cloned.1.call-start = ((), (), s32[]{:S(2)}) async-start(), calls=%async_computation.3 | async-start | bytes 4866048 | tf_op jit(solution)/shard_map/all_gather | solution.py:453
  13.8 473.6 %reduce-scatter.3.cloned.1.call-start = ((), (), s32[]{:S(2)}) async-start(), calls=%async_computation.4 | async-start | bytes 6488064 | tf_op jit(solution)/shard_map/reduce_scatter | solution.py:479
  15.1 105.0 %copy-start.70 = (f32[3]{0:T(128)}, f32[3]{0:T(128)S(1)}, u32[]{:S(2)}) copy-start(f32[3]{0:T(128)S(1)} %pad.29.clone) | copy-start | bytes 40
  114.0 6.2 copy-start.42
  114.8 6.6 %copy-start.7 = (bf16[4,8,8,3072]{3,1,2,0:T(8,128)(2,1)}, bf16[4,8,8,3072]{3,1,2,0:T(8,128)(2,1)S(1)}, u32[]{:S(2)}) copy-start(bf16[4,8,8,3072]{3,1,2,0:T(8,128)(2,1)S(1)} %copy.73) | copy-start | bytes 4718596
  134.3 6.4 copy-start.26
  134.3 6.4 copy-start.27
  134.3 6.4 copy-start.76
  151.9 2.7 copy-start
  152.0 2.7 copy-start.64
  152.0 2.6 copy-start.79
  154.6 2.5 copy-start.11
  158.9 6.4 %slice-start.2 = ((s8[4718592]{0:T(1024)(128)(4,1)}), s8[4194304]{0:T(1024)(128)(4,1)S(1)}, s32[]{:S(2)}) async-start(s8[4718592]{0:T(1024)(128)(4,1)} %bitcast.365), calls=%async_computation.8 | async-start | bytes 8388608
  159.3 6.1 slice-start.3
  159.3 6.1 copy-start.49
  165.4 18.8 %copy-start.63 = (f32[768]{0:T(1024)S(1)}, f32[768]{0:T(1024)}, u32[]{:S(2)}) copy-start(f32[768]{0:T(1024)} %get-tuple-element.114) | copy-start | bytes 9220
  190.5 2.8 copy-start.48
  195.0 2.2 copy-start.80
  220.5 4.7 copy-start.1
  220.5 4.7 copy-start.30
  220.5 7.5 %slice-start = ((s8[4718592]{0:T(1024)(128)(4,1)}), s8[4194304]{0:T(1024)(128)(4,1)S(1)}, s32[]{:S(2)}) async-start(s8[4718592]{0:T(1024)(128)(4,1)} %bitcast.344), calls=%async_computation.6 | async-start | bytes 8388608
  225.2 2.9 slice-start.1
  240.7 3.6 copy-start.4
  240.8 3.6 copy-start.53
  245.7 3.8 copy-start.43
  245.7 3.8 copy-start.66
  249.9 3.8 copy-start.61
  253.7 4.6 copy-start.20
  253.7 1.9 copy-start.62
  262.1 2.6 copy-start.29
  262.3 2.7 copy-start.14
  268.1 3.0 copy-start.3
  272.6 2.5 copy-start.9
  278.2 2.2 copy-start.38
  306.8 3.5 copy-start.19
  308.6 3.3 copy-start.32
  312.9 3.9 copy-start.5
  312.9 3.9 copy-start.12
  312.9 3.9 copy-start.54
  316.8 2.0 copy-start.73
  316.8 2.5 copy-start.72
  316.8 3.1 copy-start.74
  316.8 3.6 copy-start.25
  326.8 1.8 copy-start.78
  326.8 2.4 copy-start.77
  326.8 2.9 copy-start.69
  333.6 3.0 copy-start.18
  337.2 3.3 copy-start.58
  337.3 3.2 copy-start.71
  337.3 4.2 copy-start.17
  343.3 2.5 copy-start.57
  343.3 2.5 copy-start.68
  343.3 2.6 copy-start.67
  343.3 2.6 copy-start.56
  343.3 2.6 copy-start.50
  343.3 2.6 copy-start.51
  343.3 2.6 copy-start.46
  343.3 2.9 copy-start.23
  354.5 3.9 copy-start.21
  373.8 254.6 %reduce-scatter.5.cloned.1.call-start = ((), (), s32[]{:S(2)}) async-start(), calls=%async_computation.5 | async-start | bytes 9732096 | tf_op jit(solution)/shard_map/reduce_scatter | solution.py:510
  374.9 2.2 copy-start.6
  374.9 2.2 copy-start.55
  487.3 5.6 copy-start.15
  (25 other events, 30.9 us)
Sparse Core Ops, SparseCore 0:
  13.2 90.9 all-gather.2
  107.1 62.0 all-gather.4
  373.9 113.3 reduce-scatter.2
  493.1 135.2 reduce-scatter.4
